TPU v7x, 256 devices: a whole 4x4x8 slice. The times are simulated.
256 devices in a mesh: node: 32 (over y, x, z_lo), shot: 8 (over z_hi, core).
Axes of the slice: x: 4, y: 4, z: 8 (z_hi: 4, z_lo: 2; z = z_hi * 2 + z_lo), core: 2. Of those that a mesh axis runs over, the one named last changes fastest.
Arguments:
- spectra: bfloat16 [64, 2, 1024, 4096], P(None, None, 'shot', 'node'), may hold values from -6 to 6
- source_block: int32 [6], replicated, may hold values from 0 to 127
- taper_window: int32 [6, 1024], replicated, may hold values from 0 to 7
Outputs:
- virtual_gathers: bfloat16 [6, 64, 2, 32, 4096], P(None, 'shot', None, None, 'node')
All inputs are finite; a program needn't handle non-finite values.
Results may differ from a plain program's by a relative error of at most 0.0047.
Values may be sent and summed in bfloat16 or wider, within the bound.
No kernel may reach another device: no remote copies, remote signals or barrier semaphores. Data moves between devices by JAX's collectives and lax.ppermute only.
A program may use at most 128 MiB of HBM per device.

v0:
```python
import jax
import jax.numpy as jnp
from jax import lax
from jax.sharding import PartitionSpec as P

SB = 32
ROUNDS = 6
WINDOWS = 8


def from_root(x, axis, root):
    mine = lax.axis_index(axis) == root
    return lax.psum(jnp.where(mine, x, jnp.zeros_like(x)), axis)


def taper_weights(taper_windows):
    return 0.5 - 0.5 * jnp.cos(jnp.pi * (taper_windows.astype(jnp.float32) + 1.0) / (WINDOWS + 1.0))


def correlate(tapered_spectra, receiver_nodes):
    real_part = tapered_spectra[:, 0]
    imag_part = tapered_spectra[:, 1]
    real_row = jnp.stack((real_part, imag_part), axis=1)
    imag_row = jnp.stack((-imag_part, real_part), axis=1)
    operator = jnp.stack((real_row, imag_row), axis=1)
    return jnp.einsum(
        "mochn,mchr->monr", operator, receiver_nodes, preferred_element_type=jnp.float32
    )


def source_piece(spectrum_holder, block, per_device):
    offset = block % per_device * SB
    return lax.dynamic_slice_in_dim(spectrum_holder, offset, SB, 3)


def body(spectra, source_block, taper_window):
    shot_dev = spectra.shape[2]
    node_dev = spectra.shape[3]
    per_device = node_dev // SB
    shot_count = shot_dev * lax.axis_size("shot")
    scale = 1.0 / jnp.sqrt(jnp.float32(shot_count))
    shot_weights = taper_weights(taper_window)
    gather_results = []
    first_shot = lax.axis_index("shot") * shot_dev
    local_weights = lax.dynamic_slice_in_dim(shot_weights, first_shot, shot_dev, 1)
    for turn in range(ROUNDS):
        block = source_block[turn]
        piece = source_piece(spectra, block, per_device)
        received_spectra = from_root(piece, "node", block // per_device)
        tapered_spectra = (
            received_spectra.astype(jnp.float32) * local_weights[turn][:, None]
        ).astype(jnp.bfloat16)
        summed = lax.psum_scatter(
            correlate(tapered_spectra, spectra) * scale, "shot", scatter_dimension=0, tiled=True
        )
        gather_results.append(summed.astype(jnp.bfloat16))
    return jnp.stack(gather_results, axis=0)


def solution(mesh):
    in_specs = (P(None, None, "shot", "node"), P(), P())
    out_specs = P(None, "shot", None, None, "node")
    return jax.shard_map(body, mesh=mesh, in_specs=in_specs, out_specs=out_specs, check_vma=False)
```

profile of v0, /device:TPU:73, one launch (start us, length us, event | category | flops | bytes accessed | tf_op | source)
XLA Modules:
  0.0 723.6 jit_solution(17395319209034421145)
XLA Ops:
  6.5 1.6 fusion.50
  24.1 24.5 %constant_dynamic-slice_fusion = (bf16[64,2,128,32]{3,2,1,0:T(8,128)(2,1)}, bf16[64,2,128,32]{3,2,1,0:T(8,128)(2,1)}, bf16[64,2,128,32]{3,2,1,0:T(8,128)(2,1)}, ...) fusion(bf16[64,2,128,128]{3,2,1,0:T(8,128)(2,1)} %param.3, ...), kind=kLoop, calls=%fused_computation.67 | loop fusion | bytes 12582936 | tf_op jit(solution)/shard_map/dynamic_slice | solution.py:33
  48.6 4.6 copy.28
  53.1 4.6 copy.27
  57.7 4.6 copy.26
  62.3 3.6 copy.25
  65.9 3.6 copy.24
  69.4 3.6 copy.23
  73.0 1.2 broadcast_select_fusion
  74.2 0.4 copy-done.7
  74.6 1.0 broadcast_select_fusion.1
  75.7 1.0 broadcast_select_fusion.2
  76.7 1.0 broadcast_select_fusion.3
  77.7 1.1 broadcast_select_fusion.4
  78.8 1.0 broadcast_select_fusion.5
  79.9 0.0 reduce-scatter.7.cloned.1.call-start
  79.9 0.7 fusion.48
  80.7 337.2 %all-reduce.3.cloned.1.call-done = (bf16[64,2,128,32]{2,3,1,0:T(8,128)(2,1)}, bf16[64,2,128,32]{2,3,1,0:T(8,128)(2,1)}, bf16[64,2,128,32]{2,3,1,0:T(8,128)(2,1)}...) async-done(((bf16[64,2,128,32]{2,3,1,0:T(8,128)(2,1)}, bf16[64,2,128,32]{2,3,1,0:T(8,128)(2,1)}, ...) | async-done | bytes 6291472 | tf_op jit(solution)/shard_map/psum | solution.py:13
  417.8 2.0 multiply_convert_fusion.4
  419.8 0.1 slice_negate_fusion.5
  419.9 0.1 maximum_bitcast_fusion
  420.0 2.0 copy-done
  422.0 2.1 bitcast_multiply_fusion.5
  424.1 0.0 reduce-scatter.9.cloned.1.call-start
  424.2 0.1 slice_negate_fusion.4
  424.3 0.1 maximum_bitcast_fusion.1
  424.4 2.0 copy-done.1
  426.4 2.2 bitcast_multiply_fusion.4
  428.6 0.0 reduce-scatter.11.cloned.1.call-start
  428.6 1.1 copy-done.10
  429.8 0.3 copy-done.11
  430.1 0.4 multiply_convert_fusion.2
  430.6 0.1 slice_negate_fusion.3
  430.7 0.1 maximum_bitcast_fusion.2
  430.8 2.0 copy-done.2
  432.7 2.3 bitcast_multiply_fusion.3
  435.1 0.1 slice_negate_fusion.2
  435.2 0.1 maximum_bitcast_fusion.3
  435.3 2.0 copy-done.3
  437.3 2.3 bitcast_multiply_fusion.2
  439.6 0.2 reduce-scatter.15.cloned.1.call-start
  439.8 1.0 copy-done.8
  440.8 0.3 copy-done.9
  441.1 0.4 multiply_convert_fusion
  441.6 0.1 slice_negate_fusion.1
  441.7 0.1 maximum_bitcast_fusion.4
  441.8 2.0 copy-done.4
  443.7 2.3 bitcast_multiply_fusion.1
  446.1 0.1 slice_negate_fusion
  446.2 0.1 maximum_bitcast_fusion.5
  446.3 2.0 copy-done.5
  448.3 2.2 bitcast_multiply_fusion
  450.6 39.8 %reduce-scatter.7.cloned.1.call-done = f32[8,2,32,128]{3,2,1,0:T(8,128)} async-done(((f32[64,2,32,128]{3,2,1,0:T(8,128)}), f32[8,2,32,128]{3,2,1,0:T(8,128)}) %reduce-scatter.7.cloned.1.call-update) | async-done | bytes 262160 | tf_op jit(solution)/shard_map/reduce_scatter | solution.py:53
  490.4 1.0 bitcast_dynamic-update-slice_fusion.5
  491.3 43.8 %reduce-scatter.9.cloned.1.call-done = f32[8,2,32,128]{3,2,1,0:T(8,128)} async-done(((f32[64,2,32,128]{3,2,1,0:T(8,128)}), f32[8,2,32,128]{3,2,1,0:T(8,128)}) %reduce-scatter.9.cloned.1.call-update) | async-done | bytes 262160 | tf_op jit(solution)/shard_map/reduce_scatter | solution.py:53
  535.2 1.0 bitcast_dynamic-update-slice_fusion.4
  536.2 43.9 %reduce-scatter.11.cloned.1.call-done = f32[8,2,32,128]{3,2,1,0:T(8,128)} async-done(((f32[64,2,32,128]{3,2,1,0:T(8,128)}), f32[8,2,32,128]{3,2,1,0:T(8,128)}) %reduce-scatter.11.cloned.1.call-update) | async-done | bytes 262160 | tf_op jit(solution)/shard_map/reduce_scatter | solution.py:53
  580.0 1.0 bitcast_dynamic-update-slice_fusion.3
  581.0 43.7 %reduce-scatter.13.cloned.1.call-done = f32[8,2,32,128]{3,2,1,0:T(8,128)} async-done(((f32[64,2,32,128]{3,2,1,0:T(8,128)}), f32[8,2,32,128]{3,2,1,0:T(8,128)}) %reduce-scatter.13.cloned.1.call-update) | async-done | bytes 262160 | tf_op jit(solution)/shard_map/reduce_scatter | solution.py:53
  624.8 1.0 bitcast_dynamic-update-slice_fusion.2
  625.8 44.3 %reduce-scatter.15.cloned.1.call-done = f32[8,2,32,128]{3,2,1,0:T(8,128)} async-done(((f32[64,2,32,128]{3,2,1,0:T(8,128)}), f32[8,2,32,128]{3,2,1,0:T(8,128)}) %reduce-scatter.15.cloned.1.call-update) | async-done | bytes 262160 | tf_op jit(solution)/shard_map/reduce_scatter | solution.py:53
  670.1 1.0 bitcast_dynamic-update-slice_fusion.1
  671.1 44.1 %reduce-scatter.17.cloned.1.call-done = f32[8,2,32,128]{3,2,1,0:T(8,128)} async-done(((f32[64,2,32,128]{3,2,1,0:T(8,128)}), f32[8,2,32,128]{3,2,1,0:T(8,128)}) %reduce-scatter.17.cloned.1.call-update) | async-done | bytes 262160 | tf_op jit(solution)/shard_map/reduce_scatter | solution.py:53
  715.2 1.6 bitcast_dynamic-update-slice_fusion
  (26 shorter events, 0.3 us)
Async XLA Ops:
  6.5 411.3 %all-reduce.3.cloned.1.call-start = ((), (), s32[]{:S(2)}) async-start(), calls=%async_computation.12 | async-start | bytes 12582912 | tf_op jit(solution)/shard_map/psum | solution.py:13
  73.0 1.6 copy-start.7
  73.0 2.6 copy-start.6
  79.9 410.5 %reduce-scatter.7.cloned.1.call-start = ((), (), s32[]{:S(2)}) async-start(), calls=%async_computation.6 | async-start | bytes 2359296 | tf_op jit(solution)/shard_map/reduce_scatter | solution.py:53
  419.8 2.2 copy-start
  424.1 111.1 %reduce-scatter.9.cloned.1.call-start = ((), (), s32[]{:S(2)}) async-start(), calls=%async_computation.7 | async-start | bytes 2359296 | tf_op jit(solution)/shard_map/reduce_scatter | solution.py:53
  424.2 2.2 copy-start.1
  428.6 1.2 copy-start.10
  428.6 1.5 copy-start.11
  428.6 151.5 %reduce-scatter.11.cloned.1.call-start = ((), (), s32[]{:S(2)}) async-start(), calls=%async_computation.8 | async-start | bytes 2359296 | tf_op jit(solution)/shard_map/reduce_scatter | solution.py:53
  430.6 2.2 copy-start.2
  435.0 189.7 %reduce-scatter.13.cloned.1.call-start = ((), (), s32[]{:S(2)}) async-start(), calls=%async_computation.9 | async-start | bytes 2359296 | tf_op jit(solution)/shard_map/reduce_scatter | solution.py:53
  435.1 2.2 copy-start.3
  439.6 1.2 copy-start.8
  439.6 1.5 copy-start.9
  439.6 230.5 %reduce-scatter.15.cloned.1.call-start = ((), (), s32[]{:S(2)}) async-start(), calls=%async_computation.10 | async-start | bytes 2359296 | tf_op jit(solution)/shard_map/reduce_scatter | solution.py:53
  441.6 2.2 copy-start.4
  446.1 269.1 %reduce-scatter.17.cloned.1.call-start = ((), (), s32[]{:S(2)}) async-start(), calls=%async_computation.11 | async-start | bytes 2359296 | tf_op jit(solution)/shard_map/reduce_scatter | solution.py:53
  446.1 2.2 copy-start.5
  671.0 44.1 %copy-start.12 = (bf16[6,8,2,32,128]{4,3,2,1,0:T(8,128)(2,1)}, bf16[6,8,2,32,128]{4,3,2,1,0:T(8,128)(2,1)S(1)}, u32[]{:S(2)}) copy-start(bf16[6,8,2,32,128]{4,3,2,1,0:T(8,128)(2,1)S(1)} %bitcast_dynamic-update-slice_fusion.1) | copy-start | bytes 2359300
Sparse Core Ops, SparseCore 0:
  80.0 337.8 all-reduce.2
  424.2 66.0 reduce-scatter.6
  492.9 42.2 reduce-scatter.8
  537.6 42.4 reduce-scatter.10
  582.4 42.2 reduce-scatter.12
  627.2 42.8 reduce-scatter.14
  672.6 42.5 reduce-scatter.16
where the time goes:
time: 725 us; the launch traced here: 724 us
  waiting for transfers between devices  597 us (82%)
  local copies, waits for them, and re-layouts  65.5 us (9%)
  between operations  29.7 us (4%)
  other arithmetic  17.6 us (2%)
  matrix products  13.4 us (2%)
    psum x1, waiting for transfers between devices, from_root(): return lax.psum(jnp.where(mine, x, jnp.zeros_like(x)), axis)  337 us
    reduce_scatter x6, waiting for transfers between devices, body(): lax.psum_scatter(correlate(tapered_spectra, spectra) * scale, 'shot', sca...  260 us
    unnamed x32, local copies, waits for them, and re-layouts  39.4 us
    dynamic_slice x1, local copies, waits for them, and re-layouts, source_piece(): return lax.dynamic_slice_in_dim(spectrum_holder, offset, SB, 3)  24.5 us
  transfers between devices with their start and end apart: 7, of which 7 were waited for; matrix products, arithmetic and copies ran while one was open for 3% of the time, Pallas kernels for 0%

commit v1 on v0

v1 whole, which is shorter than its diff:
```python
import jax
import jax.numpy as jnp
import numpy as np
from jax import lax
from jax.sharding import Mesh, PartitionSpec as P

SB = 32
ROUNDS = 6
WINDOWS = 8
PLANE = ("y", "x")


def taper_weights(taper_windows):
    return 0.5 - 0.5 * jnp.cos(jnp.pi * (taper_windows.astype(jnp.float32) + 1.0) / (WINDOWS + 1.0))


def gather_sources(spectra, source_block):
    node_dev = spectra.shape[3]
    per_device = node_dev // SB
    zl_size = lax.axis_size("zl")
    me = (lax.axis_index("y") * lax.axis_size("x") + lax.axis_index("x")) * zl_size + lax.axis_index("zl")
    pieces = []
    for turn in range(ROUNDS):
        block = source_block[turn]
        piece = lax.dynamic_slice_in_dim(spectra, block % per_device * SB, SB, 3)
        mine = me == block // per_device
        pieces.append(jnp.where(mine, piece, jnp.zeros_like(piece)))
    stacked = jnp.stack(pieces, axis=1)
    part = lax.psum_scatter(stacked, PLANE, scatter_dimension=0, tiled=True)
    other = lax.ppermute(part, "zl", perm=[(0, 1), (1, 0)])
    part = part + other
    return lax.all_gather(part, PLANE, axis=0, tiled=True)


def body(spectra, source_block, taper_window):
    shot_dev = spectra.shape[2]
    shot_groups = lax.axis_size("zh") * lax.axis_size("c")
    shot_count = shot_dev * shot_groups
    scale = 1.0 / jnp.sqrt(jnp.float32(shot_count))
    shot_weights = taper_weights(taper_window)
    shot_index = lax.axis_index("zh") * lax.axis_size("c") + lax.axis_index("c")
    local_weights = lax.dynamic_slice_in_dim(shot_weights, shot_index * shot_dev, shot_dev, 1)

    source = gather_sources(spectra, source_block)
    tapered = (
        source.astype(jnp.float32) * local_weights[None, :, None, :, None]
    ).astype(jnp.bfloat16)
    real_part = tapered[:, :, 0]
    imag_part = tapered[:, :, 1]
    real_row = jnp.stack((real_part, imag_part), axis=2)
    imag_row = jnp.stack((-imag_part, real_part), axis=2)
    operator = jnp.stack((real_row, imag_row), axis=2)
    summed = jnp.einsum(
        "froCks,fCkn->frosn", operator, spectra, preferred_element_type=jnp.float32
    )
    reduced = lax.psum_scatter(summed * scale, ("zh", "c"), scatter_dimension=0, tiled=True)
    return jnp.transpose(reduced, (1, 0, 2, 3, 4)).astype(jnp.bfloat16)


def solution(mesh):
    devices = np.asarray(mesh.devices).reshape(4, 4, 2, 4, 2)
    fine = Mesh(devices, ("y", "x", "zl", "zh", "c"))
    in_specs = (P(None, None, ("zh", "c"), ("y", "x", "zl")), P(), P())
    out_specs = P(None, ("zh", "c"), None, None, ("y", "x", "zl"))
    return jax.shard_map(body, mesh=fine, in_specs=in_specs, out_specs=out_specs, check_vma=False)
```

time: 725 us -> 418 us (0.58)
  waiting for transfers between devices: 597 us -> 297 us
  local copies, waits for them, and re-layouts: 65.5 us -> 53.3 us
  other arithmetic: 17.6 us -> 25.8 us
    psum x1 -> x0, waiting for transfers between devices: 337 us -> none  [from_root(): return lax.psum(jnp.where(mine, x, jnp.zeros_like(x)), axis)]
    all_gather x0 -> x1, waiting for transfers between devices: none -> 67.2 us  [gather_sources(): return lax.all_gather(part, PLANE, axis=0, tiled=True)]
    reduce_scatter x6 -> x2, waiting for transfers between devices: 260 us -> 222 us  [the longest x1 134 us: body(): lax.psum_scatter(summed * scale, ('zh', 'c'), scatter_dimension=0, tiled=...]
    unnamed x32 -> x14, local copies, waits for them, and re-layouts: 39.4 us -> 26.4 us
    ppermute x0 -> x1, waiting for transfers between devices: none -> 7.8 us  [gather_sources(): other = lax.ppermute(part, 'zl', perm=[(0, 1), (1, 0)])]
    another operation x7 -> x3, other arithmetic: 2.19 us -> 9.82 us  [the longest x2 8.46 us: body(): operator = jnp.stack((real_row, imag_row), axis=2)]
  transfers between devices with their start and end apart: 7 -> 4, of which waited for: 7 -> 4; matrix products, arithmetic and copies ran while one was open for 3% -> 0% of each run, Pallas kernels for 0% -> 0%
where the time goes in v1:
time: 418 us; the launch traced here: 414 us
  waiting for transfers between devices  297 us (71%)
  local copies, waits for them, and re-layouts  53.3 us (13%)
  between operations  28 us (7%)
  other arithmetic  25.8 us (6%)
  matrix products  8.22 us (2%)
    reduce_scatter x1, waiting for transfers between devices, body(): lax.psum_scatter(summed * scale, ('zh', 'c'), scatter_dimension=0, tiled=...  134 us
    reduce_scatter x1, waiting for transfers between devices, gather_sources(): part = lax.psum_scatter(stacked, PLANE, scatter_dimension=0, tiled=True)  88.3 us
    all_gather x1, waiting for transfers between devices, gather_sources(): return lax.all_gather(part, PLANE, axis=0, tiled=True)  67.2 us
    unnamed x14, local copies, waits for them, and re-layouts  26.4 us
    dynamic_slice x1, local copies, waits for them, and re-layouts, gather_sources(): piece = lax.dynamic_slice_in_dim(spectra, block % per_device * SB, SB, 3)  24.5 us
    another operation x2, other arithmetic, body(): operator = jnp.stack((real_row, imag_row), axis=2)  8.46 us
  transfers between devices with their start and end apart: 4, of which 4 were waited for; matrix products, arithmetic and copies ran while one was open for 0% of the time, Pallas kernels for 0%

profile of v1, /device:TPU:73, one launch (start us, length us, event | category | flops | bytes accessed | tf_op | source)
XLA Modules:
  0.0 413.8 jit_solution(8506234749643340615)
XLA Ops:
  6.5 0.0 reduce-scatter.3.cloned.1.call-start
  6.5 1.5 fusion.13
  22.8 24.5 %constant_dynamic-slice_fusion = (bf16[64,2,128,32]{3,2,1,0:T(8,128)(2,1)}, bf16[64,2,128,32]{3,2,1,0:T(8,128)(2,1)}, bf16[64,2,128,32]{3,2,1,0:T(8,128)(2,1)}, ...) fusion(bf16[64,2,128,128]{3,2,1,0:T(8,128)(2,1)} %param.3, ...), kind=kLoop, calls=%fused_computation.22 | loop fusion | bytes 12582936 | tf_op jit(solution)/shard_map/dynamic_slice | solution.py:25
  47.3 3.6 copy.37
  50.9 3.6 copy.36
  54.5 3.6 copy.35
  58.1 4.6 %copy.34 = bf16[64,2,128,32]{2,3,1,0:T(8,128)(2,1)} copy(bf16[64,2,128,32]{3,2,1,0:T(8,128)(2,1)} %get-tuple-element.10) | data formatting | bytes 2097152
  62.6 4.6 %copy.33 = bf16[64,2,128,32]{2,3,1,0:T(8,128)(2,1)} copy(bf16[64,2,128,32]{3,2,1,0:T(8,128)(2,1)} %get-tuple-element.11) | data formatting | bytes 2097152
  67.2 4.6 %copy.32 = bf16[64,2,128,32]{2,3,1,0:T(8,128)(2,1)} copy(bf16[64,2,128,32]{3,2,1,0:T(8,128)(2,1)} %get-tuple-element.12) | data formatting | bytes 2097152
  71.8 1.3 bitcast_dynamic-update-slice_fusion.4
  73.2 1.4 bitcast_dynamic-update-slice_fusion.3
  74.5 1.4 bitcast_dynamic-update-slice_fusion.2
  75.9 1.3 bitcast_dynamic-update-slice_fusion.1
  77.2 1.3 bitcast_dynamic-update-slice_fusion
  78.5 1.4 bitcast_dynamic-update-slice_fusion.5
  79.9 0.0 reduce-scatter.3.cloned.1.call-update
  79.9 0.0 all-gather.2.cloned.1.call-start
  80.0 88.3 %reduce-scatter.3.cloned.1.call-done = bf16[4,6,2,128,32]{3,4,2,1,0:T(8,128)(2,1)} async-done(((bf16[64,6,2,128,32]{3,4,2,1,0:T(8,128)(2,1)}), bf16[4,6,2,128,32]{3,4,2,1,0:T(8,128)(2,1)}) %reduce-scatter.3.cloned.1.call-update) | async-done | bytes 393232 | tf_op jit(solution)/shard_map/reduce_scatter | solution.py:29
  168.2 1.2 collective-permute-start
  169.5 7.8 %collective-permute-done = bf16[4,6,2,128,32]{3,4,2,1,0:T(8,128)(2,1)S(1)} collective-permute-done((bf16[4,6,2,128,32]{3,4,2,1,0:T(8,128)(2,1)}, bf16[4,6,2,128,32]{3,4,2,1,0:T(8,128)(2,1)S(1)}, u32[]{:S(2)}, u32[]{:S(2)}) %collective-permute-start) | collective-permute-done | bytes 393248 | tf_op jit(solution)/shard_map/ppermute | solution.py:30
  177.3 1.9 add.82
  179.2 0.0 all-gather.2.cloned.1.call-update
  179.2 0.2 reduce-scatter.5.cloned.1.call-start
  179.4 0.7 fusion.11
  180.2 67.2 %all-gather.2.cloned.1.call-done = bf16[64,6,2,128,32]{3,4,2,1,0:T(8,128)(2,1)} async-done(((bf16[4,6,2,128,32]{3,4,2,1,0:T(8,128)(2,1)}), bf16[64,6,2,128,32]{3,4,2,1,0:T(8,128)(2,1)}) %all-gather.2.cloned.1.call-update) | async-done | bytes 6291472 | tf_op jit(solution)/shard_map/all_gather | solution.py:32
  247.4 4.4 %multiply_convert_fusion = bf16[64,6,2,128,32]{3,4,2,1,0:T(8,128)(2,1)S(1)} fusion(bf16[64,6,2,128,32]{3,4,2,1,0:T(8,128)(2,1)} %all-gather.2.cloned.1.call-done, f32[6,128]{1,0:T(8,128)S(1)} %fusion.11), kind=kLoop, calls=%fused_computation.5 | loop fusion | flops 9437184 | bytes 12585984 | tf_op jit(solution)/shard_map/convert_element_type | solution.py:47
  251.8 0.0 slice-start
  251.8 0.6 slice_negate_fusion
  252.5 0.0 slice-start.1
  252.5 3.4 maximum_bitcast_fusion
  255.9 0.0 slice-done
  255.9 0.6 slice-done.1
  256.5 0.0 copy-start
  256.5 0.0 copy-start.1
  256.5 5.0 %fusion.14 = bf16[64,6,1,2,128,32]{4,5,3,2,1,0:T(8,128)(2,1)} fusion(f32[6,128]{1,0:T(8,128)S(1)} %fusion.11, bf16[64,6,2,128,32]{3,4,2,1,0:T(8,128)(2,1)S(1)} %bitcast.45), kind=kLoop, calls=%fused_computation.30 | loop fusion | flops 9437184 | bytes 12585984 | tf_op jit(solution)/shard_map/stack | solution.py:52
  261.5 0.0 copy-done
  261.5 1.3 copy-done.1
  262.8 8.2 %bitcast_multiply_fusion = f32[64,6,2,32,128]{4,3,2,1,0:T(8,128)} fusion(bf16[64,6,1,2,128,32]{4,5,3,2,1,0:T(8,128)(2,1)S(1)} %copy-done.1, bf16[64,6,1,2,128,32]{4,5,3,2,1,0:T(8,128)(2,1)} %fusion.14, bf16[64,2,128,128]{3,2,1,0:T(8,128)(2,1)S(1)} %copy-done), kind=kOutput, calls=%fused_computation.4 | convolution fusion | flops 1620049920 | bytes 29360128 | tf_op jit(solution)/shard_map/froCks,fCkn->frosn/dot_general | solution.py:53
  271.1 0.0 reduce-scatter.5.cloned.1.call-update
  271.1 133.6 %reduce-scatter.5.cloned.1.call-done = f32[8,6,2,32,128]{4,3,2,1,0:T(8,128)} async-done(((f32[64,6,2,32,128]{4,3,2,1,0:T(8,128)}), f32[8,6,2,32,128]{4,3,2,1,0:T(8,128)}) %reduce-scatter.5.cloned.1.call-update) | async-done | bytes 1572880 | tf_op jit(solution)/shard_map/reduce_scatter | solution.py:56
  404.7 1.6 convert_bitcast_fusion
  406.3 0.9 copy.29
  (1 shorter events, 0.0 us)
Async XLA Ops:
  6.5 161.7 %reduce-scatter.3.cloned.1.call-start = ((), (), s32[]{:S(2)}) async-start(), calls=%async_computation.2 | async-start | bytes 6684672 | tf_op jit(solution)/shard_map/reduce_scatter | solution.py:29
  79.9 167.5 %all-gather.2.cloned.1.call-start = ((), (), s32[]{:S(2)}) async-start(), calls=%async_computation.3 | async-start | bytes 6684672 | tf_op jit(solution)/shard_map/all_gather | solution.py:32
  168.2 9.0 %collective-permute-start = (bf16[4,6,2,128,32]{3,4,2,1,0:T(8,128)(2,1)}, bf16[4,6,2,128,32]{3,4,2,1,0:T(8,128)(2,1)S(1)}, u32[]{:S(2)}, u32[]{:S(2)}) collective-permute-start(bf16[4,6,2,128,32]{3,4,2,1,0:T(8,128)(2,1)} %reduce-scatter.3.cloned.1.call-done), channel_id=1, source_target_pairs={{0,8},{8,0},{1,9},{9,1},{2,10},{10,2},{3,11},{11,3},{4,12},{12,4},... | collective-permute-start | bytes 1179656 | tf_op jit(solution)/shard_map/ppermute | solution.py:30
  179.2 225.5 %reduce-scatter.5.cloned.1.call-start = ((), (), s32[]{:S(2)}) async-start(), calls=%async_computation.4 | async-start | bytes 14155776 | tf_op jit(solution)/shard_map/reduce_scatter | solution.py:56
  251.8 4.1 slice-start
  252.5 4.0 slice-start.1
  256.5 5.0 %copy-start = (bf16[64,2,128,128]{3,2,1,0:T(8,128)(2,1)S(1)}, bf16[64,2,128,128]{3,2,1,0:T(8,128)(2,1)}, u32[]{:S(2)}) copy-start(bf16[64,2,128,128]{3,2,1,0:T(8,128)(2,1)} %param.3) | copy-start | bytes 12582916
  256.5 6.3 %copy-start.1 = (bf16[64,6,1,2,128,32]{4,5,3,2,1,0:T(8,128)(2,1)S(1)}, bf16[64,6,1,2,128,32]{4,5,3,2,1,0:T(8,128)(2,1)}, u32[]{:S(2)}) copy-start(bf16[64,6,1,2,128,32]{4,5,3,2,1,0:T(8,128)(2,1)} %maximum_bitcast_fusion) | copy-start | bytes 18874372
Sparse Core Ops, SparseCore 0:
  80.1 88.1 reduce-scatter.2
  179.3 68.0 all-gather.1
  271.2 133.4 reduce-scatter.4

commit v2 on v1

v2 whole, which is shorter than its diff:
```python
import jax
import jax.numpy as jnp
import numpy as np
from jax import lax
from jax.sharding import Mesh, PartitionSpec as P

SB = 32
ROUNDS = 6
WINDOWS = 8
PLANE = ("y", "x")


def taper_weights(taper_windows):
    return 0.5 - 0.5 * jnp.cos(jnp.pi * (taper_windows.astype(jnp.float32) + 1.0) / (WINDOWS + 1.0))


def gather_sources(spectra, source_block):
    node_dev = spectra.shape[3]
    per_device = node_dev // SB
    me = (lax.axis_index("y") * lax.axis_size("x") + lax.axis_index("x")) * lax.axis_size("zl") + lax.axis_index("zl")
    owner = source_block // per_device
    first = source_block % per_device * SB
    column = jnp.arange(ROUNDS * SB, dtype=jnp.int32)
    wanted = first[column // SB] + column % SB
    keep = owner[column // SB] == me
    node = jnp.arange(node_dev, dtype=jnp.int32)
    select = ((node[:, None] == wanted[None, :]) & keep[None, :]).astype(spectra.dtype)
    picked = jnp.einsum("fckn,nq->fcqk", spectra, select, preferred_element_type=jnp.float32)
    picked = picked.astype(spectra.dtype)
    part = lax.psum_scatter(picked, PLANE, scatter_dimension=0, tiled=True)
    other = lax.ppermute(part, "zl", perm=[(0, 1), (1, 0)])
    return lax.all_gather(part + other, PLANE, axis=0, tiled=True)


def body(spectra, source_block, taper_window):
    freqs, _, shot_dev, node_dev = spectra.shape
    shot_groups = lax.axis_size("zh") * lax.axis_size("c")
    scale = 1.0 / jnp.sqrt(jnp.float32(shot_dev * shot_groups))
    shot_weights = taper_weights(taper_window)
    shot_index = lax.axis_index("zh") * lax.axis_size("c") + lax.axis_index("c")
    local_weights = lax.dynamic_slice_in_dim(shot_weights, shot_index * shot_dev, shot_dev, 1)
    weight_rows = jnp.repeat(local_weights, SB, axis=0)

    source = gather_sources(spectra, source_block)
    tapered = (source.astype(jnp.float32) * weight_rows[None, None]).astype(jnp.bfloat16)
    real_part = tapered[:, 0]
    imag_part = tapered[:, 1]
    real_row = jnp.concatenate((real_part, imag_part), axis=2)
    imag_row = jnp.concatenate((-imag_part, real_part), axis=2)
    operator = jnp.stack((real_row, imag_row), axis=1)
    receivers = spectra.reshape(freqs, 2 * shot_dev, node_dev)
    summed = jnp.einsum("foqK,fKn->foqn", operator, receivers, preferred_element_type=jnp.float32)
    reduced = lax.psum_scatter(summed * scale, ("zh", "c"), scatter_dimension=0, tiled=True)
    local_f = reduced.shape[0]
    reduced = reduced.reshape(local_f, 2, ROUNDS, SB, node_dev)
    return jnp.transpose(reduced, (2, 0, 1, 3, 4)).astype(jnp.bfloat16)


def solution(mesh):
    devices = np.asarray(mesh.devices).reshape(4, 4, 2, 4, 2)
    fine = Mesh(devices, ("y", "x", "zl", "zh", "c"))
    in_specs = (P(None, None, ("zh", "c"), ("y", "x", "zl")), P(), P())
    out_specs = P(None, ("zh", "c"), None, None, ("y", "x", "zl"))
    return jax.shard_map(body, mesh=fine, in_specs=in_specs, out_specs=out_specs, check_vma=False)
```

time: 418 us -> 353 us (0.84)
  local copies, waits for them, and re-layouts: 53.3 us -> 2.14 us
  between operations: 28 us -> 13.2 us
  matrix products: 8.22 us -> 15.5 us
  other arithmetic: 25.8 us -> 19.3 us
    unnamed x14 -> x0, local copies, waits for them, and re-layouts: 26.4 us -> none
    dynamic_slice x1 -> x0, local copies, waits for them, and re-layouts: 24.5 us -> none  [gather_sources(): piece = lax.dynamic_slice_in_dim(spectra, block % per_device * SB, SB, 3)]
    another operation x3 -> x1, other arithmetic: 9.82 us -> 2.14 us  [body(): operator = jnp.stack((real_row, imag_row), axis=1)]
    dot_general x1 -> x2, matrix products: 8.22 us -> 15.5 us  [the longest x1 8.85 us: body(): jnp.einsum('foqK,fKn->foqn', operator, receivers, preferred_element_type=...]
    unnamed x6 -> x0, other arithmetic: 6.74 us -> none
where the time goes in v2:
time: 353 us; the launch traced here: 348 us
  waiting for transfers between devices  297 us (84%)
  other arithmetic  19.3 us (5%)
  matrix products  15.5 us (4%)
  between operations  13.2 us (4%)
    reduce_scatter x1, waiting for transfers between devices, body(): lax.psum_scatter(summed * scale, ('zh', 'c'), scatter_dimension=0, tiled=...  134 us
    reduce_scatter x1, waiting for transfers between devices, gather_sources(): part = lax.psum_scatter(picked, PLANE, scatter_dimension=0, tiled=True)  87.2 us
    all_gather x1, waiting for transfers between devices, gather_sources(): return lax.all_gather(part + other, PLANE, axis=0, tiled=True)  67.4 us
    dot_general x1, matrix products, body(): jnp.einsum('foqK,fKn->foqn', operator, receivers, preferred_element_type=...  8.85 us
    ppermute x1, waiting for transfers between devices, gather_sources(): other = lax.ppermute(part, 'zl', perm=[(0, 1), (1, 0)])  7.78 us
  transfers between devices with their start and end apart: 4, of which 4 were waited for; matrix products, arithmetic and copies ran while one was open for 0% of the time, Pallas kernels for 0%

profile of v2, /device:TPU:73, one launch (start us, length us, event | category | flops | bytes accessed | tf_op | source)
XLA Modules:
  0.0 348.2 jit_solution(2583839031813979429)
XLA Ops:
  6.5 0.0 reduce-scatter.3.cloned.1.call-start
  6.5 0.7 and_select_fusion.1
  7.2 0.7 fusion.20
  7.9 3.7 %compare_select_fusion.1 = s32[192,1]{0,1:T(1,128)S(1)} fusion(s32[]{:T(128)} %bitcast, s32[]{:T(128)} %bitcast.1, s32[]{:T(128)} %bitcast.2, s32[]{:T(128)} %bitcast.3, s32[]{:T(128)} %bitcast.5, s32[]{:T(128)} %bitcast.4), kind=kLoop, calls=%fused_computation.26 | loop fusion | flops 4032 | bytes 792 | tf_op jit(solution)/shard_map/gather | solution.py:24
  11.6 3.8 %compare_reduce_fusion = pred[192]{0:T(512)(128)(4,1)S(1)} fusion(s32[]{:T(128)S(6)} %add.75, s32[]{:T(128)} %bitcast.7, s32[]{:T(128)} %bitcast.8, s32[]{:T(128)} %bitcast.9, s32[]{:T(128)} %bitcast.10, s32[]{:T(128)} %bitcast.12, s32[]{:T(128)} %bitcast.11), kind=kLoop, calls=%fused_computation.24 | loop fusion | flops 4224 | bytes 220 | tf_op jit(solution)/shard_map/eq | solution.py:25
  15.4 6.7 %convert_bitcast_fusion = bf16[64,2,192,128]{3,2,1,0:T(8,128)(2,1)} fusion(bf16[64,2,128,128]{3,2,1,0:T(8,128)(2,1)} %param.3, s32[192]{0:T(256)S(1)} %fusion.16, pred[192]{0:T(512)(128)(4,1)S(1)} %compare_reduce_fusion), kind=kOutput, calls=%fused_computation.8 | convolution fusion | flops 808501248 | bytes 10486720 | tf_op jit(solution)/shard_map/fckn,nq->fcqk/dot_general | solution.py:28
  22.1 0.0 reduce-scatter.3.cloned.1.call-update
  22.1 0.0 all-gather.2.cloned.1.call-start
  22.2 87.2 %reduce-scatter.3.cloned.1.call-done = bf16[4,2,192,128]{3,2,1,0:T(8,128)(2,1)} async-done(((bf16[64,2,192,128]{3,2,1,0:T(8,128)(2,1)}), bf16[4,2,192,128]{3,2,1,0:T(8,128)(2,1)}) %reduce-scatter.3.cloned.1.call-update) | async-done | bytes 393232 | tf_op jit(solution)/shard_map/reduce_scatter | solution.py:30
  109.4 1.3 collective-permute-start
  110.6 7.8 %collective-permute-done = bf16[4,2,192,128]{3,2,1,0:T(8,128)(2,1)S(1)} collective-permute-done((bf16[4,2,192,128]{3,2,1,0:T(8,128)(2,1)}, bf16[4,2,192,128]{3,2,1,0:T(8,128)(2,1)S(1)}, u32[]{:S(2)}, u32[]{:S(2)}) %collective-permute-start) | collective-permute-done | bytes 393248 | tf_op jit(solution)/shard_map/ppermute | solution.py:31
  118.4 1.8 add.76
  120.3 0.0 all-gather.2.cloned.1.call-update
  120.3 0.0 reduce-scatter.5.cloned.1.call-start
  120.3 0.7 fusion.15
  121.1 67.4 %all-gather.2.cloned.1.call-done = bf16[64,2,192,128]{3,2,1,0:T(8,128)(2,1)} async-done(((bf16[4,2,192,128]{3,2,1,0:T(8,128)(2,1)}), bf16[64,2,192,128]{3,2,1,0:T(8,128)(2,1)}) %all-gather.2.cloned.1.call-update) | async-done | bytes 6291472 | tf_op jit(solution)/shard_map/all_gather | solution.py:32
  188.5 4.5 %multiply_convert_fusion = bf16[64,2,192,128]{3,2,0,1:T(8,128)(2,1)S(1)} fusion(bf16[64,2,192,128]{3,2,1,0:T(8,128)(2,1)} %all-gather.2.cloned.1.call-done, f32[192,128]{1,0:T(8,128)S(1)} %bitcast.46), kind=kLoop, calls=%fused_computation.4 | loop fusion | flops 9437184 | bytes 12681216 | tf_op jit(solution)/shard_map/convert_element_type | solution.py:45
  193.0 0.4 fusion.19
  193.5 0.4 slice_bitcast_fusion
  193.9 2.1 maximum_bitcast_fusion
  196.1 8.8 %broadcast_multiply_fusion = f32[64,2,192,128]{3,2,1,0:T(8,128)} fusion(bf16[64,256,128,1]{2,1,3,0:T(8,128)(2,1)} %bitcast.44, bf16[64,1,192,256]{3,2,1,0:T(8,128)(2,1)S(1)} %get-tuple-element.8, bf16[64,1,192,256]{3,2,1,0:T(8,128)(2,1)S(1)} %get-tuple-element.7), kind=kOutput, calls=%fused_computation.7 | convolution fusion | flops 1620049920 | bytes 29360128 | tf_op jit(solution)/shard_map/foqK,fKn->foqn/dot_general | solution.py:52
  204.9 0.0 reduce-scatter.5.cloned.1.call-update
  204.9 134.2 %reduce-scatter.5.cloned.1.call-done = f32[8,2,192,128]{3,2,1,0:T(8,128)} async-done(((f32[64,2,192,128]{3,2,1,0:T(8,128)}), f32[8,2,192,128]{3,2,1,0:T(8,128)}) %reduce-scatter.5.cloned.1.call-update) | async-done | bytes 1572880 | tf_op jit(solution)/shard_map/reduce_scatter | solution.py:53
  339.1 1.5 convert_element_type.30
  340.7 1.0 copy.17
  (2 shorter events, 0.0 us)
Async XLA Ops:
  6.5 102.8 %reduce-scatter.3.cloned.1.call-start = ((), (), s32[]{:S(2)}) async-start(), calls=%async_computation.2 | async-start | bytes 6684672 | tf_op jit(solution)/shard_map/reduce_scatter | solution.py:30
  22.1 166.4 %all-gather.2.cloned.1.call-start = ((), (), s32[]{:S(2)}) async-start(), calls=%async_computation.3 | async-start | bytes 6684672 | tf_op jit(solution)/shard_map/all_gather | solution.py:32
  109.4 9.1 %collective-permute-start = (bf16[4,2,192,128]{3,2,1,0:T(8,128)(2,1)}, bf16[4,2,192,128]{3,2,1,0:T(8,128)(2,1)S(1)}, u32[]{:S(2)}, u32[]{:S(2)}) collective-permute-start(bf16[4,2,192,128]{3,2,1,0:T(8,128)(2,1)} %reduce-scatter.3.cloned.1.call-done), channel_id=1, source_target_pairs={{0,8},{8,0},{1,9},{9,1},{2,10},{10,2},{3,11},{11,3},{4,12},{12,4},... | collective-permute-start | bytes 1179656 | tf_op jit(solution)/shard_map/ppermute | solution.py:31
  120.3 218.9 %reduce-scatter.5.cloned.1.call-start = ((), (), s32[]{:S(2)}) async-start(), calls=%async_computation.4 | async-start | bytes 14155776 | tf_op jit(solution)/shard_map/reduce_scatter | solution.py:53
Sparse Core Ops, SparseCore 0:
  22.2 87.0 reduce-scatter.2
  120.4 68.0 all-gather.1
  205.1 134.0 reduce-scatter.4

commit v3 on v2

v3 whole, which is shorter than its diff:
```python
import jax
import jax.numpy as jnp
import numpy as np
from jax import lax
from jax.sharding import Mesh, PartitionSpec as P

SB = 32
ROUNDS = 6
WINDOWS = 8
CHUNKS = 2
PLANE = ("y", "x")


def taper_weights(taper_windows):
    return 0.5 - 0.5 * jnp.cos(jnp.pi * (taper_windows.astype(jnp.float32) + 1.0) / (WINDOWS + 1.0))


def pick_sources(spectra, source_block):
    node_dev = spectra.shape[3]
    per_device = node_dev // SB
    me = (lax.axis_index("y") * lax.axis_size("x") + lax.axis_index("x")) * lax.axis_size("zl") + lax.axis_index("zl")
    owner = source_block // per_device
    first = source_block % per_device * SB
    column = jnp.arange(ROUNDS * SB, dtype=jnp.int32)
    wanted = first[column // SB] + column % SB
    keep = owner[column // SB] == me
    node = jnp.arange(node_dev, dtype=jnp.int32)
    select = ((node[:, None] == wanted[None, :]) & keep[None, :]).astype(spectra.dtype)
    select = select.reshape(node_dev, CHUNKS, ROUNDS * SB // CHUNKS)
    picked = jnp.einsum("fckn,nhq->hfcqk", spectra, select, preferred_element_type=jnp.float32)
    return picked.astype(spectra.dtype)


def broadcast(piece, pending=None):
    part = lax.psum_scatter(piece, PLANE, scatter_dimension=0, tiled=True)
    other = lax.ppermute(part, "zl", perm=[(0, 1), (1, 0)])
    part = part + other
    if pending is not None:
        part, pending = lax.optimization_barrier((part, pending))
    return lax.all_gather(part, PLANE, axis=0, tiled=True), pending


def shot_reduce(partial):
    nz = lax.axis_size("zh")
    nc = lax.axis_size("c")
    zh = lax.axis_index("zh")
    c = lax.axis_index("c")
    freqs = partial.shape[0]
    grouped = partial.reshape(nz, nc, freqs // (nz * nc), *partial.shape[1:])
    send = lax.dynamic_index_in_dim(grouped, 1 - c, axis=1, keepdims=False)
    keep = lax.dynamic_index_in_dim(grouped, c, axis=1, keepdims=False)
    mine = keep + lax.ppermute(send, "c", perm=[(0, 1), (1, 0)])
    half = mine.shape[-1] // 2
    forward = mine[..., :half]
    backward = mine[..., half:]
    up = [(j, (j + 1) % nz) for j in range(nz)]
    down = [(j, (j - 1) % nz) for j in range(nz)]
    acc_f = lax.dynamic_index_in_dim(forward, (zh - 1) % nz, axis=0, keepdims=False)
    acc_b = lax.dynamic_index_in_dim(backward, (zh + 1) % nz, axis=0, keepdims=False)
    for step in range(nz - 1):
        got_f = lax.ppermute(acc_f, "zh", perm=up)
        got_b = lax.ppermute(acc_b, "zh", perm=down)
        acc_f = got_f + lax.dynamic_index_in_dim(forward, (zh - 2 - step) % nz, axis=0, keepdims=False)
        acc_b = got_b + lax.dynamic_index_in_dim(backward, (zh + 2 + step) % nz, axis=0, keepdims=False)
    return jnp.concatenate((acc_f, acc_b), axis=-1)


def body(spectra, source_block, taper_window):
    freqs, _, shot_dev, node_dev = spectra.shape
    shot_groups = lax.axis_size("zh") * lax.axis_size("c")
    scale = 1.0 / jnp.sqrt(jnp.float32(shot_dev * shot_groups))
    shot_weights = taper_weights(taper_window)
    shot_index = lax.axis_index("zh") * lax.axis_size("c") + lax.axis_index("c")
    local_weights = lax.dynamic_slice_in_dim(shot_weights, shot_index * shot_dev, shot_dev, 1)
    weight_rows = jnp.repeat(local_weights, SB, axis=0).reshape(CHUNKS, -1, shot_dev)
    receivers = spectra.reshape(freqs, 2 * shot_dev, node_dev)

    picked = pick_sources(spectra, source_block)
    results = []
    summed = None
    for chunk in range(CHUNKS):
        piece = picked[chunk]
        pending = None
        if summed is not None:
            piece, summed = lax.optimization_barrier((piece, summed))
            pending = shot_reduce(summed * scale)
        source, pending = broadcast(piece, pending)
        if pending is not None:
            results.append(pending)
        tapered = (source.astype(jnp.float32) * weight_rows[chunk][None, None]).astype(jnp.bfloat16)
        real_part = tapered[:, 0]
        imag_part = tapered[:, 1]
        real_row = jnp.concatenate((real_part, imag_part), axis=2)
        imag_row = jnp.concatenate((-imag_part, real_part), axis=2)
        operator = jnp.stack((real_row, imag_row), axis=1)
        summed = jnp.einsum("foqK,fKn->foqn", operator, receivers, preferred_element_type=jnp.float32)
    results.append(shot_reduce(summed * scale))
    reduced = jnp.concatenate(results, axis=2)
    local_f = reduced.shape[0]
    reduced = reduced.reshape(local_f, 2, ROUNDS, SB, node_dev)
    return jnp.transpose(reduced, (2, 0, 1, 3, 4)).astype(jnp.bfloat16)


def solution(mesh):
    devices = np.asarray(mesh.devices).reshape(4, 4, 2, 4, 2)
    fine = Mesh(devices, ("y", "x", "zl", "zh", "c"))
    in_specs = (P(None, None, ("zh", "c"), ("y", "x", "zl")), P(), P())
    out_specs = P(None, ("zh", "c"), None, None, ("y", "x", "zl"))
    return jax.shard_map(body, mesh=fine, in_specs=in_specs, out_specs=out_specs, check_vma=False)
```

time: 353 us -> 473 us (1.34)
  local copies, waits for them, and re-layouts: 2.14 us -> 58.1 us
  other arithmetic: 19.3 us -> 50.2 us
  starting transfers between devices: 1.36 us -> 26.7 us
  waiting for transfers between devices: 297 us -> 308 us
  matrix products: 15.5 us -> 9.63 us
    reduce_scatter x2, waiting for transfers between devices: 221 us -> 80.6 us  [broadcast(): part = lax.psum_scatter(piece, PLANE, scatter_dimension=0, tiled=True)]
    ppermute x1 -> x16, waiting for transfers between devices: 7.78 us -> 119 us  [the longest x6 73.8 us: shot_reduce(): got_b = lax.ppermute(acc_b, 'zh', perm=down)]
    all_gather x1 -> x2, waiting for transfers between devices: 67.4 us -> 109 us  [broadcast(): return (lax.all_gather(part, PLANE, axis=0, tiled=True), pending)]
    dynamic_slice x0 -> x16, local copies, waits for them, and re-layouts: none -> 32.2 us  [the longest x6 11.7 us: shot_reduce(): lax.dynamic_index_in_dim(forward, (zh - 2 - step) % nz, axis=0, keepdims=...]
    ppermute x1 -> x16, starting transfers between devices: 1.27 us -> 26.5 us  [the longest x6 12.1 us: shot_reduce(): got_b = lax.ppermute(acc_b, 'zh', perm=down)]
    add x2 -> x15, other arithmetic: 1.85 us -> 24.9 us  [the longest x5 9.51 us: shot_reduce(): got_f + lax.dynamic_index_in_dim(forward, (zh - 2 - step) % nz, axis=0, k...]
    ppermute x0 -> x4, local copies, waits for them, and re-layouts: none -> 8.8 us  [the longest x2 4.4 us: shot_reduce(): got_b = lax.ppermute(acc_b, 'zh', perm=down)]
    unnamed x0 -> x14, local copies, waits for them, and re-layouts: none -> 8.17 us
  transfers between devices with their start and end apart: 4 -> 20, of which waited for: 4 -> 17; matrix products, arithmetic and copies ran while one was open for 0% -> 13% of each run, Pallas kernels for 0% -> 0%
where the time goes in v3:
time: 473 us; the launch traced here: 466 us
  waiting for transfers between devices  308 us (65%)
  local copies, waits for them, and re-layouts  58.1 us (12%)
  other arithmetic  50.2 us (11%)
  starting transfers between devices  26.7 us (6%)
  between operations  13.4 us (3%)
  matrix products  9.63 us (2%)
    all_gather x2, waiting for transfers between devices, broadcast(): return (lax.all_gather(part, PLANE, axis=0, tiled=True), pending)  109 us
    reduce_scatter x2, waiting for transfers between devices, broadcast(): part = lax.psum_scatter(piece, PLANE, scatter_dimension=0, tiled=True)  80.6 us
    ppermute x6, waiting for transfers between devices, shot_reduce(): got_b = lax.ppermute(acc_b, 'zh', perm=down)  73.8 us
    ppermute x6, waiting for transfers between devices, shot_reduce(): got_f = lax.ppermute(acc_f, 'zh', perm=up)  30.2 us
    ppermute x6, starting transfers between devices, shot_reduce(): got_b = lax.ppermute(acc_b, 'zh', perm=down)  12.1 us
    dynamic_slice x6, local copies, waits for them, and re-layouts, shot_reduce(): lax.dynamic_index_in_dim(forward, (zh - 2 - step) % nz, axis=0, keepdims=...  11.7 us
    dynamic_slice x6, local copies, waits for them, and re-layouts, shot_reduce(): lax.dynamic_index_in_dim(backward, (zh + 2 + step) % nz, axis=0, keepdims...  11.7 us
    ppermute x2, waiting for transfers between devices, shot_reduce(): mine = keep + lax.ppermute(send, 'c', perm=[(0, 1), (1, 0)])  10.6 us
  transfers between devices with their start and end apart: 20, of which 17 were waited for; matrix products, arithmetic and copies ran while one was open for 13% of the time, Pallas kernels for 0%

profile of v3, /device:TPU:73, one launch (start us, length us, event | category | flops | bytes accessed | tf_op | source)
XLA Modules:
  0.0 466.2 jit_solution(1348825625948598850)
XLA Ops:
  7.9 3.7 fusion.28
  11.7 3.8 compare_reduce_fusion
  15.6 4.0 convert_bitcast_fusion
  19.6 3.9 slice_bitcast_fusion
  23.5 80.6 %reduce-scatter.3.cloned.1.call-done = bf16[4,2,96,128]{3,2,1,0:T(8,128)(2,1)} async-done(((bf16[64,2,96,128]{3,2,1,0:T(8,128)(2,1)}), bf16[4,2,96,128]{3,2,1,0:T(8,128)(2,1)}) %reduce-scatter.3.cloned.1.call-update) | async-done | bytes 196624 | tf_op jit(solution)/shard_map/reduce_scatter | solution.py:35
  105.4 3.5 collective-permute-done
  108.8 1.7 add.230
  111.3 53.5 %all-gather.3.cloned.1.call-done = bf16[64,2,96,128]{3,2,1,0:T(8,128)(2,1)} async-done(((bf16[4,2,96,128]{3,2,1,0:T(8,128)(2,1)}), bf16[64,2,96,128]{3,2,1,0:T(8,128)(2,1)}) %all-gather.3.cloned.1.call-update) | async-done | bytes 3145744 | tf_op jit(solution)/shard_map/all_gather | solution.py:40
  164.8 2.5 multiply_convert_fusion.1
  169.9 3.6 fusion
  173.6 3.4 broadcast_multiply_fusion.1
  177.3 2.4 copy-done
  179.7 1.6 collective-permute-start.2
  181.4 5.3 %collective-permute-done.2 = f32[4,8,2,96,128]{4,3,2,1,0:T(8,128)} collective-permute-done((f32[4,8,2,96,128]{4,3,2,1,0:T(8,128)S(1)}, f32[4,8,2,96,128]{4,3,2,1,0:T(8,128)}, u32[]{:S(2)}, u32[]{:S(2)}) %collective-permute-start.2) | collective-permute-done | bytes 3145760 | tf_op jit(solution)/shard_map/ppermute | solution.py:52
  186.7 3.4 bitcast_add_fusion.1
  191.3 1.6 copy-done.1
  194.4 2.2 copy.19
  196.7 1.5 constant_dynamic-slice_fusion.9
  198.2 2.2 copy.15
  200.4 3.5 collective-permute-start.3
  203.8 2.2 copy.20
  206.0 2.2 copy.16
  208.2 15.2 %collective-permute-done.6 = f32[8,2,96,64]{2,3,1,0:T(8,128)} collective-permute-done((f32[8,2,96,64]{2,3,1,0:T(8,128)}, f32[8,2,96,64]{2,3,1,0:T(8,128)}, u32[]{:S(2)}, u32[]{:S(2)}) %collective-permute-start.6) | collective-permute-done | bytes 393248 | tf_op jit(solution)/shard_map/ppermute | solution.py:62
  223.5 2.1 bitcast_add_fusion.11
  225.5 5.6 %collective-permute-start.7 = (f32[8,2,96,64]{2,3,1,0:T(8,128)}, f32[8,2,96,64]{2,3,1,0:T(8,128)}, u32[]{:S(2)}, u32[]{:S(2)}) collective-permute-start(f32[8,2,96,64]{2,3,1,0:T(8,128)} %bitcast_add_fusion.11), channel_id=1, source_target_pairs={{0,6},{2,0},{4,2},{6,4},{1,7},{3,1},{5,3},{7,5},{8,14},{10,8},{12,... | collective-permute-start | bytes 1179656 | tf_op jit(solution)/shard_map/ppermute | solution.py:62
  231.2 2.0 bitcast_add_fusion.13
  233.2 2.2 copy.21
  235.4 2.2 copy.17
  237.6 11.0 %collective-permute-done.7 = f32[8,2,96,64]{2,3,1,0:T(8,128)} collective-permute-done((f32[8,2,96,64]{2,3,1,0:T(8,128)}, f32[8,2,96,64]{2,3,1,0:T(8,128)}, u32[]{:S(2)}, u32[]{:S(2)}) %collective-permute-start.7) | collective-permute-done | bytes 393248 | tf_op jit(solution)/shard_map/ppermute | solution.py:62
  248.7 2.1 bitcast_add_fusion.10
  251.0 8.3 %collective-permute-done.4 = f32[8,2,96,64]{2,3,1,0:T(8,128)} collective-permute-done((f32[8,2,96,64]{2,3,1,0:T(8,128)}, f32[8,2,96,64]{2,3,1,0:T(8,128)}, u32[]{:S(2)}, u32[]{:S(2)}) %collective-permute-start.4) | collective-permute-done | bytes 393248 | tf_op jit(solution)/shard_map/ppermute | solution.py:61
  259.3 2.1 bitcast_add_fusion.12
  261.4 10.6 %collective-permute-done.8 = f32[8,2,96,64]{2,3,1,0:T(8,128)} collective-permute-done((f32[8,2,96,64]{2,3,1,0:T(8,128)}, f32[8,2,96,64]{2,3,1,0:T(8,128)}, u32[]{:S(2)}, u32[]{:S(2)}) %collective-permute-start.8) | collective-permute-done | bytes 393248 | tf_op jit(solution)/shard_map/ppermute | solution.py:62
  272.0 2.2 copy.22
  274.2 7.6 %collective-permute-done.5 = f32[8,2,96,64]{2,3,1,0:T(8,128)} collective-permute-done((f32[8,2,96,64]{2,3,1,0:T(8,128)}, f32[8,2,96,64]{2,3,1,0:T(8,128)}, u32[]{:S(2)}, u32[]{:S(2)}) %collective-permute-start.5) | collective-permute-done | bytes 393248 | tf_op jit(solution)/shard_map/ppermute | solution.py:61
  281.8 2.2 copy.18
  284.0 1.5 bitcast_add_fusion.4
  285.5 2.9 collective-permute-start.1
  292.4 55.1 %all-gather.5.cloned.1.call-done = bf16[64,2,96,128]{3,2,1,0:T(8,128)(2,1)} async-done(((bf16[4,2,96,128]{3,2,1,0:T(8,128)(2,1)}), bf16[64,2,96,128]{3,2,1,0:T(8,128)(2,1)}) %all-gather.5.cloned.1.call-update) | async-done | bytes 3145744 | tf_op jit(solution)/shard_map/all_gather | solution.py:40
  347.4 2.5 multiply_convert_fusion
  352.6 2.0 broadcast_multiply_fusion
  354.8 1.7 collective-permute-start.9
  356.5 5.3 %collective-permute-done.9 = f32[4,8,2,96,128]{4,3,2,1,0:T(8,128)S(1)} collective-permute-done((f32[4,8,2,96,128]{4,3,2,1,0:T(8,128)S(1)}, f32[4,8,2,96,128]{4,3,2,1,0:T(8,128)S(1)}, u32[]{:S(2)}, u32[]{:S(2)}) %collective-permute-start.9) | collective-permute-done | bytes 3145760 | tf_op jit(solution)/shard_map/ppermute | solution.py:52
  363.5 1.6 copy-done.2
  366.6 2.2 copy.29
  368.9 1.4 constant_dynamic-slice_fusion.3
  370.4 2.2 copy.25
  372.5 3.5 collective-permute-start.10
  376.0 2.2 copy.30
  378.2 17.4 %collective-permute-done.13 = f32[8,2,96,64]{2,3,1,0:T(8,128)} collective-permute-done((f32[8,2,96,64]{2,3,1,0:T(8,128)}, f32[8,2,96,64]{2,3,1,0:T(8,128)}, u32[]{:S(2)}, u32[]{:S(2)}) %collective-permute-start.13) | collective-permute-done | bytes 393248 | tf_op jit(solution)/shard_map/ppermute | solution.py:62
  395.7 2.1 bitcast_add_fusion.7
  397.8 5.7 %collective-permute-start.14 = (f32[8,2,96,64]{2,3,1,0:T(8,128)}, f32[8,2,96,64]{2,3,1,0:T(8,128)}, u32[]{:S(2)}, u32[]{:S(2)}) collective-permute-start(f32[8,2,96,64]{2,3,1,0:T(8,128)} %bitcast_add_fusion.7), channel_id=1, source_target_pairs={{0,6},{2,0},{4,2},{6,4},{1,7},{3,1},{5,3},{7,5},{8,14},{10,8},{12,... | collective-permute-start | bytes 1179656 | tf_op jit(solution)/shard_map/ppermute | solution.py:62
  403.4 2.2 copy.26
  405.7 2.1 bitcast_add_fusion.9
  407.8 2.2 copy.31
  410.0 2.2 copy.27
  412.2 8.8 %collective-permute-done.14 = f32[8,2,96,64]{2,3,1,0:T(8,128)} collective-permute-done((f32[8,2,96,64]{2,3,1,0:T(8,128)}, f32[8,2,96,64]{2,3,1,0:T(8,128)}, u32[]{:S(2)}, u32[]{:S(2)}) %collective-permute-start.14) | collective-permute-done | bytes 393248 | tf_op jit(solution)/shard_map/ppermute | solution.py:62
  422.5 9.0 %collective-permute-done.11 = f32[8,2,96,64]{2,3,1,0:T(8,128)} collective-permute-done((f32[8,2,96,64]{2,3,1,0:T(8,128)}, f32[8,2,96,64]{2,3,1,0:T(8,128)}, u32[]{:S(2)}, u32[]{:S(2)}) %collective-permute-start.11) | collective-permute-done | bytes 393248 | tf_op jit(solution)/shard_map/ppermute | solution.py:61
  431.5 2.1 bitcast_add_fusion.8
  433.6 10.7 %collective-permute-done.15 = f32[8,2,96,64]{2,3,1,0:T(8,128)} collective-permute-done((f32[8,2,96,64]{2,3,1,0:T(8,128)S(1)}, f32[8,2,96,64]{2,3,1,0:T(8,128)}, u32[]{:S(2)}, u32[]{:S(2)}) %collective-permute-start.15) | collective-permute-done | bytes 393248 | tf_op jit(solution)/shard_map/ppermute | solution.py:62
  444.2 2.2 copy.32
  446.4 2.2 fusion.14
  448.6 5.4 %collective-permute-done.12 = f32[8,2,96,64]{2,3,1,0:T(8,128)} collective-permute-done((f32[8,2,96,64]{2,3,1,0:T(8,128)}, f32[8,2,96,64]{2,3,1,0:T(8,128)}, u32[]{:S(2)}, u32[]{:S(2)}) %collective-permute-start.12) | collective-permute-done | bytes 393248 | tf_op jit(solution)/shard_map/ppermute | solution.py:61
  454.0 2.2 copy.28
  (61 shorter events, 24.7 us)
Async XLA Ops:
  6.5 97.6 %reduce-scatter.3.cloned.1.call-start = ((), (), s32[]{:S(2)}) async-start(), calls=%async_computation.2 | async-start | bytes 3342336 | tf_op jit(solution)/shard_map/reduce_scatter | solution.py:35
  23.5 141.3 %all-gather.3.cloned.1.call-start = ((), (), s32[]{:S(2)}) async-start(), calls=%async_computation.3 | async-start | bytes 3342336 | tf_op jit(solution)/shard_map/all_gather | solution.py:40
  104.1 4.7 %collective-permute-start = (bf16[4,2,96,128]{3,2,1,0:T(8,128)(2,1)}, bf16[4,2,96,128]{3,2,1,0:T(8,128)(2,1)S(1)}, u32[]{:S(2)}, u32[]{:S(2)}) collective-permute-start(bf16[4,2,96,128]{3,2,1,0:T(8,128)(2,1)} %reduce-scatter.3.cloned.1.call-done), channel_id=1, source_target_pairs={{0,8},{8,0},{1,9},{9,1},{2,10},{10,2},{3,11},{11,3},{4,12},{12,4},... | collective-permute-start | bytes 589832 | tf_op jit(solution)/shard_map/ppermute | solution.py:36
  110.5 174.9 %reduce-scatter.5.cloned.1.call-start = ((), (), s32[]{:S(2)}) async-start(), calls=%async_computation.4 | async-start | bytes 3342336 | tf_op jit(solution)/shard_map/reduce_scatter | solution.py:35
  167.8 2.2 copy-start.3
  177.0 2.6 copy-start
  179.7 7.0 %collective-permute-start.2 = (f32[4,8,2,96,128]{4,3,2,1,0:T(8,128)S(1)}, f32[4,8,2,96,128]{4,3,2,1,0:T(8,128)}, u32[]{:S(2)}, u32[]{:S(2)}) collective-permute-start(f32[4,8,2,96,128]{4,3,2,1,0:T(8,128)S(1)} %dynamic-slice_bitcast_fusion.1), channel_id=1, source_target_pairs={{0,1},{1,0},{2,3},{3,2},{4,5},{5,4},{6,7},{7,6},{8,9},{9,8},{10,11... | collective-permute-start | bytes 9437192 | tf_op jit(solution)/shard_map/ppermute | solution.py:52
  181.3 166.1 %all-gather.5.cloned.1.call-start = ((), (), s32[]{:S(2)}) async-start(), calls=%async_computation.5 | async-start | bytes 3342336 | tf_op jit(solution)/shard_map/all_gather | solution.py:40
  191.3 1.6 copy-start.1
  196.6 26.9 %collective-permute-start.6 = (f32[8,2,96,64]{2,3,1,0:T(8,128)}, f32[8,2,96,64]{2,3,1,0:T(8,128)}, u32[]{:S(2)}, u32[]{:S(2)}) collective-permute-start(f32[8,2,96,64]{2,3,1,0:T(8,128)} %bitcast.113), channel_id=1, source_target_pairs={{0,6},{2,0},{4,2},{6,4},{1,7},{3,1},{5,3},{7,5},{8,14},{10,8},{12,... | collective-permute-start | bytes 1179656 | tf_op jit(solution)/shard_map/ppermute | solution.py:62
  200.4 30.8 %collective-permute-start.3 = (f32[8,2,96,64]{2,3,1,0:T(8,128)}, f32[8,2,96,64]{2,3,1,0:T(8,128)}, u32[]{:S(2)}, u32[]{:S(2)}) collective-permute-start(f32[8,2,96,64]{2,3,1,0:T(8,128)} %bitcast.115), channel_id=1, source_target_pairs={{0,2},{2,4},{4,6},{6,0},{1,3},{3,5},{5,7},{7,1},{8,10},{10,12},{12... | collective-permute-start | bytes 1179656 | tf_op jit(solution)/shard_map/ppermute | solution.py:61
  225.5 23.1 %collective-permute-start.7 = (f32[8,2,96,64]{2,3,1,0:T(8,128)}, f32[8,2,96,64]{2,3,1,0:T(8,128)}, u32[]{:S(2)}, u32[]{:S(2)}) collective-permute-start(f32[8,2,96,64]{2,3,1,0:T(8,128)} %bitcast_add_fusion.11), channel_id=1, source_target_pairs={{0,6},{2,0},{4,2},{6,4},{1,7},{3,1},{5,3},{7,5},{8,14},{10,8},{12,... | collective-permute-start | bytes 1179656 | tf_op jit(solution)/shard_map/ppermute | solution.py:62
  233.2 26.0 %collective-permute-start.4 = (f32[8,2,96,64]{2,3,1,0:T(8,128)}, f32[8,2,96,64]{2,3,1,0:T(8,128)}, u32[]{:S(2)}, u32[]{:S(2)}) collective-permute-start(f32[8,2,96,64]{2,3,1,0:T(8,128)} %bitcast_add_fusion.13), channel_id=1, source_target_pairs={{0,2},{2,4},{4,6},{6,0},{1,3},{3,5},{5,7},{7,1},{8,10},{10,12},{12... | collective-permute-start | bytes 1179656 | tf_op jit(solution)/shard_map/ppermute | solution.py:61
  250.7 21.2 %collective-permute-start.8 = (f32[8,2,96,64]{2,3,1,0:T(8,128)}, f32[8,2,96,64]{2,3,1,0:T(8,128)}, u32[]{:S(2)}, u32[]{:S(2)}) collective-permute-start(f32[8,2,96,64]{2,3,1,0:T(8,128)} %bitcast_add_fusion.10), channel_id=1, source_target_pairs={{0,6},{2,0},{4,2},{6,4},{1,7},{3,1},{5,3},{7,5},{8,14},{10,8},{12,... | collective-permute-start | bytes 1179656 | tf_op jit(solution)/shard_map/ppermute | solution.py:62
  261.3 20.4 %collective-permute-start.5 = (f32[8,2,96,64]{2,3,1,0:T(8,128)}, f32[8,2,96,64]{2,3,1,0:T(8,128)}, u32[]{:S(2)}, u32[]{:S(2)}) collective-permute-start(f32[8,2,96,64]{2,3,1,0:T(8,128)} %bitcast_add_fusion.12), channel_id=1, source_target_pairs={{0,2},{2,4},{4,6},{6,0},{1,3},{3,5},{5,7},{7,1},{8,10},{10,12},{12... | collective-permute-start | bytes 1179656 | tf_op jit(solution)/shard_map/ppermute | solution.py:61
  285.5 6.1 %copy-start.6 = (bf16[4,2,96,128]{3,2,1,0:T(8,128)(2,1)S(1)}, bf16[4,2,96,128]{3,2,1,0:T(8,128)(2,1)}, u32[]{:S(2)}) copy-start(bf16[4,2,96,128]{3,2,1,0:T(8,128)(2,1)} %reduce-scatter.5.cloned.1.call-done) | copy-start | bytes 589828
  285.5 6.1 %collective-permute-start.1 = (bf16[4,2,96,128]{3,2,1,0:T(8,128)(2,1)}, bf16[4,2,96,128]{3,2,1,0:T(8,128)(2,1)S(1)}, u32[]{:S(2)}, u32[]{:S(2)}) collective-permute-start(bf16[4,2,96,128]{3,2,1,0:T(8,128)(2,1)} %reduce-scatter.5.cloned.1.call-done), channel_id=1, source_target_pairs={{0,8},{8,0},{1,9},{9,1},{2,10},{10,2},{3,11},{11,3},{4,12},{12,4},... | collective-permute-start | bytes 589832 | tf_op jit(solution)/shard_map/ppermute | solution.py:36
  350.4 2.2 copy-start.4
  354.8 7.0 %collective-permute-start.9 = (f32[4,8,2,96,128]{4,3,2,1,0:T(8,128)S(1)}, f32[4,8,2,96,128]{4,3,2,1,0:T(8,128)S(1)}, u32[]{:S(2)}, u32[]{:S(2)}) collective-permute-start(f32[4,8,2,96,128]{4,3,2,1,0:T(8,128)S(1)} %dynamic-slice_bitcast_fusion), channel_id=1, source_target_pairs={{0,1},{1,0},{2,3},{3,2},{4,5},{5,4},{6,7},{7,6},{8,9},{9,8},{10,11... | collective-permute-start | bytes 9437192 | tf_op jit(solution)/shard_map/ppermute | solution.py:52
  363.5 1.6 copy-start.2
  368.8 26.9 %collective-permute-start.13 = (f32[8,2,96,64]{2,3,1,0:T(8,128)}, f32[8,2,96,64]{2,3,1,0:T(8,128)}, u32[]{:S(2)}, u32[]{:S(2)}) collective-permute-start(f32[8,2,96,64]{2,3,1,0:T(8,128)} %bitcast.114), channel_id=1, source_target_pairs={{0,6},{2,0},{4,2},{6,4},{1,7},{3,1},{5,3},{7,5},{8,14},{10,8},{12,... | collective-permute-start | bytes 1179656 | tf_op jit(solution)/shard_map/ppermute | solution.py:62
  372.5 33.1 %collective-permute-start.10 = (f32[8,2,96,64]{2,3,1,0:T(8,128)}, f32[8,2,96,64]{2,3,1,0:T(8,128)}, u32[]{:S(2)}, u32[]{:S(2)}) collective-permute-start(f32[8,2,96,64]{2,3,1,0:T(8,128)} %bitcast.116), channel_id=1, source_target_pairs={{0,2},{2,4},{4,6},{6,0},{1,3},{3,5},{5,7},{7,1},{8,10},{10,12},{12... | collective-permute-start | bytes 1179656 | tf_op jit(solution)/shard_map/ppermute | solution.py:61
  397.8 23.1 %collective-permute-start.14 = (f32[8,2,96,64]{2,3,1,0:T(8,128)}, f32[8,2,96,64]{2,3,1,0:T(8,128)}, u32[]{:S(2)}, u32[]{:S(2)}) collective-permute-start(f32[8,2,96,64]{2,3,1,0:T(8,128)} %bitcast_add_fusion.7), channel_id=1, source_target_pairs={{0,6},{2,0},{4,2},{6,4},{1,7},{3,1},{5,3},{7,5},{8,14},{10,8},{12,... | collective-permute-start | bytes 1179656 | tf_op jit(solution)/shard_map/ppermute | solution.py:62
  407.8 23.7 %collective-permute-start.11 = (f32[8,2,96,64]{2,3,1,0:T(8,128)}, f32[8,2,96,64]{2,3,1,0:T(8,128)}, u32[]{:S(2)}, u32[]{:S(2)}) collective-permute-start(f32[8,2,96,64]{2,3,1,0:T(8,128)} %bitcast_add_fusion.9), channel_id=1, source_target_pairs={{0,2},{2,4},{4,6},{6,0},{1,3},{3,5},{5,7},{7,1},{8,10},{10,12},{12... | collective-permute-start | bytes 1179656 | tf_op jit(solution)/shard_map/ppermute | solution.py:61
  422.2 22.1 %collective-permute-start.15 = (f32[8,2,96,64]{2,3,1,0:T(8,128)S(1)}, f32[8,2,96,64]{2,3,1,0:T(8,128)}, u32[]{:S(2)}, u32[]{:S(2)}) collective-permute-start(f32[8,2,96,64]{2,3,1,0:T(8,128)S(1)} %bitcast_add_fusion.6), channel_id=1, source_target_pairs={{0,6},{2,0},{4,2},{6,4},{1,7},{3,1},{5,3},{7,5},{8,14},{10,8},{12,... | collective-permute-start | bytes 1179656 | tf_op jit(solution)/shard_map/ppermute | solution.py:62
  433.6 23.9 %copy-start.5 = (bf16[8,2,96,128]{3,2,1,0:T(8,128)(2,1)S(1)}, bf16[8,2,96,128]{3,2,1,0:T(8,128)(2,1)}, u32[]{:S(2)}) copy-start(bf16[8,2,96,128]{3,2,1,0:T(8,128)(2,1)} %pad_maximum_fusion) | copy-start | bytes 1179652
  433.6 20.4 %collective-permute-start.12 = (f32[8,2,96,64]{2,3,1,0:T(8,128)}, f32[8,2,96,64]{2,3,1,0:T(8,128)}, u32[]{:S(2)}, u32[]{:S(2)}) collective-permute-start(f32[8,2,96,64]{2,3,1,0:T(8,128)} %bitcast_add_fusion.8), channel_id=1, source_target_pairs={{0,2},{2,4},{4,6},{6,0},{1,3},{3,5},{5,7},{7,1},{8,10},{10,12},{12... | collective-permute-start | bytes 1179656 | tf_op jit(solution)/shard_map/ppermute | solution.py:61
Sparse Core Ops, SparseCore 0:
  23.6 80.4 reduce-scatter.2
  110.6 54.1 all-gather.2
  181.4 78.0 reduce-scatter.4
  292.5 54.8 all-gather.4

commit v4 on v2

v4 whole, which is shorter than its diff:
```python
import jax
import jax.numpy as jnp
import numpy as np
from jax import lax
from jax.sharding import Mesh, PartitionSpec as P

SB = 32
ROUNDS = 6
WINDOWS = 8
PLANE = ("y", "x")
SHOT = ("zh", "c")


def taper_weights(taper_windows):
    return 0.5 - 0.5 * jnp.cos(jnp.pi * (taper_windows.astype(jnp.float32) + 1.0) / (WINDOWS + 1.0))


def pick_sources(receivers, source_block):
    node_dev = receivers.shape[3]
    per_device = node_dev // SB
    me = (lax.axis_index("y") * lax.axis_size("x") + lax.axis_index("x")) * lax.axis_size("zl") + lax.axis_index("zl")
    owner = source_block // per_device
    first = source_block % per_device * SB
    column = jnp.arange(ROUNDS * SB, dtype=jnp.int32)
    wanted = first[column // SB] + column % SB
    keep = owner[column // SB] == me
    node = jnp.arange(node_dev, dtype=jnp.int32)
    select = ((node[:, None] == wanted[None, :]) & keep[None, :]).astype(receivers.dtype)
    picked = jnp.einsum("fckn,nq->cfqk", receivers, select, preferred_element_type=jnp.float32)
    return picked.astype(receivers.dtype)


def broadcast(picked):
    planes = lax.axis_size("y") * lax.axis_size("x")
    shape = picked.shape
    pieces = picked.reshape(planes, *shape[2:])
    got = lax.all_to_all(pieces, PLANE, 0, 0, tiled=True)
    mine = jnp.sum(got, axis=0, keepdims=True)
    mine = mine + lax.ppermute(mine, "zl", perm=[(0, 1), (1, 0)])
    return lax.all_gather(mine, PLANE, axis=0, tiled=True).reshape(shape)


def body(spectra, source_block, taper_window):
    receivers = lax.all_to_all(spectra, SHOT, 0, 2, tiled=True)
    freqs, _, shots, node_dev = receivers.shape
    scale = 1.0 / jnp.sqrt(jnp.float32(shots))
    weight_rows = jnp.repeat(taper_weights(taper_window), SB, axis=0)

    source = broadcast(pick_sources(receivers, source_block))
    tapered = (source.astype(jnp.float32) * weight_rows[None, None]).astype(jnp.bfloat16)
    real_part = tapered[0]
    imag_part = tapered[1]
    real_row = jnp.concatenate((real_part, imag_part), axis=2)
    imag_row = jnp.concatenate((-imag_part, real_part), axis=2)
    operator = jnp.stack((real_row, imag_row), axis=1)
    stacked = receivers.reshape(freqs, 2 * shots, node_dev)
    summed = jnp.einsum("foqK,fKn->foqn", operator, stacked, preferred_element_type=jnp.float32)
    out = (summed * scale).astype(jnp.bfloat16).reshape(freqs, 2, ROUNDS, SB, node_dev)
    return jnp.transpose(out, (2, 0, 1, 3, 4))


def solution(mesh):
    devices = np.asarray(mesh.devices).reshape(4, 4, 2, 4, 2)
    fine = Mesh(devices, ("y", "x", "zl", "zh", "c"))
    in_specs = (P(None, None, SHOT, ("y", "x", "zl")), P(), P())
    out_specs = P(None, SHOT, None, None, ("y", "x", "zl"))
    return jax.shard_map(body, mesh=fine, in_specs=in_specs, out_specs=out_specs, check_vma=False)
```

time: 353 us -> 295 us (0.84)
  waiting for transfers between devices: 297 us -> 160 us
  blocking collectives: 0 us -> 77 us
  matrix products: 15.5 us -> 5.91 us
  starting transfers between devices: 1.36 us -> 8.66 us
  local copies, waits for them, and re-layouts: 2.14 us -> 8.96 us
    reduce_scatter x2 -> x0, waiting for transfers between devices: 221 us -> none  [the longest x1 134 us: body(): lax.psum_scatter(summed * scale, ('zh', 'c'), scatter_dimension=0, tiled=...]
    all_to_all x0 -> x1, waiting for transfers between devices: none -> 85.8 us  [body(): receivers = lax.all_to_all(spectra, SHOT, 0, 2, tiled=True)]
    all_to_all x0 -> x1, blocking collectives: none -> 77 us  [broadcast(): got = lax.all_to_all(pieces, PLANE, 0, 0, tiled=True)]
    dot_general x2, matrix products: 15.5 us -> 5.91 us  [the longest x1 4.08 us: body(): jnp.einsum('foqK,fKn->foqn', operator, stacked, preferred_element_type=jn...]
    all_to_all x0 -> x1, starting transfers between devices: none -> 8.56 us  [body(): receivers = lax.all_to_all(spectra, SHOT, 0, 2, tiled=True)]
    reduce_sum x0 -> x1, other arithmetic: none -> 4.3 us  [broadcast(): mine = jnp.sum(got, axis=0, keepdims=True)]
  transfers between devices with their start and end apart: 4 -> 3, of which waited for: 4 -> 3; matrix products, arithmetic and copies ran while one was open for 0% -> 3% of each run, Pallas kernels for 0% -> 0%
where the time goes in v4:
time: 295 us; the launch traced here: 293 us
  waiting for transfers between devices  160 us (54%)
  blocking collectives  77 us (26%)
  other arithmetic  19.1 us (6%)
  between operations  13.5 us (5%)
  local copies, waits for them, and re-layouts  8.96 us (3%)
  starting transfers between devices  8.66 us (3%)
  matrix products  5.91 us (2%)
    all_to_all x1, waiting for transfers between devices, body(): receivers = lax.all_to_all(spectra, SHOT, 0, 2, tiled=True)  85.8 us
    all_to_all x1, blocking collectives, broadcast(): got = lax.all_to_all(pieces, PLANE, 0, 0, tiled=True)  77 us
    all_gather x1, waiting for transfers between devices, broadcast(): return lax.all_gather(mine, PLANE, axis=0, tiled=True).reshape(shape)  65.5 us
    ppermute x1, waiting for transfers between devices, broadcast(): mine = mine + lax.ppermute(mine, 'zl', perm=[(0, 1), (1, 0)])  8.84 us
    all_to_all x1, starting transfers between devices, body(): receivers = lax.all_to_all(spectra, SHOT, 0, 2, tiled=True)  8.56 us
  transfers between devices with their start and end apart: 3, of which 3 were waited for; matrix products, arithmetic and copies ran while one was open for 3% of the time, Pallas kernels for 0%

profile of v4, /device:TPU:73, one launch (start us, length us, event | category | flops | bytes accessed | tf_op | source)
XLA Modules:
  0.0 293.3 jit_solution(13768796242992410530)
XLA Ops:
  6.5 0.0 copy-start.3
  6.5 8.6 %all-to-all-start = ((bf16[64,2,128,128]{3,2,1,0:T(8,128)(2,1)}), bf16[64,2,128,128]{3,2,1,0:T(8,128)(2,1)}, u32[]{:S(2)}, u32[]{:S(2)}) async-start(bf16[64,2,128,128]{3,2,1,0:T(8,128)(2,1)} %param.3), calls=%async_computation | async-start | bytes 8388608 | tf_op jit(solution)/shard_map/all_to_all | solution.py:44
  15.1 0.0 all-gather.2.cloned.1.call-start
  15.1 0.0 copy-done.3
  15.1 0.7 fusion.16
  15.8 3.8 %compare_reduce_fusion = pred[192]{0:T(512)(128)(4,1)S(1)} fusion(s32[]{:T(128)S(6)} %add.65, s32[]{:T(128)} %bitcast.7, s32[]{:T(128)} %bitcast.8, s32[]{:T(128)} %bitcast.9, s32[]{:T(128)} %bitcast.10, s32[]{:T(128)} %bitcast.12, s32[]{:T(128)} %bitcast.11), kind=kLoop, calls=%fused_computation.20 | loop fusion | flops 4224 | bytes 220 | tf_op jit(solution)/shard_map/eq | solution.py:26
  19.6 3.7 %compare_select_fusion.1 = s32[192,1]{0,1:T(1,128)S(1)} fusion(s32[]{:T(128)} %bitcast, s32[]{:T(128)} %bitcast.1, s32[]{:T(128)} %bitcast.2, s32[]{:T(128)} %bitcast.3, s32[]{:T(128)} %bitcast.5, s32[]{:T(128)} %bitcast.4), kind=kLoop, calls=%fused_computation.22 | loop fusion | flops 4032 | bytes 792 | tf_op jit(solution)/shard_map/gather | solution.py:25
  23.4 85.8 %all-to-all-done = bf16[64,2,128,128]{3,2,1,0:T(8,128)(2,1)} async-done(((bf16[64,2,128,128]{3,2,1,0:T(8,128)(2,1)}), bf16[64,2,128,128]{3,2,1,0:T(8,128)(2,1)}, u32[]{:S(2)}, u32[]{:S(2)}) %all-to-all-start) | async-done | bytes 4194336 | tf_op jit(solution)/shard_map/all_to_all | solution.py:44
  109.2 2.7 copy.11
  111.9 0.0 copy-start
  111.9 2.0 copy-done
  113.9 1.8 convert_bitcast_fusion
  115.8 1.0 copy.12
  116.8 77.0 %all_to_all.23 = bf16[16,192,1024]{2,1,0:T(8,128)(2,1)} all-to-all(bf16[16,192,1024]{2,1,0:T(8,128)(2,1)S(1)} %bitcast.54), channel_id=1, replica_groups=mesh['y'=4,'x'=4,'zl'=2,'zh'=4,'c'=2] {'y','x'}, dimensions={0} | all-to-all | bytes 12582912 | tf_op jit(solution)/shard_map/all_to_all | solution.py:37
  193.8 0.0 copy-start.2
  193.8 4.3 %reduce_sum.12 = bf16[192,1024]{1,0:T(8,128)(2,1)S(1)} reduce(bf16[16,192,1024]{2,1,0:T(8,128)(2,1)} %all_to_all.23, bf16[]{:T(256)} %constant.87.clone.1), dimensions={0}, to_apply=%region_0.1 | reduce | flops 2949120 | bytes 6684674 | tf_op jit(solution)/shard_map/reduce_sum | solution.py:38
  198.1 0.1 collective-permute-start
  198.2 8.8 %collective-permute-done = bf16[1,192,1024]{2,1,0:T(8,128)(2,1)S(1)} collective-permute-done((bf16[1,192,1024]{2,1,0:T(8,128)(2,1)S(1)}, bf16[1,192,1024]{2,1,0:T(8,128)(2,1)S(1)}, u32[]{:S(2)}, u32[]{:S(2)}) %collective-permute-start) | collective-permute-done | bytes 393248 | tf_op jit(solution)/shard_map/ppermute | solution.py:39
  207.0 0.8 bitcast_add_fusion
  207.8 0.0 all-gather.2.cloned.1.call-update
  207.8 0.0 copy-done.2
  207.8 0.1 multiply_subtract_fusion
  208.0 65.5 %all-gather.2.cloned.1.call-done = bf16[16,192,1024]{2,1,0:T(8,128)(2,1)} async-done(((bf16[1,192,1024]{2,1,0:T(8,128)(2,1)}), bf16[16,192,1024]{2,1,0:T(8,128)(2,1)}) %all-gather.2.cloned.1.call-update) | async-done | bytes 6291472 | tf_op jit(solution)/shard_map/all_gather | solution.py:40
  273.4 0.1 broadcast_in_dim.2
  273.5 4.7 %fusion.4 = bf16[2,8,192,1024]{3,2,1,0:T(8,128)(2,1)S(1)} fusion(bf16[2,8,192,1024]{3,2,1,0:T(8,128)(2,1)} %bitcast.57, f32[192,1024]{1,0:T(8,128)S(1)} %bitcast.58), kind=kLoop, calls=%fused_computation.5 | loop fusion | flops 9437184 | bytes 13369344 | tf_op jit(solution)/shard_map/convert_element_type | solution.py:50
  278.2 0.2 fusion.15
  278.5 0.8 slice_bitcast_fusion
  279.2 0.0 copy-start.1
  279.2 1.4 maximum_bitcast_fusion
  280.6 0.8 copy-done.1
  281.4 4.1 %multiply_convert_fusion = bf16[8,2,192,128]{3,2,1,0:T(8,128)(2,1)S(1)} fusion(bf16[8,2048,128,1]{2,1,3,0:T(8,128)(2,1)S(1)} %bitcast.56, bf16[8,1,192,2048]{3,2,1,0:T(8,128)(2,1)S(1)} %get-tuple-element.8, bf16[8,1,192,2048]{3,2,1,0:T(8,128)(2,1)S(1)} %get-tuple-element.7), kind=kOutput, calls=%fused_computation.11 | convolution fusion | flops 1617690624 | bytes 17563648 | tf_op jit(solution)/shard_map/foqK,fKn->foqn/dot_general | solution.py:57
  285.5 1.0 copy.18
  (2 shorter events, 0.0 us)
Async XLA Ops:
  6.5 8.6 %copy-start.3 = (s32[6]{0:T(128)S(1)}, s32[6]{0:T(128)}, u32[]{:S(2)}) copy-start(s32[6]{0:T(128)} %param.4) | copy-start | bytes 76
  6.5 102.7 %all-to-all-start = ((bf16[64,2,128,128]{3,2,1,0:T(8,128)(2,1)}), bf16[64,2,128,128]{3,2,1,0:T(8,128)(2,1)}, u32[]{:S(2)}, u32[]{:S(2)}) async-start(bf16[64,2,128,128]{3,2,1,0:T(8,128)(2,1)} %param.3), calls=%async_computation | async-start | bytes 8388608 | tf_op jit(solution)/shard_map/all_to_all | solution.py:44
  15.1 258.3 %all-gather.2.cloned.1.call-start = ((), (), s32[]{:S(2)}) async-start(), calls=%async_computation.2 | async-start | bytes 6684672 | tf_op jit(solution)/shard_map/all_gather | solution.py:40
  111.9 2.0 copy-start
  193.8 14.1 %copy-start.2 = (s32[6,1024]{1,0:T(8,128)S(1)}, s32[6,1024]{1,0:T(8,128)}, u32[]{:S(2)}) copy-start(s32[6,1024]{1,0:T(8,128)} %param.5) | copy-start | bytes 73732
  198.1 8.9 %collective-permute-start = (bf16[1,192,1024]{2,1,0:T(8,128)(2,1)S(1)}, bf16[1,192,1024]{2,1,0:T(8,128)(2,1)S(1)}, u32[]{:S(2)}, u32[]{:S(2)}) collective-permute-start(bf16[1,192,1024]{2,1,0:T(8,128)(2,1)S(1)} %bitcast.59), channel_id=1, source_target_pairs={{0,8},{8,0},{1,9},{9,1},{2,10},{10,2},{3,11},{11,3},{4,12},{12,4},... | collective-permute-start | bytes 1179656 | tf_op jit(solution)/shard_map/ppermute | solution.py:39
  279.2 2.2 copy-start.1
Sparse Core Ops, SparseCore 0:
  207.9 65.4 all-gather.1

commit v5 on v4

v5 whole, which is shorter than its diff:
```python
import jax
import jax.numpy as jnp
import numpy as np
from jax import lax
from jax.sharding import Mesh, PartitionSpec as P

SB = 32
ROUNDS = 6
WINDOWS = 8
HALVES = 2
PLANE = ("y", "x")
SHOT = ("zh", "c")


def taper_weights(taper_windows):
    return 0.5 - 0.5 * jnp.cos(jnp.pi * (taper_windows.astype(jnp.float32) + 1.0) / (WINDOWS + 1.0))


def selection(node_dev, source_block, dtype):
    per_device = node_dev // SB
    me = (lax.axis_index("y") * lax.axis_size("x") + lax.axis_index("x")) * lax.axis_size("zl") + lax.axis_index("zl")
    owner = source_block // per_device
    first = source_block % per_device * SB
    column = jnp.arange(ROUNDS * SB, dtype=jnp.int32)
    wanted = first[column // SB] + column % SB
    keep = owner[column // SB] == me
    node = jnp.arange(node_dev, dtype=jnp.int32)
    return ((node[:, None] == wanted[None, :]) & keep[None, :]).astype(dtype)


def scatter_piece(receivers, select):
    planes = lax.axis_size("y") * lax.axis_size("x")
    picked = jnp.einsum("fckn,nq->cfqk", receivers, select, preferred_element_type=jnp.float32)
    picked = picked.astype(receivers.dtype)
    pieces = picked.reshape(planes, -1, picked.shape[-1])
    got = lax.all_to_all(pieces, PLANE, 0, 0, tiled=True)
    mine = jnp.sum(got, axis=0, keepdims=True)
    return mine + lax.ppermute(mine, "zl", perm=[(0, 1), (1, 0)])


def body(spectra, source_block, taper_window):
    freqs, comps, shot_dev, node_dev = spectra.shape
    groups = lax.axis_size("zh") * lax.axis_size("c")
    select = selection(node_dev, source_block, spectra.dtype)
    split = spectra.reshape(groups, HALVES, freqs // (groups * HALVES), comps, shot_dev, node_dev)
    receivers = []
    sources = []
    previous = None
    for half in range(HALVES):
        part = split[:, half].reshape(-1, comps, shot_dev, node_dev)
        if previous is not None:
            part, previous = lax.optimization_barrier((part, previous))
            sources.append(lax.all_gather(previous, PLANE, axis=0, tiled=True))
        got = lax.all_to_all(part, SHOT, 0, 2, tiled=True)
        receivers.append(got)
        previous = scatter_piece(got, select)
    sources.append(lax.all_gather(previous, PLANE, axis=0, tiled=True))
    receivers = jnp.concatenate(receivers, axis=0)
    local_f, _, shots, _ = receivers.shape
    fh = local_f // HALVES
    source = jnp.stack([s.reshape(comps, fh, ROUNDS * SB, shots) for s in sources], axis=1)
    source = source.reshape(comps, local_f, ROUNDS * SB, shots)

    scale = 1.0 / jnp.sqrt(jnp.float32(shots))
    weight_rows = jnp.repeat(taper_weights(taper_window), SB, axis=0)
    tapered = (source.astype(jnp.float32) * weight_rows[None, None]).astype(jnp.bfloat16)
    real_part = tapered[0]
    imag_part = tapered[1]
    real_row = jnp.concatenate((real_part, imag_part), axis=2)
    imag_row = jnp.concatenate((-imag_part, real_part), axis=2)
    operator = jnp.stack((real_row, imag_row), axis=1)
    stacked = receivers.reshape(local_f, 2 * shots, node_dev)
    summed = jnp.einsum("foqK,fKn->foqn", operator, stacked, preferred_element_type=jnp.float32)
    out = (summed * scale).astype(jnp.bfloat16).reshape(local_f, 2, ROUNDS, SB, node_dev)
    return jnp.transpose(out, (2, 0, 1, 3, 4))


def solution(mesh):
    devices = np.asarray(mesh.devices).reshape(4, 4, 2, 4, 2)
    fine = Mesh(devices, ("y", "x", "zl", "zh", "c"))
    in_specs = (P(None, None, SHOT, ("y", "x", "zl")), P(), P())
    out_specs = P(None, SHOT, None, None, ("y", "x", "zl"))
    return jax.shard_map(body, mesh=fine, in_specs=in_specs, out_specs=out_specs, check_vma=False)
```

time: 295 us -> 307 us (1.041)
  waiting for transfers between devices: 160 us -> 143 us
  starting transfers between devices: 8.66 us -> 23.8 us
  blocking collectives: 77 us -> 84.3 us
    all_gather x1 -> x2, waiting for transfers between devices: 65.5 us -> 53 us  [body(): sources.append(lax.all_gather(previous, PLANE, axis=0, tiled=True))]
    all_to_all x1 -> x2, starting transfers between devices: 8.56 us -> 16.3 us  [body(): got = lax.all_to_all(part, SHOT, 0, 2, tiled=True)]
    ppermute x1 -> x2, starting transfers between devices: 0.09 us -> 7.5 us  [scatter_piece(): return mine + lax.ppermute(mine, 'zl', perm=[(0, 1), (1, 0)])]
    all_to_all x1 -> x2, blocking collectives: 77 us -> 84.3 us  [scatter_piece(): got = lax.all_to_all(pieces, PLANE, 0, 0, tiled=True)]
    all_to_all x1 -> x2, waiting for transfers between devices: 85.8 us -> 81 us  [body(): got = lax.all_to_all(part, SHOT, 0, 2, tiled=True)]
    slice x0 -> x1, local copies, waits for them, and re-layouts: none -> 4.83 us  [body(): part = split[:, half].reshape(-1, comps, shot_dev, node_dev)]
    another operation x0 -> x1, other arithmetic: none -> 3.42 us  [body(): jnp.stack([s.reshape(comps, fh, ROUNDS * SB, shots) for s in sources], ax...]
    ppermute x1 -> x2, waiting for transfers between devices: 8.84 us -> 8.11 us  [scatter_piece(): return mine + lax.ppermute(mine, 'zl', perm=[(0, 1), (1, 0)])]
  transfers between devices with their start and end apart: 3 -> 6, of which waited for: 3 -> 5; matrix products, arithmetic and copies ran while one was open for 3% -> 4% of each run, Pallas kernels for 0% -> 0%
where the time goes in v5:
time: 307 us; the launch traced here: 303 us
  waiting for transfers between devices  143 us (47%)
  blocking collectives  84.3 us (27%)
  starting transfers between devices  23.8 us (8%)
  other arithmetic  19.6 us (6%)
  between operations  13.6 us (4%)
  local copies, waits for them, and re-layouts  11.6 us (4%)
  matrix products  7.61 us (2%)
    all_to_all x2, blocking collectives, scatter_piece(): got = lax.all_to_all(pieces, PLANE, 0, 0, tiled=True)  84.3 us
    all_to_all x2, waiting for transfers between devices, body(): got = lax.all_to_all(part, SHOT, 0, 2, tiled=True)  81 us
    all_gather x2, waiting for transfers between devices, body(): sources.append(lax.all_gather(previous, PLANE, axis=0, tiled=True))  53 us
    all_to_all x2, starting transfers between devices, body(): got = lax.all_to_all(part, SHOT, 0, 2, tiled=True)  16.3 us
    ppermute x2, waiting for transfers between devices, scatter_piece(): return mine + lax.ppermute(mine, 'zl', perm=[(0, 1), (1, 0)])  8.11 us
    ppermute x2, starting transfers between devices, scatter_piece(): return mine + lax.ppermute(mine, 'zl', perm=[(0, 1), (1, 0)])  7.5 us
  transfers between devices with their start and end apart: 6, of which 5 were waited for; matrix products, arithmetic and copies ran while one was open for 4% of the time, Pallas kernels for 0%

profile of v5, /device:TPU:73, one launch (start us, length us, event | category | flops | bytes accessed | tf_op | source)
XLA Modules:
  0.0 303.4 jit_solution(16434045181645490174)
XLA Ops:
  6.5 4.8 %fusion.21 = (bf16[8,1,4,2,128,128]{5,4,3,2,1,0:T(8,128)(2,1)}, bf16[8,1,4,2,128,128]{5,4,3,2,1,0:T(8,128)(2,1)}) fusion(bf16[8,2,4,2,128,128]{5,4,3,2,1,0:T(8,128)(2,1)} %bitcast.91), kind=kLoop, calls=%fused_computation.54 | loop fusion | bytes 8388608 | tf_op jit(solution)/shard_map/slice | solution.py:50
  11.4 0.0 copy-start.5
  11.4 8.6 %all-to-all-start = ((bf16[32,2,128,128]{3,2,1,0:T(8,128)(2,1)}), bf16[32,2,128,128]{3,2,1,0:T(8,128)(2,1)S(1)}, u32[]{:S(2)}, u32[]{:S(2)}) async-start(bf16[32,2,128,128]{3,2,1,0:T(8,128)(2,1)} %bitcast.90), calls=%async_computation | async-start | bytes 4194304 | tf_op jit(solution)/shard_map/all_to_all | solution.py:54
  19.9 0.0 copy-done.5
  19.9 0.7 fusion.22
  20.7 3.7 %compare_reduce_fusion = pred[192]{0:T(512)(128)(4,1)S(1)} fusion(s32[]{:T(128)S(6)} %add.68, s32[]{:T(128)} %bitcast.9, s32[]{:T(128)} %bitcast.10, s32[]{:T(128)} %bitcast.11, s32[]{:T(128)} %bitcast.12, s32[]{:T(128)} %bitcast.14, s32[]{:T(128)} %bitcast.13), kind=kLoop, calls=%fused_computation.27 | loop fusion | flops 4224 | bytes 220 | tf_op jit(solution)/shard_map/eq | solution.py:26
  24.4 3.8 %compare_select_fusion.1 = s32[192,1]{0,1:T(1,128)S(1)} fusion(s32[]{:T(128)} %bitcast.2, s32[]{:T(128)} %bitcast.3, s32[]{:T(128)} %bitcast.4, s32[]{:T(128)} %bitcast.5, s32[]{:T(128)} %bitcast.7, s32[]{:T(128)} %bitcast.6), kind=kLoop, calls=%fused_computation.29 | loop fusion | flops 4032 | bytes 792 | tf_op jit(solution)/shard_map/gather | solution.py:25
  28.2 40.8 %all-to-all-done = bf16[32,2,128,128]{3,2,1,0:T(8,128)(2,1)S(1)} async-done(((bf16[32,2,128,128]{3,2,1,0:T(8,128)(2,1)}), bf16[32,2,128,128]{3,2,1,0:T(8,128)(2,1)S(1)}, u32[]{:S(2)}, u32[]{:S(2)}) %all-to-all-start) | async-done | bytes 2097184 | tf_op jit(solution)/shard_map/all_to_all | solution.py:54
  69.0 0.2 copy.18
  69.2 0.0 copy-start
  69.2 1.3 copy-done
  70.6 1.0 convert_bitcast_fusion.1
  71.6 0.3 copy.19
  71.9 43.2 %all_to_all.46 = bf16[16,96,1024]{2,1,0:T(8,128)(2,1)S(1)} all-to-all(bf16[16,96,1024]{2,1,0:T(8,128)(2,1)S(1)} %bitcast.81), channel_id=1, replica_groups=mesh['y'=4,'x'=4,'zl'=2,'zh'=4,'c'=2] {'y','x'}, dimensions={0} | all-to-all | bytes 6291456 | tf_op jit(solution)/shard_map/all_to_all | solution.py:36
  115.1 0.6 reduce_sum.24
  115.8 0.1 collective-permute-start
  115.9 4.5 %collective-permute-done = bf16[1,96,1024]{2,1,0:T(8,128)(2,1)S(1)} collective-permute-done((bf16[1,96,1024]{2,1,0:T(8,128)(2,1)S(1)}, bf16[1,96,1024]{2,1,0:T(8,128)(2,1)S(1)}, u32[]{:S(2)}, u32[]{:S(2)}) %collective-permute-start) | collective-permute-done | bytes 196640 | tf_op jit(solution)/shard_map/ppermute | solution.py:38
  120.4 0.7 bitcast_add_fusion.1
  121.1 7.7 %all-to-all-start.2 = ((bf16[32,2,128,128]{3,2,1,0:T(8,128)(2,1)}), bf16[32,2,128,128]{3,2,1,0:T(8,128)(2,1)S(1)}, u32[]{:S(2)}, u32[]{:S(2)}) async-start(bf16[32,2,128,128]{3,2,1,0:T(8,128)(2,1)} %bitcast.89), calls=%async_computation.2 | async-start | bytes 4194304 | tf_op jit(solution)/shard_map/all_to_all | solution.py:54
  128.8 0.0 all-gather.3.cloned.1.call-start
  128.8 0.7 all-gather.3.cloned.1.call-update
  129.5 0.0 all-gather.5.cloned.1.call-start
  129.6 40.2 %all-to-all-done.2 = bf16[32,2,128,128]{3,2,1,0:T(8,128)(2,1)S(1)} async-done(((bf16[32,2,128,128]{3,2,1,0:T(8,128)(2,1)}), bf16[32,2,128,128]{3,2,1,0:T(8,128)(2,1)S(1)}, u32[]{:S(2)}, u32[]{:S(2)}) %all-to-all-start.2) | async-done | bytes 2097184 | tf_op jit(solution)/shard_map/all_to_all | solution.py:54
  169.8 0.2 copy.20
  170.0 0.0 copy-start.2
  170.0 1.4 copy-done.2
  171.4 1.0 convert_bitcast_fusion
  172.4 0.3 copy.21
  172.7 41.1 %all_to_all.47 = bf16[16,96,1024]{2,1,0:T(8,128)(2,1)S(1)} all-to-all(bf16[16,96,1024]{2,1,0:T(8,128)(2,1)S(1)} %bitcast.82), channel_id=1, replica_groups=mesh['y'=4,'x'=4,'zl'=2,'zh'=4,'c'=2] {'y','x'}, dimensions={0} | all-to-all | bytes 6291456 | tf_op jit(solution)/shard_map/all_to_all | solution.py:36
  213.8 0.0 copy-start.4
  213.8 0.6 reduce_sum.25
  214.5 7.4 %collective-permute-start.1 = (bf16[1,96,1024]{2,1,0:T(8,128)(2,1)S(1)}, bf16[1,96,1024]{2,1,0:T(8,128)(2,1)S(1)}, u32[]{:S(2)}, u32[]{:S(2)}) collective-permute-start(bf16[1,96,1024]{2,1,0:T(8,128)(2,1)S(1)} %bitcast.96), channel_id=1, source_target_pairs={{0,8},{8,0},{1,9},{9,1},{2,10},{10,2},{3,11},{11,3},{4,12},{12,4},... | collective-permute-start | bytes 589832 | tf_op jit(solution)/shard_map/ppermute | solution.py:38
  221.9 3.6 %collective-permute-done.1 = bf16[1,96,1024]{2,1,0:T(8,128)(2,1)S(1)} collective-permute-done((bf16[1,96,1024]{2,1,0:T(8,128)(2,1)S(1)}, bf16[1,96,1024]{2,1,0:T(8,128)(2,1)S(1)}, u32[]{:S(2)}, u32[]{:S(2)}) %collective-permute-start.1) | collective-permute-done | bytes 196640 | tf_op jit(solution)/shard_map/ppermute | solution.py:38
  225.5 0.7 bitcast_add_fusion
  226.2 0.0 all-gather.5.cloned.1.call-update
  226.2 0.0 copy-done.4
  226.2 0.1 multiply_subtract_fusion
  226.4 0.0 all-gather.3.cloned.1.call-done
  226.4 53.0 %all-gather.5.cloned.1.call-done = bf16[16,96,1024]{2,1,0:T(8,128)(2,1)} async-done(((bf16[1,96,1024]{2,1,0:T(8,128)(2,1)}), bf16[16,96,1024]{2,1,0:T(8,128)(2,1)}) %all-gather.5.cloned.1.call-update) | async-done | bytes 3145744 | tf_op jit(solution)/shard_map/all_gather | solution.py:57
  279.4 3.4 %pad_maximum_fusion = bf16[2,2,4,192,1024]{4,3,2,1,0:T(8,128)(2,1)S(1)} fusion(bf16[2,1,4,192,1024]{4,3,2,1,0:T(8,128)(2,1)} %bitcast.94, bf16[2,1,4,192,1024]{4,3,2,1,0:T(8,128)(2,1)} %bitcast.93), kind=kLoop, calls=%fused_computation.6 | loop fusion | flops 3145728 | bytes 12582912 | tf_op jit(solution)/shard_map/stack | solution.py:61
  282.8 0.1 broadcast_in_dim.2
  282.9 2.0 fusion.4
  284.9 0.2 fusion.20
  285.1 0.8 slice_bitcast_fusion
  285.9 0.0 copy-start.1
  285.9 0.0 copy-start.3
  285.9 3.6 %maximum_bitcast_fusion = (bf16[8,1,192,2048]{3,2,1,0:T(8,128)(2,1)S(1)}, bf16[8,1,192,2048]{3,2,1,0:T(8,128)(2,1)}) fusion(bf16[8,192,1024]{2,1,0:T(8,128)(2,1)S(1)} %get-tuple-element.9, bf16[8,192,1024]{2,1,0:T(8,128)(2,1)S(1)} %get-tuple-element.10, bf16[8,192,1024]{2,1,0:T(8,128)(2,1)S(1)} %fusion.20), kind=kLoop, calls=%fused_computation.7 | loop fusion | flops 25165824 | bytes 22020096 | tf_op jit(solution)/shard_map/stack | solution.py:71
  289.5 0.0 copy-done.1
  289.5 0.4 copy-done.3
  290.0 5.6 %multiply_convert_fusion = bf16[8,2,192,128]{3,2,1,0:T(8,128)(2,1)S(1)} fusion(bf16[4,2048,128]{2,1,0:T(8,128)(2,1)S(1)} %bitcast.87, bf16[4,2048,128]{2,1,0:T(8,128)(2,1)S(1)} %bitcast.84, bf16[8,1,192,2048]{3,2,1,0:T(8,128)(2,1)} %get-tuple-element.14, bf16[8,1,192,2048]{3,2,1,0:T(8,128)(2,1)S(1)} %get-tuple-element.13), kind=kOutput, calls=%fused_computation.16 | convolution fusion | flops 1619787776 | bytes 17563648 | tf_op jit(solution)/shard_map/foqK,fKn->foqn/dot_general | solution.py:73
  295.6 1.0 copy.33
  (2 shorter events, 0.0 us)
Async XLA Ops:
  11.4 8.6 %copy-start.5 = (s32[6]{0:T(128)S(1)}, s32[6]{0:T(128)}, u32[]{:S(2)}) copy-start(s32[6]{0:T(128)} %param.4) | copy-start | bytes 76
  11.4 57.6 %all-to-all-start = ((bf16[32,2,128,128]{3,2,1,0:T(8,128)(2,1)}), bf16[32,2,128,128]{3,2,1,0:T(8,128)(2,1)S(1)}, u32[]{:S(2)}, u32[]{:S(2)}) async-start(bf16[32,2,128,128]{3,2,1,0:T(8,128)(2,1)} %bitcast.90), calls=%async_computation | async-start | bytes 4194304 | tf_op jit(solution)/shard_map/all_to_all | solution.py:54
  69.2 1.3 copy-start
  115.8 4.6 %collective-permute-start = (bf16[1,96,1024]{2,1,0:T(8,128)(2,1)S(1)}, bf16[1,96,1024]{2,1,0:T(8,128)(2,1)S(1)}, u32[]{:S(2)}, u32[]{:S(2)}) collective-permute-start(bf16[1,96,1024]{2,1,0:T(8,128)(2,1)S(1)} %bitcast.97), channel_id=1, source_target_pairs={{0,8},{8,0},{1,9},{9,1},{2,10},{10,2},{3,11},{11,3},{4,12},{12,4},... | collective-permute-start | bytes 589832 | tf_op jit(solution)/shard_map/ppermute | solution.py:38
  121.1 48.7 %all-to-all-start.2 = ((bf16[32,2,128,128]{3,2,1,0:T(8,128)(2,1)}), bf16[32,2,128,128]{3,2,1,0:T(8,128)(2,1)S(1)}, u32[]{:S(2)}, u32[]{:S(2)}) async-start(bf16[32,2,128,128]{3,2,1,0:T(8,128)(2,1)} %bitcast.89), calls=%async_computation.2 | async-start | bytes 4194304 | tf_op jit(solution)/shard_map/all_to_all | solution.py:54
  128.8 97.6 %all-gather.3.cloned.1.call-start = ((), (), s32[]{:S(2)}) async-start(), calls=%async_computation.4 | async-start | bytes 3342336 | tf_op jit(solution)/shard_map/all_gather | solution.py:53
  129.5 149.9 %all-gather.5.cloned.1.call-start = ((), (), s32[]{:S(2)}) async-start(), calls=%async_computation.5 | async-start | bytes 3342336 | tf_op jit(solution)/shard_map/all_gather | solution.py:57
  170.0 1.4 copy-start.2
  213.8 12.4 %copy-start.4 = (s32[6,1024]{1,0:T(8,128)S(1)}, s32[6,1024]{1,0:T(8,128)}, u32[]{:S(2)}) copy-start(s32[6,1024]{1,0:T(8,128)} %param.5) | copy-start | bytes 73732
  214.5 11.0 %collective-permute-start.1 = (bf16[1,96,1024]{2,1,0:T(8,128)(2,1)S(1)}, bf16[1,96,1024]{2,1,0:T(8,128)(2,1)S(1)}, u32[]{:S(2)}, u32[]{:S(2)}) collective-permute-start(bf16[1,96,1024]{2,1,0:T(8,128)(2,1)S(1)} %bitcast.96), channel_id=1, source_target_pairs={{0,8},{8,0},{1,9},{9,1},{2,10},{10,2},{3,11},{11,3},{4,12},{12,4},... | collective-permute-start | bytes 589832 | tf_op jit(solution)/shard_map/ppermute | solution.py:38
  285.9 3.7 %copy-start.1 = (bf16[4,2,8,128,128]{4,3,2,1,0:T(8,128)(2,1)S(1)}, bf16[4,2,8,128,128]{4,3,2,1,0:T(8,128)(2,1)}, u32[]{:S(2)}) copy-start(bf16[4,2,8,128,128]{4,3,2,1,0:T(8,128)(2,1)} %copy-done) | copy-start | bytes 6291460
  285.9 4.1 %copy-start.3 = (bf16[4,2,8,128,128]{4,3,2,1,0:T(8,128)(2,1)S(1)}, bf16[4,2,8,128,128]{4,3,2,1,0:T(8,128)(2,1)}, u32[]{:S(2)}) copy-start(bf16[4,2,8,128,128]{4,3,2,1,0:T(8,128)(2,1)} %copy-done.2) | copy-start | bytes 6291460
Sparse Core Ops, SparseCore 0:
  132.1 52.7 all-gather.2
  226.3 53.0 all-gather.4

commit v6 on v4

v6 whole, which is shorter than its diff:
```python
import jax
import jax.numpy as jnp
import numpy as np
from jax import lax
from jax.sharding import Mesh, PartitionSpec as P

SB = 32
ROUNDS = 6
WINDOWS = 8
PLANE = ("y", "x")
SHOT = ("zh", "c")


def taper_weights(taper_windows):
    return 0.5 - 0.5 * jnp.cos(jnp.pi * (taper_windows.astype(jnp.float32) + 1.0) / (WINDOWS + 1.0))


def gather_sources(receivers, source_block):
    freqs, comps, shots, node_dev = receivers.shape
    planes = lax.axis_size("y") * lax.axis_size("x")
    zl_size = lax.axis_size("zl")
    zl = lax.axis_index("zl")
    per_device = node_dev // SB
    slices = receivers.reshape(planes, shots, node_dev)
    plane_nodes = lax.all_to_all(slices, PLANE, 0, 0, tiled=True)
    owner = source_block // per_device
    column = jnp.arange(ROUNDS * SB, dtype=jnp.int32)
    owner_q = owner[column // SB]
    wanted = source_block[column // SB] % per_device * SB + column % SB
    keep = owner_q % zl_size == zl
    node = jnp.arange(node_dev, dtype=jnp.int32)
    where = jnp.arange(planes, dtype=jnp.int32)
    select = (
        (where[:, None, None] == (owner_q // zl_size)[None, None, :])
        & (node[None, :, None] == wanted[None, None, :])
        & keep[None, None, :]
    ).astype(receivers.dtype)
    picked = jnp.einsum("jkn,jnq->qk", plane_nodes, select, preferred_element_type=jnp.float32)
    picked = picked.astype(receivers.dtype)[None]
    picked = picked + lax.ppermute(picked, "zl", perm=[(0, 1), (1, 0)])
    gathered = lax.all_gather(picked, PLANE, axis=0, tiled=True)
    return gathered.reshape(freqs, comps, ROUNDS * SB, shots)


def body(spectra, source_block, taper_window):
    receivers = lax.all_to_all(spectra, SHOT, 0, 2, tiled=True)
    freqs, _, shots, node_dev = receivers.shape
    scale = 1.0 / jnp.sqrt(jnp.float32(shots))
    weight_rows = jnp.repeat(taper_weights(taper_window), SB, axis=0)

    source = gather_sources(receivers, source_block)
    tapered = (source.astype(jnp.float32) * weight_rows[None, None]).astype(jnp.bfloat16)
    real_part = tapered[:, 0]
    imag_part = tapered[:, 1]
    real_row = jnp.concatenate((real_part, imag_part), axis=2)
    imag_row = jnp.concatenate((-imag_part, real_part), axis=2)
    operator = jnp.stack((real_row, imag_row), axis=1)
    stacked = receivers.reshape(freqs, 2 * shots, node_dev)
    summed = jnp.einsum("foqK,fKn->foqn", operator, stacked, preferred_element_type=jnp.float32)
    out = (summed * scale).astype(jnp.bfloat16).reshape(freqs, 2, ROUNDS, SB, node_dev)
    return jnp.transpose(out, (2, 0, 1, 3, 4))


def solution(mesh):
    devices = np.asarray(mesh.devices).reshape(4, 4, 2, 4, 2)
    fine = Mesh(devices, ("y", "x", "zl", "zh", "c"))
    in_specs = (P(None, None, SHOT, ("y", "x", "zl")), P(), P())
    out_specs = P(None, SHOT, None, None, ("y", "x", "zl"))
    return jax.shard_map(body, mesh=fine, in_specs=in_specs, out_specs=out_specs, check_vma=False)
```

time: 295 us -> 281 us (0.953)
  waiting for transfers between devices: 160 us -> 126 us
  blocking collectives: 77 us -> 102 us
  other arithmetic: 19.1 us -> 15.1 us
    all_to_all x1, waiting for transfers between devices: 85.8 us -> 51.1 us  [gather_sources(): plane_nodes = lax.all_to_all(slices, PLANE, 0, 0, tiled=True)]
    all_to_all x1, blocking collectives: 77 us -> 102 us  [body(): receivers = lax.all_to_all(spectra, SHOT, 0, 2, tiled=True)]
    reduce_sum x1 -> x0, other arithmetic: 4.3 us -> none  [broadcast(): mine = jnp.sum(got, axis=0, keepdims=True)]
    gather x1 -> x2, other arithmetic: 3.75 us -> 7.66 us  [the longest x1 3.83 us: gather_sources(): wanted = source_block[column // SB] % per_device * SB + column % SB]
    eq x1 -> x3, other arithmetic: 3.79 us -> 0.12 us  [the longest x1 0.09 us: gather_sources(): node[None, :, None] == wanted[None, None, :]]
where the time goes in v6:
time: 281 us; the launch traced here: 279 us
  waiting for transfers between devices  126 us (45%)
  blocking collectives  102 us (36%)
  other arithmetic  15.1 us (5%)
  between operations  13.5 us (5%)
  matrix products  7.78 us (3%)
  starting transfers between devices  7.09 us (3%)
  local copies, waits for them, and re-layouts  6.29 us (2%)
    all_to_all x1, blocking collectives, body(): receivers = lax.all_to_all(spectra, SHOT, 0, 2, tiled=True)  102 us
    all_gather x1, waiting for transfers between devices, gather_sources(): gathered = lax.all_gather(picked, PLANE, axis=0, tiled=True)  66.8 us
    all_to_all x1, waiting for transfers between devices, gather_sources(): plane_nodes = lax.all_to_all(slices, PLANE, 0, 0, tiled=True)  51.1 us
    ppermute x1, waiting for transfers between devices, gather_sources(): picked = picked + lax.ppermute(picked, 'zl', perm=[(0, 1), (1, 0)])  8.58 us
    all_to_all x1, starting transfers between devices, gather_sources(): plane_nodes = lax.all_to_all(slices, PLANE, 0, 0, tiled=True)  6.96 us
  transfers between devices with their start and end apart: 3, of which 3 were waited for; matrix products, arithmetic and copies ran while one was open for 3% of the time, Pallas kernels for 0%

profile of v6, /device:TPU:73, one launch (start us, length us, event | category | flops | bytes accessed | tf_op | source)
XLA Modules:
  0.0 278.6 jit_solution(7365527908600892323)
XLA Ops:
  6.5 102.3 %all_to_all.20 = bf16[64,2,128,128]{3,2,1,0:T(8,128)(2,1)S(1)} all-to-all(bf16[64,2,128,128]{3,2,1,0:T(8,128)(2,1)} %param.3), channel_id=1, replica_groups=mesh['y'=4,'x'=4,'zl'=2,'zh'=4,'c'=2] {'zh','c'}, dimensions={0} | all-to-all | bytes 8388608 | tf_op jit(solution)/shard_map/all_to_all | solution.py:46
  108.8 2.3 copy.15
  111.2 0.0 copy-start.2
  111.2 0.0 copy-start.1
  111.2 7.0 %all-to-all-start.1 = ((bf16[16,1024,128]{2,1,0:T(8,128)(2,1)}), bf16[16,1024,128]{2,1,0:T(8,128)(2,1)}, u32[]{:S(2)}, u32[]{:S(2)}) async-start(bf16[16,1024,128]{2,1,0:T(8,128)(2,1)} %bitcast.53), calls=%async_computation.1 | async-start | bytes 8388608 | tf_op jit(solution)/shard_map/all_to_all | solution.py:25
  118.1 0.0 all-gather.2.cloned.1.call-start
  118.2 0.0 copy-done.2
  118.2 0.7 fusion.29
  118.9 3.8 %compare_select_fusion.1 = s32[192,1]{0,1:T(1,128)S(1)} fusion(s32[]{:T(128)} %bitcast, s32[]{:T(128)} %bitcast.1, s32[]{:T(128)} %bitcast.2, s32[]{:T(128)} %bitcast.3, s32[]{:T(128)} %bitcast.5, s32[]{:T(128)} %bitcast.4), kind=kLoop, calls=%fused_computation.26 | loop fusion | flops 4032 | bytes 792 | tf_op jit(solution)/shard_map/gather | solution.py:28
  122.7 0.7 fusion.28
  123.4 3.8 %compare_select_fusion.2 = s32[192,1]{0,1:T(1,128)S(1)} fusion(s32[]{:T(128)} %bitcast.7, s32[]{:T(128)} %bitcast.8, s32[]{:T(128)} %bitcast.9, s32[]{:T(128)} %bitcast.10, s32[]{:T(128)} %bitcast.12, s32[]{:T(128)} %bitcast.11), kind=kLoop, calls=%fused_computation.27 | loop fusion | flops 4032 | bytes 792 | tf_op jit(solution)/shard_map/gather | solution.py:29
  127.3 0.1 iota_compare_fusion
  127.4 51.1 %all-to-all-done.1 = bf16[16,1024,128]{2,1,0:T(8,128)(2,1)} async-done(((bf16[16,1024,128]{2,1,0:T(8,128)(2,1)}), bf16[16,1024,128]{2,1,0:T(8,128)(2,1)}, u32[]{:S(2)}, u32[]{:S(2)}) %all-to-all-start.1) | async-done | bytes 4194336 | tf_op jit(solution)/shard_map/all_to_all | solution.py:25
  178.5 3.7 %fusion.16 = bf16[1,192,1024]{2,1,0:T(8,128)(2,1)S(1)} fusion(bf16[16,1024,128]{2,1,0:T(8,128)(2,1)} %all-to-all-done.1, pred[192]{0:T(512)(128)(4,1)S(1)} %fusion.25, pred[128,192]{0,1:T(8,128)(4,1)S(1)} %iota_compare_fusion, pred[16,192]{1,0:T(8,128)(4,1)S(1)} %iota_compare_fusion.1), kind=kOutput, calls=%fused_computation.16 | convolution fusion | flops 806289408 | bytes 4615360 | tf_op jit(solution)/shard_map/jkn,jnq->qk/dot_general | solution.py:38
  182.2 0.1 collective-permute-start
  182.3 8.6 %collective-permute-done = bf16[1,192,1024]{2,1,0:T(8,128)(2,1)S(1)} collective-permute-done((bf16[1,192,1024]{2,1,0:T(8,128)(2,1)S(1)}, bf16[1,192,1024]{2,1,0:T(8,128)(2,1)S(1)}, u32[]{:S(2)}, u32[]{:S(2)}) %collective-permute-start) | collective-permute-done | bytes 393248 | tf_op jit(solution)/shard_map/ppermute | solution.py:40
  190.9 0.9 add.74
  191.8 0.0 all-gather.2.cloned.1.call-update
  191.8 0.0 copy-done.1
  191.8 0.1 multiply_subtract_fusion
  192.0 66.8 %all-gather.2.cloned.1.call-done = bf16[16,192,1024]{2,1,0:T(8,128)(2,1)} async-done(((bf16[1,192,1024]{2,1,0:T(8,128)(2,1)}), bf16[16,192,1024]{2,1,0:T(8,128)(2,1)}) %all-gather.2.cloned.1.call-update) | async-done | bytes 6291472 | tf_op jit(solution)/shard_map/all_gather | solution.py:41
  258.7 0.1 broadcast_in_dim.5
  258.8 4.7 %fusion.4 = bf16[8,2,192,1024]{3,2,0,1:T(8,128)(2,1)S(1)} fusion(f32[192,1024]{1,0:T(8,128)S(1)} %bitcast.57, bf16[8,2,192,1024]{3,2,1,0:T(8,128)(2,1)} %bitcast.56), kind=kLoop, calls=%fused_computation.5 | loop fusion | flops 9437184 | bytes 13369344 | tf_op jit(solution)/shard_map/convert_element_type | solution.py:52
  263.5 0.2 fusion.27
  263.7 0.8 slice_bitcast_fusion
  264.5 0.0 copy-start
  264.5 1.4 maximum_bitcast_fusion
  265.9 0.8 copy-done
  266.7 4.1 %multiply_convert_fusion = bf16[8,2,192,128]{3,2,1,0:T(8,128)(2,1)S(1)} fusion(bf16[8,2048,128,1]{2,1,3,0:T(8,128)(2,1)S(1)} %bitcast.54, bf16[8,1,192,2048]{3,2,1,0:T(8,128)(2,1)S(1)} %get-tuple-element.8, bf16[8,1,192,2048]{3,2,1,0:T(8,128)(2,1)S(1)} %get-tuple-element.7), kind=kOutput, calls=%fused_computation.10 | convolution fusion | flops 1617690624 | bytes 17563648 | tf_op jit(solution)/shard_map/foqK,fKn->foqn/dot_general | solution.py:59
  270.8 1.0 copy.24
  (5 shorter events, 0.1 us)
Async XLA Ops:
  111.2 7.0 %copy-start.2 = (s32[6]{0:T(128)S(1)}, s32[6]{0:T(128)}, u32[]{:S(2)}) copy-start(s32[6]{0:T(128)} %param.4) | copy-start | bytes 76
  111.2 80.7 %copy-start.1 = (s32[6,1024]{1,0:T(8,128)S(1)}, s32[6,1024]{1,0:T(8,128)}, u32[]{:S(2)}) copy-start(s32[6,1024]{1,0:T(8,128)} %param.5) | copy-start | bytes 73732
  111.2 67.4 %all-to-all-start.1 = ((bf16[16,1024,128]{2,1,0:T(8,128)(2,1)}), bf16[16,1024,128]{2,1,0:T(8,128)(2,1)}, u32[]{:S(2)}, u32[]{:S(2)}) async-start(bf16[16,1024,128]{2,1,0:T(8,128)(2,1)} %bitcast.53), calls=%async_computation.1 | async-start | bytes 8388608 | tf_op jit(solution)/shard_map/all_to_all | solution.py:25
  118.1 140.6 %all-gather.2.cloned.1.call-start = ((), (), s32[]{:S(2)}) async-start(), calls=%async_computation.2 | async-start | bytes 6684672 | tf_op jit(solution)/shard_map/all_gather | solution.py:41
  182.2 8.7 %collective-permute-start = (bf16[1,192,1024]{2,1,0:T(8,128)(2,1)S(1)}, bf16[1,192,1024]{2,1,0:T(8,128)(2,1)S(1)}, u32[]{:S(2)}, u32[]{:S(2)}) collective-permute-start(bf16[1,192,1024]{2,1,0:T(8,128)(2,1)S(1)} %fusion.16), channel_id=1, source_target_pairs={{0,8},{8,0},{1,9},{9,1},{2,10},{10,2},{3,11},{11,3},{4,12},{12,4},... | collective-permute-start | bytes 1179656 | tf_op jit(solution)/shard_map/ppermute | solution.py:40
  264.5 2.2 copy-start
Sparse Core Ops, SparseCore 0:
  191.9 66.7 all-gather.1

commit v7 on v6

--- a/solution.py
+++ b/solution.py
@@ -15,14 +15,15 @@
     return 0.5 - 0.5 * jnp.cos(jnp.pi * (taper_windows.astype(jnp.float32) + 1.0) / (WINDOWS + 1.0))
 
 
-def gather_sources(receivers, source_block):
-    freqs, comps, shots, node_dev = receivers.shape
+def gather_sources(spectra, source_block):
+    freqs, comps, shot_dev, node_dev = spectra.shape
+    groups = lax.axis_size("zh") * lax.axis_size("c")
     planes = lax.axis_size("y") * lax.axis_size("x")
     zl_size = lax.axis_size("zl")
     zl = lax.axis_index("zl")
     per_device = node_dev // SB
-    slices = receivers.reshape(planes, shots, node_dev)
-    plane_nodes = lax.all_to_all(slices, PLANE, 0, 0, tiled=True)
+    slots = spectra.reshape(groups, planes, shot_dev, node_dev)
+    plane_nodes = lax.all_to_all(slots, PLANE, 1, 1, tiled=True)
     owner = source_block // per_device
     column = jnp.arange(ROUNDS * SB, dtype=jnp.int32)
     owner_q = owner[column // SB]
@@ -34,21 +35,22 @@
         (where[:, None, None] == (owner_q // zl_size)[None, None, :])
         & (node[None, :, None] == wanted[None, None, :])
         & keep[None, None, :]
-    ).astype(receivers.dtype)
-    picked = jnp.einsum("jkn,jnq->qk", plane_nodes, select, preferred_element_type=jnp.float32)
-    picked = picked.astype(receivers.dtype)[None]
+    ).astype(spectra.dtype)
+    picked = jnp.einsum("gjkn,jnq->gqk", plane_nodes, select, preferred_element_type=jnp.float32)
+    picked = picked.astype(spectra.dtype)
     picked = picked + lax.ppermute(picked, "zl", perm=[(0, 1), (1, 0)])
-    gathered = lax.all_gather(picked, PLANE, axis=0, tiled=True)
-    return gathered.reshape(freqs, comps, ROUNDS * SB, shots)
+    mine = lax.all_to_all(picked, SHOT, 0, 2, tiled=True)
+    gathered = lax.all_gather(mine, PLANE, axis=0, tiled=True)
+    return gathered.reshape(freqs // groups, comps, ROUNDS * SB, shot_dev * groups)
 
 
 def body(spectra, source_block, taper_window):
+    source = gather_sources(spectra, source_block)
     receivers = lax.all_to_all(spectra, SHOT, 0, 2, tiled=True)
     freqs, _, shots, node_dev = receivers.shape
     scale = 1.0 / jnp.sqrt(jnp.float32(shots))
     weight_rows = jnp.repeat(taper_weights(taper_window), SB, axis=0)
 
-    source = gather_sources(receivers, source_block)
     tapered = (source.astype(jnp.float32) * weight_rows[None, None]).astype(jnp.bfloat16)
     real_part = tapered[:, 0]
     imag_part = tapered[:, 1]

time: 281 us -> 245 us (0.87)
  blocking collectives: 102 us -> 22.3 us
  waiting for transfers between devices: 126 us -> 154 us
  starting transfers between devices: 7.09 us -> 16.1 us
  local copies, waits for them, and re-layouts: 6.29 us -> 14.3 us
    all_to_all x1 -> x2, waiting for transfers between devices: 51.1 us -> 146 us  [the longest x1 94 us: body(): receivers = lax.all_to_all(spectra, SHOT, 0, 2, tiled=True)]
    all_to_all x1, blocking collectives: 102 us -> 22.3 us  [gather_sources(): mine = lax.all_to_all(picked, SHOT, 0, 2, tiled=True)]
    all_gather x1, waiting for transfers between devices: 66.8 us -> 0.01 us  [gather_sources(): gathered = lax.all_gather(mine, PLANE, axis=0, tiled=True)]
    all_to_all x1 -> x2, starting transfers between devices: 6.96 us -> 14.3 us  [the longest x1 7.37 us: body(): receivers = lax.all_to_all(spectra, SHOT, 0, 2, tiled=True)]
    reshape x0 -> x1, local copies, waits for them, and re-layouts: none -> 4.74 us  [gather_sources(): slots = spectra.reshape(groups, planes, shot_dev, node_dev)]
  transfers between devices with their start and end apart: 3 -> 4, of which waited for: 3 -> 3; matrix products, arithmetic and copies ran while one was open for 3% -> 6% of each run, Pallas kernels for 0% -> 0%
where the time goes in v7:
time: 245 us; the launch traced here: 242 us
  waiting for transfers between devices  154 us (63%)
  blocking collectives  22.3 us (9%)
  starting transfers between devices  16.1 us (7%)
  local copies, waits for them, and re-layouts  14.3 us (6%)
  other arithmetic  13.7 us (6%)
  between operations  13.5 us (6%)
  matrix products  7.67 us (3%)
    all_to_all x1, waiting for transfers between devices, body(): receivers = lax.all_to_all(spectra, SHOT, 0, 2, tiled=True)  94 us
    all_to_all x1, waiting for transfers between devices, gather_sources(): plane_nodes = lax.all_to_all(slots, PLANE, 1, 1, tiled=True)  52.5 us
    all_to_all x1, blocking collectives, gather_sources(): mine = lax.all_to_all(picked, SHOT, 0, 2, tiled=True)  22.3 us
    ppermute x1, waiting for transfers between devices, gather_sources(): picked = picked + lax.ppermute(picked, 'zl', perm=[(0, 1), (1, 0)])  7.5 us
    all_to_all x1, starting transfers between devices, body(): receivers = lax.all_to_all(spectra, SHOT, 0, 2, tiled=True)  7.37 us
    all_to_all x1, starting transfers between devices, gather_sources(): plane_nodes = lax.all_to_all(slots, PLANE, 1, 1, tiled=True)  6.96 us
  transfers between devices with their start and end apart: 4, of which 3 were waited for; matrix products, arithmetic and copies ran while one was open for 6% of the time, Pallas kernels for 0%

profile of v7, /device:TPU:73, one launch (start us, length us, event | category | flops | bytes accessed | tf_op | source)
XLA Modules:
  0.0 241.5 jit_solution(3172734364509222556)
XLA Ops:
  6.5 4.7 %copy.18 = bf16[8,16,128,128]{3,2,0,1:T(8,128)(2,1)} copy(bf16[8,16,128,128]{3,2,1,0:T(8,128)(2,1)} %bitcast.74) | data formatting | bytes 8388608 | tf_op jit(solution)/shard_map/reshape | solution.py:25
  11.3 0.0 copy-start.2
  11.3 7.0 %all-to-all-start = ((bf16[8,16,128,128]{3,2,0,1:T(8,128)(2,1)}), bf16[8,16,128,128]{3,2,0,1:T(8,128)(2,1)}, u32[]{:S(2)}, u32[]{:S(2)}) async-start(bf16[8,16,128,128]{3,2,0,1:T(8,128)(2,1)} %copy.18), calls=%async_computation | async-start | bytes 8388608 | tf_op jit(solution)/shard_map/all_to_all | solution.py:26
  18.2 0.0 all-gather.2.cloned.1.call-start
  18.3 0.0 copy-done.2
  18.3 0.6 fusion.30
  18.9 3.6 %compare_select_fusion.1 = s32[192,1]{0,1:T(1,128)S(1)} fusion(s32[]{:T(128)} %bitcast, s32[]{:T(128)} %bitcast.1, s32[]{:T(128)} %bitcast.2, s32[]{:T(128)} %bitcast.3, s32[]{:T(128)} %bitcast.5, s32[]{:T(128)} %bitcast.4), kind=kLoop, calls=%fused_computation.28 | loop fusion | flops 4032 | bytes 792 | tf_op jit(solution)/shard_map/gather | solution.py:29
  22.5 0.6 fusion.29
  23.1 3.6 %compare_select_fusion.2 = s32[192,1]{0,1:T(1,128)S(1)} fusion(s32[]{:T(128)} %bitcast.7, s32[]{:T(128)} %bitcast.8, s32[]{:T(128)} %bitcast.9, s32[]{:T(128)} %bitcast.10, s32[]{:T(128)} %bitcast.12, s32[]{:T(128)} %bitcast.11), kind=kLoop, calls=%fused_computation.29 | loop fusion | flops 4032 | bytes 792 | tf_op jit(solution)/shard_map/gather | solution.py:30
  26.7 0.1 iota_compare_fusion
  26.8 52.5 %all-to-all-done = bf16[8,16,128,128]{3,2,0,1:T(8,128)(2,1)} async-done(((bf16[8,16,128,128]{3,2,0,1:T(8,128)(2,1)}), bf16[8,16,128,128]{3,2,0,1:T(8,128)(2,1)}, u32[]{:S(2)}, u32[]{:S(2)}) %all-to-all-start) | async-done | bytes 4194336 | tf_op jit(solution)/shard_map/all_to_all | solution.py:26
  79.3 3.7 %fusion.17 = bf16[8,192,128]{2,1,0:T(8,128)(2,1)S(1)} fusion(bf16[8,16,128,128]{3,2,0,1:T(8,128)(2,1)} %all-to-all-done, pred[192]{0:T(512)(128)(4,1)S(1)} %fusion.26, pred[128,192]{0,1:T(8,128)(4,1)S(1)} %iota_compare_fusion, pred[16,192]{1,0:T(8,128)(4,1)S(1)} %iota_compare_fusion.1), kind=kOutput, calls=%fused_computation.17 | convolution fusion | flops 806289408 | bytes 4615360 | tf_op jit(solution)/shard_map/gjkn,jnq->gqk/dot_general | solution.py:39
  83.0 0.0 copy-start.1
  83.0 1.7 collective-permute-start
  84.7 7.5 %collective-permute-done = bf16[8,192,128]{2,1,0:T(8,128)(2,1)S(1)} collective-permute-done((bf16[8,192,128]{2,1,0:T(8,128)(2,1)S(1)}, bf16[8,192,128]{2,1,0:T(8,128)(2,1)S(1)}, u32[]{:S(2)}, u32[]{:S(2)}) %collective-permute-start) | collective-permute-done | bytes 393248 | tf_op jit(solution)/shard_map/ppermute | solution.py:41
  92.2 0.1 add.74
  92.4 22.3 %all_to_all.38 = bf16[8,192,128]{2,1,0:T(8,128)(2,1)S(1)} all-to-all(bf16[8,192,128]{2,1,0:T(8,128)(2,1)S(1)} %add.74), channel_id=1, replica_groups=mesh['y'=4,'x'=4,'zl'=2,'zh'=4,'c'=2] {'zh','c'}, dimensions={0} | all-to-all | bytes 786432 | tf_op jit(solution)/shard_map/all_to_all | solution.py:42
  114.6 0.8 copy_bitcast_fusion.1
  115.4 0.0 all-gather.2.cloned.1.call-update
  115.5 7.4 %all-to-all-start.2 = ((bf16[64,2,128,128]{3,2,1,0:T(8,128)(2,1)}), bf16[64,2,128,128]{3,2,1,0:T(8,128)(2,1)}, u32[]{:S(2)}, u32[]{:S(2)}) async-start(bf16[64,2,128,128]{3,2,1,0:T(8,128)(2,1)} %param.3), calls=%async_computation.2 | async-start | bytes 8388608 | tf_op jit(solution)/shard_map/all_to_all | solution.py:49
  122.8 0.0 copy-done.1
  122.8 0.1 multiply_subtract_fusion
  123.0 94.0 %all-to-all-done.2 = bf16[64,2,128,128]{3,2,1,0:T(8,128)(2,1)} async-done(((bf16[64,2,128,128]{3,2,1,0:T(8,128)(2,1)}), bf16[64,2,128,128]{3,2,1,0:T(8,128)(2,1)}, u32[]{:S(2)}, u32[]{:S(2)}) %all-to-all-start.2) | async-done | bytes 4194336 | tf_op jit(solution)/shard_map/all_to_all | solution.py:49
  216.9 4.8 %copy.23 = bf16[8,8,2,128,128]{4,3,0,2,1:T(8,128)(2,1)} copy(bf16[8,8,2,128,128]{4,3,2,1,0:T(8,128)(2,1)} %bitcast.28) | data formatting | bytes 8388608 | tf_op jit(solution)/shard_map/all_to_all | solution.py:49
  221.8 0.0 all-gather.2.cloned.1.call-done
  221.8 0.1 broadcast_in_dim.2
  221.8 4.7 %fusion.4 = bf16[8,2,192,1024]{3,2,0,1:T(8,128)(2,1)S(1)} fusion(f32[192,1024]{1,0:T(8,128)S(1)} %bitcast.77, bf16[8,2,192,1024]{3,2,1,0:T(8,128)(2,1)} %bitcast.75), kind=kLoop, calls=%fused_computation.5 | loop fusion | flops 9437184 | bytes 13369344 | tf_op jit(solution)/shard_map/convert_element_type | solution.py:54
  226.6 0.8 slice_bitcast_fusion
  227.3 0.2 fusion.28
  227.5 0.0 copy-start
  227.5 1.3 maximum_bitcast_fusion
  228.8 0.9 copy-done
  229.7 4.0 %multiply_convert_fusion = bf16[8,2,192,128]{3,2,1,0:T(8,128)(2,1)S(1)} fusion(bf16[8,2048,128,1]{2,1,3,0:T(8,128)(2,1)S(1)} %bitcast.76, bf16[8,1,192,2048]{3,2,1,0:T(8,128)(2,1)S(1)} %get-tuple-element.8, bf16[8,1,192,2048]{3,2,1,0:T(8,128)(2,1)S(1)} %get-tuple-element.7), kind=kOutput, calls=%fused_computation.10 | convolution fusion | flops 1617690624 | bytes 17563648 | tf_op jit(solution)/shard_map/foqK,fKn->foqn/dot_general | solution.py:61
  233.7 1.0 copy.33
  (5 shorter events, 0.1 us)
Async XLA Ops:
  11.3 7.0 %copy-start.2 = (s32[6]{0:T(128)S(1)}, s32[6]{0:T(128)}, u32[]{:S(2)}) copy-start(s32[6]{0:T(128)} %param.4) | copy-start | bytes 76
  11.3 68.0 %all-to-all-start = ((bf16[8,16,128,128]{3,2,0,1:T(8,128)(2,1)}), bf16[8,16,128,128]{3,2,0,1:T(8,128)(2,1)}, u32[]{:S(2)}, u32[]{:S(2)}) async-start(bf16[8,16,128,128]{3,2,0,1:T(8,128)(2,1)} %copy.18), calls=%async_computation | async-start | bytes 8388608 | tf_op jit(solution)/shard_map/all_to_all | solution.py:26
  18.2 203.5 %all-gather.2.cloned.1.call-start = ((), (), s32[]{:S(2)}) async-start(), calls=%async_computation.3 | async-start | bytes 6684672 | tf_op jit(solution)/shard_map/all_gather | solution.py:43
  83.0 39.8 %copy-start.1 = (s32[6,1024]{1,0:T(8,128)S(1)}, s32[6,1024]{1,0:T(8,128)}, u32[]{:S(2)}) copy-start(s32[6,1024]{1,0:T(8,128)} %param.5) | copy-start | bytes 73732
  83.0 9.2 %collective-permute-start = (bf16[8,192,128]{2,1,0:T(8,128)(2,1)S(1)}, bf16[8,192,128]{2,1,0:T(8,128)(2,1)S(1)}, u32[]{:S(2)}, u32[]{:S(2)}) collective-permute-start(bf16[8,192,128]{2,1,0:T(8,128)(2,1)S(1)} %fusion.17), channel_id=1, source_target_pairs={{0,8},{8,0},{1,9},{9,1},{2,10},{10,2},{3,11},{11,3},{4,12},{12,4},... | collective-permute-start | bytes 1179656 | tf_op jit(solution)/shard_map/ppermute | solution.py:41
  115.5 101.5 %all-to-all-start.2 = ((bf16[64,2,128,128]{3,2,1,0:T(8,128)(2,1)}), bf16[64,2,128,128]{3,2,1,0:T(8,128)(2,1)}, u32[]{:S(2)}, u32[]{:S(2)}) async-start(bf16[64,2,128,128]{3,2,1,0:T(8,128)(2,1)} %param.3), calls=%async_computation.2 | async-start | bytes 8388608 | tf_op jit(solution)/shard_map/all_to_all | solution.py:49
  227.5 2.2 copy-start
Sparse Core Ops, SparseCore 0:
  115.6 63.8 all-gather.1

commit v8 on v7

--- a/solution.py
+++ b/solution.py
@@ -44,9 +44,28 @@
     return gathered.reshape(freqs // groups, comps, ROUNDS * SB, shot_dev * groups)
 
 
+def exchange_shots(spectra):
+    freqs, comps, shot_dev, node_dev = spectra.shape
+    nz = lax.axis_size("zh")
+    nc = lax.axis_size("c")
+    groups = nz * nc
+    me = lax.axis_index("zh") * nc + lax.axis_index("c")
+    chunks = spectra.reshape(groups, freqs // groups, comps, shot_dev, node_dev)
+    arrived = [lax.dynamic_index_in_dim(chunks, me, axis=0, keepdims=False)]
+    for shift in range(1, groups):
+        target = (me + shift) % groups
+        pairs = [(a * nc + b, ((a * nc + b + shift) % groups)) for a in range(nz) for b in range(nc)]
+        piece = lax.dynamic_index_in_dim(chunks, target, axis=0, keepdims=False)
+        arrived.append(lax.ppermute(piece, SHOT, perm=pairs))
+    arrived = jnp.stack(arrived, axis=0)
+    order = (me - jnp.arange(groups, dtype=jnp.int32)) % groups
+    blocks = jnp.take(arrived, order, axis=0)
+    return jnp.transpose(blocks, (1, 2, 0, 3, 4)).reshape(freqs // groups, comps, groups * shot_dev, node_dev)
+
+
 def body(spectra, source_block, taper_window):
+    receivers = exchange_shots(spectra)
     source = gather_sources(spectra, source_block)
-    receivers = lax.all_to_all(spectra, SHOT, 0, 2, tiled=True)
     freqs, _, shots, node_dev = receivers.shape
     scale = 1.0 / jnp.sqrt(jnp.float32(shots))
     weight_rows = jnp.repeat(taper_weights(taper_window), SB, axis=0)

time: 245 us -> 254 us (1.037)
  local copies, waits for them, and re-layouts: 14.3 us -> 26.9 us
  waiting for transfers between devices: 154 us -> 143 us
  starting transfers between devices: 16.1 us -> 19.8 us
  other arithmetic: 13.7 us -> 16.8 us
    all_to_all x1 -> x0, waiting for transfers between devices: 94 us -> none  [body(): receivers = lax.all_to_all(spectra, SHOT, 0, 2, tiled=True)]
    ppermute x0 -> x7, waiting for transfers between devices: none -> 83.2 us  [exchange_shots(): arrived.append(lax.ppermute(piece, SHOT, perm=pairs))]
    ppermute x0 -> x7, starting transfers between devices: none -> 11 us  [exchange_shots(): arrived.append(lax.ppermute(piece, SHOT, perm=pairs))]
    all_to_all x1 -> x0, starting transfers between devices: 7.37 us -> none  [body(): receivers = lax.all_to_all(spectra, SHOT, 0, 2, tiled=True)]
    gather x0 -> x1, local copies, waits for them, and re-layouts: none -> 5.35 us  [exchange_shots(): blocks = jnp.take(arrived, order, axis=0)]
    unnamed x6 -> x12, local copies, waits for them, and re-layouts: 0.91 us -> 6.03 us
    all_to_all x1 -> x0, local copies, waits for them, and re-layouts: 4.81 us -> none  [body(): receivers = lax.all_to_all(spectra, SHOT, 0, 2, tiled=True)]
    gather x1, other arithmetic: 3.56 us -> 7.53 us  [gather_sources(): owner_q = owner[column // SB]]
  transfers between devices with their start and end apart: 4 -> 10, of which waited for: 3 -> 6; matrix products, arithmetic and copies ran while one was open for 6% -> 12% of each run, Pallas kernels for 0% -> 0%
where the time goes in v8:
time: 254 us; the launch traced here: 249 us
  waiting for transfers between devices  143 us (56%)
  local copies, waits for them, and re-layouts  26.9 us (11%)
  blocking collectives  22.1 us (9%)
  starting transfers between devices  19.8 us (8%)
  other arithmetic  16.8 us (7%)
  between operations  13.7 us (5%)
  matrix products  7.67 us (3%)
    ppermute x7, waiting for transfers between devices, exchange_shots(): arrived.append(lax.ppermute(piece, SHOT, perm=pairs))  83.2 us
    all_to_all x1, waiting for transfers between devices, gather_sources(): plane_nodes = lax.all_to_all(slots, PLANE, 1, 1, tiled=True)  51.9 us
    all_to_all x1, blocking collectives, gather_sources(): mine = lax.all_to_all(picked, SHOT, 0, 2, tiled=True)  22.1 us
    ppermute x7, starting transfers between devices, exchange_shots(): arrived.append(lax.ppermute(piece, SHOT, perm=pairs))  11 us
    gather x1, other arithmetic, gather_sources(): owner_q = owner[column // SB]  7.53 us
    ppermute x1, waiting for transfers between devices, gather_sources(): picked = picked + lax.ppermute(picked, 'zl', perm=[(0, 1), (1, 0)])  7.5 us
    all_to_all x1, starting transfers between devices, gather_sources(): plane_nodes = lax.all_to_all(slots, PLANE, 1, 1, tiled=True)  6.96 us
    unnamed x12, local copies, waits for them, and re-layouts  6.03 us
  transfers between devices with their start and end apart: 10, of which 6 were waited for; matrix products, arithmetic and copies ran while one was open for 12% of the time, Pallas kernels for 0%

profile of v8, /device:TPU:73, one launch (start us, length us, event | category | flops | bytes accessed | tf_op | source)
XLA Modules:
  0.0 249.5 jit_solution(11169742963479633452)
XLA Ops:
  6.5 4.8 %copy.18 = bf16[8,16,128,128]{3,2,0,1:T(8,128)(2,1)} copy(bf16[8,16,128,128]{3,2,1,0:T(8,128)(2,1)} %bitcast.104) | data formatting | bytes 8388608 | tf_op jit(solution)/shard_map/reshape | solution.py:25
  11.3 0.0 copy-start.2
  11.3 7.0 %all-to-all-start = ((bf16[8,16,128,128]{3,2,0,1:T(8,128)(2,1)}), bf16[8,16,128,128]{3,2,0,1:T(8,128)(2,1)}, u32[]{:S(2)}, u32[]{:S(2)}) async-start(bf16[8,16,128,128]{3,2,0,1:T(8,128)(2,1)} %copy.18), calls=%async_computation | async-start | bytes 8388608 | tf_op jit(solution)/shard_map/all_to_all | solution.py:26
  18.3 0.0 all-gather.2.cloned.1.call-start
  18.3 0.0 copy-done.2
  18.3 0.7 fusion.32
  19.0 0.7 fusion.33
  19.7 7.5 %compare_select_fusion.3 = (s32[192,1]{0,1:T(1,128)S(1)}, s32[192,1]{0,1:T(1,128)S(1)}) fusion(s32[]{:T(128)} %bitcast, s32[]{:T(128)} %bitcast.1, s32[]{:T(128)} %bitcast.2, s32[]{:T(128)} %bitcast.3, s32[]{:T(128)} %bitcast.5, s32[]{:T(128)} %bitcast.4, s32[]{:T(128)} %bitcast.12, s32[]{:T(128)} %bitcast.11, s32[]{:T(128)} %bitcast.10, s32[]{:T(128)} %bitcast.9, ...), kind=kLoop, calls=%fused_computation.48 | loop fusion | flops 4992 | bytes 1584 | tf_op jit(solution)/shard_map/gather | solution.py:29
  27.3 0.1 iota_compare_fusion
  27.4 51.9 %all-to-all-done = bf16[8,16,128,128]{3,2,0,1:T(8,128)(2,1)} async-done(((bf16[8,16,128,128]{3,2,0,1:T(8,128)(2,1)}), bf16[8,16,128,128]{3,2,0,1:T(8,128)(2,1)}, u32[]{:S(2)}, u32[]{:S(2)}) %all-to-all-start) | async-done | bytes 4194336 | tf_op jit(solution)/shard_map/all_to_all | solution.py:26
  79.3 3.7 %fusion.17 = bf16[8,192,128]{2,1,0:T(8,128)(2,1)S(1)} fusion(bf16[8,16,128,128]{3,2,0,1:T(8,128)(2,1)} %all-to-all-done, pred[192]{0:T(512)(128)(4,1)S(1)} %fusion.26, pred[128,192]{0,1:T(8,128)(4,1)S(1)} %iota_compare_fusion, pred[16,192]{1,0:T(8,128)(4,1)S(1)} %iota_compare_fusion.1), kind=kOutput, calls=%fused_computation.19 | convolution fusion | flops 806289408 | bytes 4615360 | tf_op jit(solution)/shard_map/gjkn,jnq->gqk/dot_general | solution.py:39
  83.0 1.7 collective-permute-start
  84.8 7.5 %collective-permute-done = bf16[8,192,128]{2,1,0:T(8,128)(2,1)S(1)} collective-permute-done((bf16[8,192,128]{2,1,0:T(8,128)(2,1)S(1)}, bf16[8,192,128]{2,1,0:T(8,128)(2,1)S(1)}, u32[]{:S(2)}, u32[]{:S(2)}) %collective-permute-start) | collective-permute-done | bytes 393248 | tf_op jit(solution)/shard_map/ppermute | solution.py:41
  92.3 0.1 add.177
  92.4 22.1 %all_to_all.23 = bf16[8,192,128]{2,1,0:T(8,128)(2,1)S(1)} all-to-all(bf16[8,192,128]{2,1,0:T(8,128)(2,1)S(1)} %add.177), channel_id=1, replica_groups=mesh['y'=4,'x'=4,'zl'=2,'zh'=4,'c'=2] {'zh','c'}, dimensions={0} | all-to-all | bytes 786432 | tf_op jit(solution)/shard_map/all_to_all | solution.py:42
  114.4 0.8 copy_bitcast_fusion.1
  115.2 0.0 all-gather.2.cloned.1.call-update
  115.4 0.0 copy-start.1
  115.4 3.5 %dynamic-slice_bitcast_fusion = (bf16[8,2,128,128]{3,2,1,0:T(8,128)(2,1)S(1)}, bf16[8,2,128,128]{3,2,1,0:T(8,128)(2,1)S(1)}, bf16[8,2,128,128]{3,2,1,0:T(8,128)(...) fusion(bf16[8,8,2,128,128]{4,3,2,1,0:T(8,128)(2,1)} %bitcast.10, ...), kind=kLoop, calls=%fused_computation.31 | loop fusion | bytes 8388640 | tf_op jit(solution)/shard_map/jit(dynamic_index_in_dim)/squeeze | solution.py:58
  118.9 1.6 collective-permute-start.1
  120.5 1.4 collective-permute-start.2
  122.0 3.7 %collective-permute-start.3 = (bf16[8,2,128,128]{3,2,1,0:T(8,128)(2,1)S(1)}, bf16[8,2,128,128]{3,2,1,0:T(8,128)(2,1)S(1)}, u32[]{:S(2)}, u32[]{:S(2)}) collective-permute-start(bf16[8,2,128,128]{3,2,1,0:T(8,128)(2,1)S(1)} %get-tuple-element.11), channel_id=1, source_target_pairs={{0,3},{1,4},{2,5},{3,6},{4,7},{5,0},{6,1},{7,2},{8,11},{9,12},{10,... | collective-permute-start | bytes 1572872 | tf_op jit(solution)/shard_map/ppermute | solution.py:59
  125.6 0.6 collective-permute-start.4
  126.2 2.5 %collective-permute-start.5 = (bf16[8,2,128,128]{3,2,1,0:T(8,128)(2,1)S(1)}, bf16[8,2,128,128]{3,2,1,0:T(8,128)(2,1)S(1)}, u32[]{:S(2)}, u32[]{:S(2)}) collective-permute-start(bf16[8,2,128,128]{3,2,1,0:T(8,128)(2,1)S(1)} %get-tuple-element.9), channel_id=1, source_target_pairs={{0,5},{1,6},{2,7},{3,0},{4,1},{5,2},{6,3},{7,4},{8,13},{9,14},{10,... | collective-permute-start | bytes 1572872 | tf_op jit(solution)/shard_map/ppermute | solution.py:59
  128.7 0.0 copy-done.1
  128.7 0.1 multiply_subtract_fusion
  128.9 9.8 %collective-permute-done.1 = bf16[8,2,128,128]{3,2,1,0:T(8,128)(2,1)S(1)} collective-permute-done((bf16[8,2,128,128]{3,2,1,0:T(8,128)(2,1)S(1)}, bf16[8,2,128,128]{3,2,1,0:T(8,128)(2,1)S(1)}, u32[]{:S(2)}, u32[]{:S(2)}) %collective-permute-start.1) | collective-permute-done | bytes 524320 | tf_op jit(solution)/shard_map/ppermute | solution.py:59
  138.7 1.2 collective-permute-start.6
  139.9 0.8 bitcast_dynamic-update-slice_fusion.6
  140.8 19.6 %collective-permute-done.2 = bf16[8,2,128,128]{3,2,1,0:T(8,128)(2,1)S(1)} collective-permute-done((bf16[8,2,128,128]{3,2,1,0:T(8,128)(2,1)S(1)}, bf16[8,2,128,128]{3,2,1,0:T(8,128)(2,1)S(1)}, u32[]{:S(2)}, u32[]{:S(2)}) %collective-permute-start.2) | collective-permute-done | bytes 524320 | tf_op jit(solution)/shard_map/ppermute | solution.py:59
  160.4 0.0 collective-permute-start.7
  160.4 0.8 bitcast_dynamic-update-slice_fusion.5
  161.2 38.0 %collective-permute-done.3 = bf16[8,2,128,128]{3,2,1,0:T(8,128)(2,1)S(1)} collective-permute-done((bf16[8,2,128,128]{3,2,1,0:T(8,128)(2,1)S(1)}, bf16[8,2,128,128]{3,2,1,0:T(8,128)(2,1)S(1)}, u32[]{:S(2)}, u32[]{:S(2)}) %collective-permute-start.3) | collective-permute-done | bytes 524320 | tf_op jit(solution)/shard_map/ppermute | solution.py:59
  199.2 0.9 bitcast_dynamic-update-slice_fusion.4
  200.1 15.9 %collective-permute-done.4 = bf16[8,2,128,128]{3,2,1,0:T(8,128)(2,1)S(1)} collective-permute-done((bf16[8,2,128,128]{3,2,1,0:T(8,128)(2,1)S(1)}, bf16[8,2,128,128]{3,2,1,0:T(8,128)(2,1)S(1)}, u32[]{:S(2)}, u32[]{:S(2)}) %collective-permute-start.4) | collective-permute-done | bytes 524320 | tf_op jit(solution)/shard_map/ppermute | solution.py:59
  215.9 0.9 bitcast_dynamic-update-slice_fusion.3
  216.8 0.0 collective-permute-done.5
  216.8 0.9 bitcast_dynamic-update-slice_fusion.2
  217.7 0.0 collective-permute-done.6
  217.7 0.8 bitcast_dynamic-update-slice_fusion.1
  218.5 0.0 collective-permute-done.7
  218.5 0.9 bitcast_dynamic-update-slice_fusion
  219.4 5.3 %gather_fusion = bf16[8,8,2,128,128]{4,3,2,1,0:T(8,128)(2,1)} fusion(bf16[8,8,2,128,128]{4,3,2,1,0:T(8,128)(2,1)} %bitcast_dynamic-update-slice_fusion, s32[1024]{0:T(1024)S(1)} %pad_clamp_fusion), kind=kCustom, calls=%fused_computation | custom fusion | bytes 8388640 | tf_op jit(solution)/shard_map/jit(_take)/gather | solution.py:62
  224.7 2.7 %select_bitcast_fusion = bf16[8,2,8,128,128]{4,3,1,0,2:T(8,128)(2,1)S(1)} fusion(bf16[8,8,2,128,128]{4,3,2,1,0:T(8,128)(2,1)} %gather_fusion, pred[8]{0:T(512)(128)(4,1)S(1)} %compare_and_fusion), kind=kLoop, calls=%fused_computation.9 | loop fusion | flops 2097152 | bytes 8388616 | tf_op jit(solution)/shard_map/jit(_take)/select_n | solution.py:62
  227.4 2.4 copy.23
  229.7 0.0 all-gather.2.cloned.1.call-done
  229.7 0.1 broadcast_in_dim.12
  229.8 4.7 %fusion.4 = bf16[8,2,192,1024]{3,2,0,1:T(8,128)(2,1)S(1)} fusion(f32[192,1024]{1,0:T(8,128)S(1)} %bitcast.108, bf16[8,2,192,1024]{3,2,1,0:T(8,128)(2,1)} %bitcast.106), kind=kLoop, calls=%fused_computation.6 | loop fusion | flops 9437184 | bytes 13369344 | tf_op jit(solution)/shard_map/convert_element_type | solution.py:73
  234.5 0.8 slice_bitcast_fusion
  235.3 0.2 fusion.31
  235.5 0.0 copy-start
  235.5 1.3 maximum_bitcast_fusion
  236.8 0.9 copy-done
  237.7 4.0 %multiply_convert_fusion = bf16[8,2,192,128]{3,2,1,0:T(8,128)(2,1)S(1)} fusion(bf16[8,2048,128,1]{2,1,3,0:T(8,128)(2,1)S(1)} %bitcast.107, bf16[8,1,192,2048]{3,2,1,0:T(8,128)(2,1)S(1)} %get-tuple-element.16, bf16[8,1,192,2048]{3,2,1,0:T(8,128)(2,1)S(1)} %get-tuple-element.15), kind=kOutput, calls=%fused_computation.12 | convolution fusion | flops 1617690624 | bytes 17563648 | tf_op jit(solution)/shard_map/foqK,fKn->foqn/dot_general | solution.py:80
  241.7 1.0 copy.33
  (8 shorter events, 0.1 us)
Async XLA Ops:
  11.3 7.0 %copy-start.2 = (s32[6]{0:T(128)S(1)}, s32[6]{0:T(128)}, u32[]{:S(2)}) copy-start(s32[6]{0:T(128)} %param.4) | copy-start | bytes 76
  11.3 68.0 %all-to-all-start = ((bf16[8,16,128,128]{3,2,0,1:T(8,128)(2,1)}), bf16[8,16,128,128]{3,2,0,1:T(8,128)(2,1)}, u32[]{:S(2)}, u32[]{:S(2)}) async-start(bf16[8,16,128,128]{3,2,0,1:T(8,128)(2,1)} %copy.18), calls=%async_computation | async-start | bytes 8388608 | tf_op jit(solution)/shard_map/all_to_all | solution.py:26
  18.3 211.5 %all-gather.2.cloned.1.call-start = ((), (), s32[]{:S(2)}) async-start(), calls=%async_computation.2 | async-start | bytes 6684672 | tf_op jit(solution)/shard_map/all_gather | solution.py:43
  83.0 9.2 %collective-permute-start = (bf16[8,192,128]{2,1,0:T(8,128)(2,1)S(1)}, bf16[8,192,128]{2,1,0:T(8,128)(2,1)S(1)}, u32[]{:S(2)}, u32[]{:S(2)}) collective-permute-start(bf16[8,192,128]{2,1,0:T(8,128)(2,1)S(1)} %fusion.17), channel_id=1, source_target_pairs={{0,8},{8,0},{1,9},{9,1},{2,10},{10,2},{3,11},{11,3},{4,12},{12,4},... | collective-permute-start | bytes 1179656 | tf_op jit(solution)/shard_map/ppermute | solution.py:41
  115.4 13.4 %copy-start.1 = (s32[6,1024]{1,0:T(8,128)S(1)}, s32[6,1024]{1,0:T(8,128)}, u32[]{:S(2)}) copy-start(s32[6,1024]{1,0:T(8,128)} %param.5) | copy-start | bytes 73732
  118.9 19.8 %collective-permute-start.1 = (bf16[8,2,128,128]{3,2,1,0:T(8,128)(2,1)S(1)}, bf16[8,2,128,128]{3,2,1,0:T(8,128)(2,1)S(1)}, u32[]{:S(2)}, u32[]{:S(2)}) collective-permute-start(bf16[8,2,128,128]{3,2,1,0:T(8,128)(2,1)S(1)} %get-tuple-element.13), channel_id=1, source_target_pairs={{0,1},{1,2},{2,3},{3,4},{4,5},{5,6},{6,7},{7,0},{8,9},{9,10},{10,1... | collective-permute-start | bytes 1572872 | tf_op jit(solution)/shard_map/ppermute | solution.py:59
  120.5 39.8 %collective-permute-start.2 = (bf16[8,2,128,128]{3,2,1,0:T(8,128)(2,1)S(1)}, bf16[8,2,128,128]{3,2,1,0:T(8,128)(2,1)S(1)}, u32[]{:S(2)}, u32[]{:S(2)}) collective-permute-start(bf16[8,2,128,128]{3,2,1,0:T(8,128)(2,1)S(1)} %get-tuple-element.12), channel_id=1, source_target_pairs={{0,2},{1,3},{2,4},{3,5},{4,6},{5,7},{6,0},{7,1},{8,10},{9,11},{10,... | collective-permute-start | bytes 1572872 | tf_op jit(solution)/shard_map/ppermute | solution.py:59
  122.0 77.2 %collective-permute-start.3 = (bf16[8,2,128,128]{3,2,1,0:T(8,128)(2,1)S(1)}, bf16[8,2,128,128]{3,2,1,0:T(8,128)(2,1)S(1)}, u32[]{:S(2)}, u32[]{:S(2)}) collective-permute-start(bf16[8,2,128,128]{3,2,1,0:T(8,128)(2,1)S(1)} %get-tuple-element.11), channel_id=1, source_target_pairs={{0,3},{1,4},{2,5},{3,6},{4,7},{5,0},{6,1},{7,2},{8,11},{9,12},{10,... | collective-permute-start | bytes 1572872 | tf_op jit(solution)/shard_map/ppermute | solution.py:59
  125.6 90.3 %collective-permute-start.4 = (bf16[8,2,128,128]{3,2,1,0:T(8,128)(2,1)S(1)}, bf16[8,2,128,128]{3,2,1,0:T(8,128)(2,1)S(1)}, u32[]{:S(2)}, u32[]{:S(2)}) collective-permute-start(bf16[8,2,128,128]{3,2,1,0:T(8,128)(2,1)S(1)} %get-tuple-element.10), channel_id=1, source_target_pairs={{0,4},{1,5},{2,6},{3,7},{4,0},{5,1},{6,2},{7,3},{8,12},{9,13},{10,... | collective-permute-start | bytes 1572872 | tf_op jit(solution)/shard_map/ppermute | solution.py:59
  126.2 90.6 %collective-permute-start.5 = (bf16[8,2,128,128]{3,2,1,0:T(8,128)(2,1)S(1)}, bf16[8,2,128,128]{3,2,1,0:T(8,128)(2,1)S(1)}, u32[]{:S(2)}, u32[]{:S(2)}) collective-permute-start(bf16[8,2,128,128]{3,2,1,0:T(8,128)(2,1)S(1)} %get-tuple-element.9), channel_id=1, source_target_pairs={{0,5},{1,6},{2,7},{3,0},{4,1},{5,2},{6,3},{7,4},{8,13},{9,14},{10,... | collective-permute-start | bytes 1572872 | tf_op jit(solution)/shard_map/ppermute | solution.py:59
  138.7 79.0 %collective-permute-start.6 = (bf16[8,2,128,128]{3,2,1,0:T(8,128)(2,1)S(1)}, bf16[8,2,128,128]{3,2,1,0:T(8,128)(2,1)S(1)}, u32[]{:S(2)}, u32[]{:S(2)}) collective-permute-start(bf16[8,2,128,128]{3,2,1,0:T(8,128)(2,1)S(1)} %get-tuple-element.8), channel_id=1, source_target_pairs={{0,6},{1,7},{2,0},{3,1},{4,2},{5,3},{6,4},{7,5},{8,14},{9,15},{10,... | collective-permute-start | bytes 1572872 | tf_op jit(solution)/shard_map/ppermute | solution.py:59
  160.4 58.1 %collective-permute-start.7 = (bf16[8,2,128,128]{3,2,1,0:T(8,128)(2,1)S(1)}, bf16[8,2,128,128]{3,2,1,0:T(8,128)(2,1)S(1)}, u32[]{:S(2)}, u32[]{:S(2)}) collective-permute-start(bf16[8,2,128,128]{3,2,1,0:T(8,128)(2,1)S(1)} %get-tuple-element.7), channel_id=1, source_target_pairs={{0,7},{1,0},{2,1},{3,2},{4,3},{5,4},{6,5},{7,6},{8,15},{9,8},{10,9... | collective-permute-start | bytes 1572872 | tf_op jit(solution)/shard_map/ppermute | solution.py:59
  235.5 2.2 copy-start
Sparse Core Ops, SparseCore 0:
  115.4 64.1 all-gather.1

commit v9 on v7

--- a/solution.py
+++ b/solution.py
@@ -15,38 +15,36 @@
     return 0.5 - 0.5 * jnp.cos(jnp.pi * (taper_windows.astype(jnp.float32) + 1.0) / (WINDOWS + 1.0))
 
 
-def gather_sources(spectra, source_block):
+def gather_sources(spectra, source_block, receivers=None):
     freqs, comps, shot_dev, node_dev = spectra.shape
     groups = lax.axis_size("zh") * lax.axis_size("c")
     planes = lax.axis_size("y") * lax.axis_size("x")
     zl_size = lax.axis_size("zl")
-    zl = lax.axis_index("zl")
     per_device = node_dev // SB
-    slots = spectra.reshape(groups, planes, shot_dev, node_dev)
-    plane_nodes = lax.all_to_all(slots, PLANE, 1, 1, tiled=True)
+    me = (lax.axis_index("y") * lax.axis_size("x") + lax.axis_index("x")) * zl_size + lax.axis_index("zl")
     owner = source_block // per_device
     column = jnp.arange(ROUNDS * SB, dtype=jnp.int32)
-    owner_q = owner[column // SB]
     wanted = source_block[column // SB] % per_device * SB + column % SB
-    keep = owner_q % zl_size == zl
+    keep = owner[column // SB] == me
     node = jnp.arange(node_dev, dtype=jnp.int32)
-    where = jnp.arange(planes, dtype=jnp.int32)
-    select = (
-        (where[:, None, None] == (owner_q // zl_size)[None, None, :])
-        & (node[None, :, None] == wanted[None, None, :])
-        & keep[None, None, :]
-    ).astype(spectra.dtype)
-    picked = jnp.einsum("gjkn,jnq->gqk", plane_nodes, select, preferred_element_type=jnp.float32)
-    picked = picked.astype(spectra.dtype)
-    picked = picked + lax.ppermute(picked, "zl", perm=[(0, 1), (1, 0)])
-    mine = lax.all_to_all(picked, SHOT, 0, 2, tiled=True)
+    select = ((node[:, None] == wanted[None, :]) & keep[None, :]).astype(spectra.dtype)
+    by_group = spectra.reshape(groups, freqs // groups, comps, shot_dev, node_dev)
+    picked = jnp.einsum("gfckn,nq->fcgqk", by_group, select, preferred_element_type=jnp.float32)
+    picked = picked.astype(spectra.dtype).reshape(planes * groups, ROUNDS * SB, shot_dev)
+    slot = lax.psum_scatter(picked, PLANE, scatter_dimension=0, tiled=True)
+    if receivers is not None:
+        slot, receivers = lax.optimization_barrier((slot, receivers))
+    both = jnp.broadcast_to(slot[None], (zl_size,) + slot.shape).reshape(zl_size * groups, ROUNDS * SB, shot_dev)
+    got = lax.all_to_all(both, ("zl",) + SHOT, 0, 0, tiled=True)
+    got = jnp.sum(got.reshape(zl_size, groups, ROUNDS * SB, shot_dev), axis=0)
+    mine = jnp.transpose(got, (1, 0, 2)).reshape(1, ROUNDS * SB, groups * shot_dev)
     gathered = lax.all_gather(mine, PLANE, axis=0, tiled=True)
-    return gathered.reshape(freqs // groups, comps, ROUNDS * SB, shot_dev * groups)
+    return gathered.reshape(freqs // groups, comps, ROUNDS * SB, shot_dev * groups), receivers
 
 
 def body(spectra, source_block, taper_window):
-    source = gather_sources(spectra, source_block)
     receivers = lax.all_to_all(spectra, SHOT, 0, 2, tiled=True)
+    source, receivers = gather_sources(spectra, source_block, receivers)
     freqs, _, shots, node_dev = receivers.shape
     scale = 1.0 / jnp.sqrt(jnp.float32(shots))
     weight_rows = jnp.repeat(taper_weights(taper_window), SB, axis=0)

time: 245 us -> 245 us (level)
  blocking collectives: 22.3 us -> 129 us
  waiting for transfers between devices: 154 us -> 64.4 us
  starting transfers between devices: 16.1 us -> 0.04 us
    all_to_all x2 -> x0, waiting for transfers between devices: 146 us -> none  [the longest x1 94 us: body(): receivers = lax.all_to_all(spectra, SHOT, 0, 2, tiled=True)]
    all_to_all x1 -> x2, blocking collectives: 22.3 us -> 129 us  [the longest x1 102 us: body(): receivers = lax.all_to_all(spectra, SHOT, 0, 2, tiled=True)]
    all_gather x1, waiting for transfers between devices: 0.01 us -> 64.4 us  [gather_sources(): gathered = lax.all_gather(mine, PLANE, axis=0, tiled=True)]
    all_to_all x2 -> x0, starting transfers between devices: 14.3 us -> none  [the longest x1 7.37 us: body(): receivers = lax.all_to_all(spectra, SHOT, 0, 2, tiled=True)]
    ppermute x1 -> x0, waiting for transfers between devices: 7.5 us -> none  [gather_sources(): picked = picked + lax.ppermute(picked, 'zl', perm=[(0, 1), (1, 0)])]
    reshape x1, local copies, waits for them, and re-layouts: 4.74 us -> 0.91 us  [gather_sources(): jnp.transpose(got, (1, 0, 2)).reshape(1, ROUNDS * SB, groups * shot_dev)]
    eq x3 -> x1, other arithmetic: 0.12 us -> 3.78 us  [gather_sources(): keep = owner[column // SB] == me]
    gather x1 -> x0, other arithmetic: 3.56 us -> none  [gather_sources(): owner_q = owner[column // SB]]
  transfers between devices with their start and end apart: 4 -> 2, of which waited for: 3 -> 1; matrix products, arithmetic and copies ran while one was open for 6% -> 1% of each run, Pallas kernels for 0% -> 0%
where the time goes in v9:
time: 245 us; the launch traced here: 243 us
  blocking collectives  129 us (53%)
  waiting for transfers between devices  64.4 us (26%)
  other arithmetic  14.8 us (6%)
  between operations  13.5 us (6%)
  local copies, waits for them, and re-layouts  12.5 us (5%)
  matrix products  8.1 us (3%)
    all_to_all x1, blocking collectives, body(): receivers = lax.all_to_all(spectra, SHOT, 0, 2, tiled=True)  102 us
    all_gather x1, waiting for transfers between devices, gather_sources(): gathered = lax.all_gather(mine, PLANE, axis=0, tiled=True)  64.4 us
    all_to_all x1, blocking collectives, gather_sources(): got = lax.all_to_all(both, ('zl',) + SHOT, 0, 0, tiled=True)  27.1 us
  transfers between devices with their start and end apart: 2, of which 1 were waited for; matrix products, arithmetic and copies ran while one was open for 1% of the time, Pallas kernels for 0%

profile of v9, /device:TPU:73, one launch (start us, length us, event | category | flops | bytes accessed | tf_op | source)
XLA Modules:
  0.0 242.8 jit_solution(16724848889324608719)
XLA Ops:
  6.5 0.0 reduce-scatter.2.cloned.1.call-start
  6.5 0.7 and_select_fusion.1
  7.2 1.6 fusion.18
  8.8 0.7 fusion.17
  9.4 3.7 %compare_select_fusion.1 = s32[192,1]{0,1:T(1,128)S(1)} fusion(s32[]{:T(128)} %bitcast, s32[]{:T(128)} %bitcast.1, s32[]{:T(128)} %bitcast.2, s32[]{:T(128)} %bitcast.3, s32[]{:T(128)} %bitcast.5, s32[]{:T(128)} %bitcast.4), kind=kLoop, calls=%fused_computation.22 | loop fusion | flops 4032 | bytes 792 | tf_op jit(solution)/shard_map/gather | solution.py:27
  13.1 3.8 %compare_reduce_fusion = pred[192]{0:T(512)(128)(4,1)S(1)} fusion(s32[]{:T(128)S(6)} %add.66, s32[]{:T(128)} %bitcast.7, s32[]{:T(128)} %bitcast.8, s32[]{:T(128)} %bitcast.9, s32[]{:T(128)} %bitcast.10, s32[]{:T(128)} %bitcast.12, s32[]{:T(128)} %bitcast.11), kind=kLoop, calls=%fused_computation.20 | loop fusion | flops 4224 | bytes 220 | tf_op jit(solution)/shard_map/eq | solution.py:28
  16.9 4.0 %convert_bitcast_fusion = bf16[8,2,8,192,128]{4,3,1,0,2:T(8,128)(2,1)S(1)} fusion(bf16[8,8,2,128,128]{4,3,2,1,0:T(8,128)(2,1)} %bitcast.56, s32[192]{0:T(256)S(1)} %fusion.12, pred[192]{0:T(512)(128)(4,1)S(1)} %compare_reduce_fusion), kind=kOutput, calls=%fused_computation.8 | convolution fusion | flops 808501248 | bytes 10486720 | tf_op jit(solution)/shard_map/gfckn,nq->fcgqk/dot_general | solution.py:32
  20.9 3.1 %copy.20 = bf16[8,2,8,192,128]{4,3,2,1,0:T(8,128)(2,1)} copy(bf16[8,2,8,192,128]{4,3,1,0,2:T(8,128)(2,1)S(1)} %convert_bitcast_fusion) | data formatting | bytes 12582912 | tf_op jit(solution)/shard_map/convert_element_type | solution.py:33
  24.0 0.0 reduce-scatter.2.cloned.1.call-update
  24.1 0.0 all-gather.2.cloned.1.call-start
  24.1 102.3 %all_to_all.23 = bf16[64,2,128,128]{3,2,1,0:T(8,128)(2,1)S(1)} all-to-all(bf16[64,2,128,128]{3,2,1,0:T(8,128)(2,1)} %param.3), channel_id=1, replica_groups=mesh['y'=4,'x'=4,'zl'=2,'zh'=4,'c'=2] {'zh','c'}, dimensions={0} | all-to-all | bytes 8388608 | tf_op jit(solution)/shard_map/all_to_all | solution.py:46
  126.4 0.0 copy-start.1
  126.4 2.3 copy.21
  128.7 0.0 reduce-scatter.2.cloned.1.call-done
  128.7 1.1 broadcast_in_dim.4
  129.9 27.1 %all_to_all.24 = bf16[16,192,128]{2,1,0:T(8,128)(2,1)S(1)} all-to-all(bf16[16,192,128]{2,1,0:T(8,128)(2,1)S(1)} %bitcast.62), channel_id=1, replica_groups=mesh['y'=4,'x'=4,'zl'=2,'zh'=4,'c'=2] {'zl','zh','c'}, dimensions={0} | all-to-all | bytes 1572864 | tf_op jit(solution)/shard_map/all_to_all | solution.py:38
  157.0 0.3 reduce_sum.12
  157.2 0.3 copy.22
  157.5 0.9 reshape.100
  158.4 0.0 all-gather.2.cloned.1.call-update
  158.4 0.0 copy-done.1
  158.4 0.1 multiply_subtract_fusion
  158.6 64.4 %all-gather.2.cloned.1.call-done = bf16[16,192,1024]{2,1,0:T(8,128)(2,1)} async-done(((bf16[1,192,1024]{2,1,0:T(8,128)(2,1)}), bf16[16,192,1024]{2,1,0:T(8,128)(2,1)}) %all-gather.2.cloned.1.call-update) | async-done | bytes 6291472 | tf_op jit(solution)/shard_map/all_gather | solution.py:41
  222.9 0.1 broadcast_in_dim.5
  223.0 4.7 %fusion.4 = bf16[8,2,192,1024]{3,2,0,1:T(8,128)(2,1)S(1)} fusion(f32[192,1024]{1,0:T(8,128)S(1)} %bitcast.60, bf16[8,2,192,1024]{3,2,1,0:T(8,128)(2,1)} %bitcast.58), kind=kLoop, calls=%fused_computation.5 | loop fusion | flops 9437184 | bytes 13369344 | tf_op jit(solution)/shard_map/convert_element_type | solution.py:52
  227.7 0.2 fusion.16
  227.9 0.8 slice_bitcast_fusion
  228.7 0.0 copy-start
  228.7 1.4 maximum_bitcast_fusion
  230.1 0.8 copy-done
  230.9 4.1 %multiply_convert_fusion = bf16[8,2,192,128]{3,2,1,0:T(8,128)(2,1)S(1)} fusion(bf16[8,2048,128,1]{2,1,3,0:T(8,128)(2,1)S(1)} %bitcast.59, bf16[8,1,192,2048]{3,2,1,0:T(8,128)(2,1)S(1)} %get-tuple-element.12, bf16[8,1,192,2048]{3,2,1,0:T(8,128)(2,1)S(1)} %get-tuple-element.11), kind=kOutput, calls=%fused_computation.11 | convolution fusion | flops 1617690624 | bytes 17563648 | tf_op jit(solution)/shard_map/foqK,fKn->foqn/dot_general | solution.py:59
  235.0 1.0 copy.32
  (1 shorter events, 0.0 us)
Async XLA Ops:
  6.5 122.2 %reduce-scatter.2.cloned.1.call-start = ((), (), s32[]{:S(2)}) async-start(), calls=%async_computation.3 | async-start | bytes 6684672 | tf_op jit(solution)/shard_map/reduce_scatter | solution.py:34
  24.1 198.9 %all-gather.2.cloned.1.call-start = ((), (), s32[]{:S(2)}) async-start(), calls=%async_computation.4 | async-start | bytes 6684672 | tf_op jit(solution)/shard_map/all_gather | solution.py:41
  126.4 32.0 %copy-start.1 = (s32[6,1024]{1,0:T(8,128)S(1)}, s32[6,1024]{1,0:T(8,128)}, u32[]{:S(2)}) copy-start(s32[6,1024]{1,0:T(8,128)} %param.5) | copy-start | bytes 73732
  228.7 2.2 copy-start
Sparse Core Ops, SparseCore 0:
  24.2 87.1 reduce-scatter.1
  158.6 64.3 all-gather.1

commit v10 on v9

--- a/solution.py
+++ b/solution.py
@@ -38,14 +38,25 @@
     got = lax.all_to_all(both, ("zl",) + SHOT, 0, 0, tiled=True)
     got = jnp.sum(got.reshape(zl_size, groups, ROUNDS * SB, shot_dev), axis=0)
     mine = jnp.transpose(got, (1, 0, 2)).reshape(1, ROUNDS * SB, groups * shot_dev)
-    gathered = lax.all_gather(mine, PLANE, axis=0, tiled=True)
-    return gathered.reshape(freqs // groups, comps, ROUNDS * SB, shot_dev * groups), receivers
+    return mine, receivers
+
+
+def exchange(part):
+    return lax.all_to_all(part, SHOT, 0, 2, tiled=True)
 
 
 def body(spectra, source_block, taper_window):
-    receivers = lax.all_to_all(spectra, SHOT, 0, 2, tiled=True)
-    source, receivers = gather_sources(spectra, source_block, receivers)
-    freqs, _, shots, node_dev = receivers.shape
+    freqs_all, comps, shot_dev, node_dev = spectra.shape
+    groups = lax.axis_size("zh") * lax.axis_size("c")
+    split = spectra.reshape(groups, 2, freqs_all // (groups * 2), comps, shot_dev, node_dev)
+    first = exchange(split[:, 0].reshape(-1, comps, shot_dev, node_dev))
+    mine, first = gather_sources(spectra, source_block, first)
+    second_part, mine = lax.optimization_barrier((split[:, 1].reshape(-1, comps, shot_dev, node_dev), mine))
+    gathered = lax.all_gather(mine, PLANE, axis=0, tiled=True)
+    second = exchange(second_part)
+    receivers = jnp.concatenate((first, second), axis=0)
+    freqs, _, shots, _ = receivers.shape
+    source = gathered.reshape(freqs, comps, ROUNDS * SB, shots)
     scale = 1.0 / jnp.sqrt(jnp.float32(shots))
     weight_rows = jnp.repeat(taper_weights(taper_window), SB, axis=0)
 

time: 245 us -> 228 us (0.931)
  blocking collectives: 129 us -> 87.3 us
  waiting for transfers between devices: 64.4 us -> 81 us
  starting transfers between devices: 0.04 us -> 4.63 us
  local copies, waits for them, and re-layouts: 12.5 us -> 16.7 us
    all_gather x1, waiting for transfers between devices: 64.4 us -> 7.52 us  [body(): gathered = lax.all_gather(mine, PLANE, axis=0, tiled=True)]
    all_to_all x0 -> x1, waiting for transfers between devices: none -> 48.9 us  [exchange(): return lax.all_to_all(part, SHOT, 0, 2, tiled=True)]
    all_to_all x1, blocking collectives: 102 us -> 57.2 us  [exchange(): return lax.all_to_all(part, SHOT, 0, 2, tiled=True)]
    reduce_scatter x1, waiting for transfers between devices: 0.01 us -> 24.5 us  [gather_sources(): slot = lax.psum_scatter(picked, PLANE, scatter_dimension=0, tiled=True)]
    all_to_all x0 -> x1, starting transfers between devices: none -> 4.59 us  [exchange(): return lax.all_to_all(part, SHOT, 0, 2, tiled=True)]
    slice x0 -> x1, local copies, waits for them, and re-layouts: none -> 4.13 us  [body(): first = exchange(split[:, 0].reshape(-1, comps, shot_dev, node_dev))]
    all_to_all x1, blocking collectives: 27.1 us -> 30.1 us  [gather_sources(): got = lax.all_to_all(both, ('zl',) + SHOT, 0, 0, tiled=True)]
  transfers between devices with their start and end apart: 2 -> 3, of which waited for: 1 -> 3; matrix products, arithmetic and copies ran while one was open for 1% -> 3% of each run, Pallas kernels for 0% -> 0%
where the time goes in v10:
time: 228 us; the launch traced here: 226 us
  blocking collectives  87.3 us (38%)
  waiting for transfers between devices  81 us (36%)
  local copies, waits for them, and re-layouts  16.7 us (7%)
  other arithmetic  14.9 us (7%)
  between operations  13.5 us (6%)
  matrix products  7.77 us (3%)
  starting transfers between devices  4.63 us (2%)
    all_to_all x1, blocking collectives, exchange(): return lax.all_to_all(part, SHOT, 0, 2, tiled=True)  57.2 us
    all_to_all x1, waiting for transfers between devices, exchange(): return lax.all_to_all(part, SHOT, 0, 2, tiled=True)  48.9 us
    all_to_all x1, blocking collectives, gather_sources(): got = lax.all_to_all(both, ('zl',) + SHOT, 0, 0, tiled=True)  30.1 us
    reduce_scatter x1, waiting for transfers between devices, gather_sources(): slot = lax.psum_scatter(picked, PLANE, scatter_dimension=0, tiled=True)  24.5 us
    all_gather x1, waiting for transfers between devices, body(): gathered = lax.all_gather(mine, PLANE, axis=0, tiled=True)  7.52 us
    convert_element_type x1, other arithmetic, body(): (source.astype(jnp.float32) * weight_rows[None, None]).astype(jnp.bfloat16)  4.71 us
    all_to_all x1, starting transfers between devices, exchange(): return lax.all_to_all(part, SHOT, 0, 2, tiled=True)  4.59 us
  transfers between devices with their start and end apart: 3, of which 3 were waited for; matrix products, arithmetic and copies ran while one was open for 3% of the time, Pallas kernels for 0%

profile of v10, /device:TPU:73, one launch (start us, length us, event | category | flops | bytes accessed | tf_op | source)
XLA Modules:
  0.0 225.9 jit_solution(5424237416384504300)
XLA Ops:
  6.5 0.0 reduce-scatter.2.cloned.1.call-start
  6.5 0.7 and_select_fusion.1
  7.2 1.5 fusion.21
  8.7 0.7 fusion.20
  9.4 3.8 %compare_select_fusion.1 = s32[192,1]{0,1:T(1,128)S(1)} fusion(s32[]{:T(128)} %bitcast.2, s32[]{:T(128)} %bitcast.3, s32[]{:T(128)} %bitcast.4, s32[]{:T(128)} %bitcast.5, s32[]{:T(128)} %bitcast.7, s32[]{:T(128)} %bitcast.6), kind=kLoop, calls=%fused_computation.25 | loop fusion | flops 4032 | bytes 792 | tf_op jit(solution)/shard_map/gather | solution.py:27
  13.3 3.7 %compare_reduce_fusion = pred[192]{0:T(512)(128)(4,1)S(1)} fusion(s32[]{:T(128)S(6)} %add.66, s32[]{:T(128)} %bitcast.9, s32[]{:T(128)} %bitcast.10, s32[]{:T(128)} %bitcast.11, s32[]{:T(128)} %bitcast.12, s32[]{:T(128)} %bitcast.14, s32[]{:T(128)} %bitcast.13), kind=kLoop, calls=%fused_computation.23 | loop fusion | flops 4224 | bytes 220 | tf_op jit(solution)/shard_map/eq | solution.py:28
  17.0 4.0 %convert_bitcast_fusion = bf16[8,2,8,192,128]{4,3,1,0,2:T(8,128)(2,1)S(1)} fusion(bf16[8,8,2,128,128]{4,3,2,1,0:T(8,128)(2,1)} %bitcast.69, s32[192]{0:T(256)S(1)} %fusion.14, pred[192]{0:T(512)(128)(4,1)S(1)} %compare_reduce_fusion), kind=kOutput, calls=%fused_computation.8 | convolution fusion | flops 808501248 | bytes 10486720 | tf_op jit(solution)/shard_map/gfckn,nq->fcgqk/dot_general | solution.py:32
  21.0 3.1 %copy.30 = bf16[8,2,8,192,128]{4,3,2,1,0:T(8,128)(2,1)} copy(bf16[8,2,8,192,128]{4,3,1,0,2:T(8,128)(2,1)S(1)} %convert_bitcast_fusion) | data formatting | bytes 12582912 | tf_op jit(solution)/shard_map/convert_element_type | solution.py:33
  24.1 0.0 reduce-scatter.2.cloned.1.call-update
  24.1 0.0 all-gather.2.cloned.1.call-start
  24.2 4.1 %fusion.19 = (bf16[8,1,4,2,128,128]{5,4,3,2,1,0:T(8,128)(2,1)S(1)}, bf16[8,1,4,2,128,128]{5,4,3,2,1,0:T(8,128)(2,1)}) fusion(bf16[8,2,4,2,128,128]{5,4,3,2,1,0:T(8,128)(2,1)} %bitcast.70), kind=kLoop, calls=%fused_computation.51 | loop fusion | bytes 8388608 | tf_op jit(solution)/shard_map/slice | solution.py:52
  28.3 57.2 %all_to_all.38 = bf16[32,2,128,128]{3,2,1,0:T(8,128)(2,1)S(1)} all-to-all(bf16[32,2,128,128]{3,2,1,0:T(8,128)(2,1)S(1)} %bitcast.74), channel_id=1, replica_groups=mesh['y'=4,'x'=4,'zl'=2,'zh'=4,'c'=2] {'zh','c'}, dimensions={0} | all-to-all | bytes 4194304 | tf_op jit(solution)/shard_map/all_to_all | solution.py:45
  85.6 0.0 copy-start.1
  85.6 1.5 copy.32
  87.0 24.5 %reduce-scatter.2.cloned.1.call-done = bf16[8,192,128]{2,1,0:T(8,128)(2,1)} async-done(((bf16[128,192,128]{2,1,0:T(8,128)(2,1)}), bf16[8,192,128]{2,1,0:T(8,128)(2,1)}) %reduce-scatter.2.cloned.1.call-update) | async-done | bytes 393232 | tf_op jit(solution)/shard_map/reduce_scatter | solution.py:34
  111.5 1.1 broadcast_in_dim.4
  112.7 30.1 %all_to_all.39 = bf16[16,192,128]{2,1,0:T(8,128)(2,1)S(1)} all-to-all(bf16[16,192,128]{2,1,0:T(8,128)(2,1)S(1)} %bitcast.78), channel_id=1, replica_groups=mesh['y'=4,'x'=4,'zl'=2,'zh'=4,'c'=2] {'zl','zh','c'}, dimensions={0} | all-to-all | bytes 1572864 | tf_op jit(solution)/shard_map/all_to_all | solution.py:38
  142.8 0.3 reduce_sum.12
  143.1 0.3 copy.33
  143.3 0.9 reshape.105
  144.2 0.0 all-gather.2.cloned.1.call-update
  144.3 4.6 %all-to-all-start.2 = ((bf16[32,2,128,128]{3,2,1,0:T(8,128)(2,1)}), bf16[32,2,128,128]{3,2,1,0:T(8,128)(2,1)S(1)}, u32[]{:S(2)}, u32[]{:S(2)}) async-start(bf16[32,2,128,128]{3,2,1,0:T(8,128)(2,1)} %bitcast.73), calls=%async_computation.3 | async-start | bytes 4194304 | tf_op jit(solution)/shard_map/all_to_all | solution.py:45
  148.8 0.0 copy-done.1
  148.8 0.1 multiply_subtract_fusion
  149.0 48.9 %all-to-all-done.2 = bf16[32,2,128,128]{3,2,1,0:T(8,128)(2,1)S(1)} async-done(((bf16[32,2,128,128]{3,2,1,0:T(8,128)(2,1)}), bf16[32,2,128,128]{3,2,1,0:T(8,128)(2,1)S(1)}, u32[]{:S(2)}, u32[]{:S(2)}) %all-to-all-start.2) | async-done | bytes 2097184 | tf_op jit(solution)/shard_map/all_to_all | solution.py:45
  197.9 1.5 copy.36
  199.4 7.5 %all-gather.2.cloned.1.call-done = bf16[16,192,1024]{2,1,0:T(8,128)(2,1)} async-done(((bf16[1,192,1024]{2,1,0:T(8,128)(2,1)}), bf16[16,192,1024]{2,1,0:T(8,128)(2,1)}) %all-gather.2.cloned.1.call-update) | async-done | bytes 6291472 | tf_op jit(solution)/shard_map/all_gather | solution.py:55
  206.9 0.1 broadcast_in_dim.5
  207.0 4.7 %fusion.4 = bf16[8,2,192,1024]{3,2,0,1:T(8,128)(2,1)S(1)} fusion(f32[192,1024]{1,0:T(8,128)S(1)} %bitcast.76, bf16[8,2,192,1024]{3,2,1,0:T(8,128)(2,1)} %bitcast.75), kind=kLoop, calls=%fused_computation.5 | loop fusion | flops 9437184 | bytes 13369344 | tf_op jit(solution)/shard_map/convert_element_type | solution.py:63
  211.7 0.2 fusion.18
  211.9 0.8 slice_bitcast_fusion
  212.7 0.0 copy-start
  212.7 1.4 maximum_bitcast_fusion
  214.1 0.2 copy-done
  214.3 3.8 %multiply_convert_fusion = bf16[8,2,192,128]{3,2,1,0:T(8,128)(2,1)S(1)} fusion(bf16[4,2048,128]{2,1,0:T(8,128)(2,1)} %bitcast.80, bf16[4,2048,128]{2,1,0:T(8,128)(2,1)S(1)} %bitcast.79, bf16[8,1,192,2048]{3,2,1,0:T(8,128)(2,1)S(1)} %get-tuple-element.18, bf16[8,1,192,2048]{3,2,1,0:T(8,128)(2,1)S(1)} %get-tuple-element.17), kind=kOutput, calls=%fused_computation.14 | convolution fusion | flops 1619787776 | bytes 17563648 | tf_op jit(solution)/shard_map/foqK,fKn->foqn/dot_general | solution.py:70
  218.0 1.0 copy.46
  (1 shorter events, 0.0 us)
Async XLA Ops:
  6.5 105.0 %reduce-scatter.2.cloned.1.call-start = ((), (), s32[]{:S(2)}) async-start(), calls=%async_computation.4 | async-start | bytes 6684672 | tf_op jit(solution)/shard_map/reduce_scatter | solution.py:34
  24.1 182.8 %all-gather.2.cloned.1.call-start = ((), (), s32[]{:S(2)}) async-start(), calls=%async_computation.5 | async-start | bytes 6684672 | tf_op jit(solution)/shard_map/all_gather | solution.py:55
  85.6 63.3 %copy-start.1 = (s32[6,1024]{1,0:T(8,128)S(1)}, s32[6,1024]{1,0:T(8,128)}, u32[]{:S(2)}) copy-start(s32[6,1024]{1,0:T(8,128)} %param.5) | copy-start | bytes 73732
  144.3 53.6 %all-to-all-start.2 = ((bf16[32,2,128,128]{3,2,1,0:T(8,128)(2,1)}), bf16[32,2,128,128]{3,2,1,0:T(8,128)(2,1)S(1)}, u32[]{:S(2)}, u32[]{:S(2)}) async-start(bf16[32,2,128,128]{3,2,1,0:T(8,128)(2,1)} %bitcast.73), calls=%async_computation.3 | async-start | bytes 4194304 | tf_op jit(solution)/shard_map/all_to_all | solution.py:45
  212.7 1.6 copy-start
Sparse Core Ops, SparseCore 0:
  24.3 87.2 reduce-scatter.1
  144.4 62.4 all-gather.1

commit v11 on v10

--- a/solution.py
+++ b/solution.py
@@ -22,10 +22,10 @@
     zl_size = lax.axis_size("zl")
     per_device = node_dev // SB
     me = (lax.axis_index("y") * lax.axis_size("x") + lax.axis_index("x")) * zl_size + lax.axis_index("zl")
-    owner = source_block // per_device
+    block = jnp.repeat(source_block, SB, total_repeat_length=ROUNDS * SB)
     column = jnp.arange(ROUNDS * SB, dtype=jnp.int32)
-    wanted = source_block[column // SB] % per_device * SB + column % SB
-    keep = owner[column // SB] == me
+    wanted = block % per_device * SB + column % SB
+    keep = block // per_device == me
     node = jnp.arange(node_dev, dtype=jnp.int32)
     select = ((node[:, None] == wanted[None, :]) & keep[None, :]).astype(spectra.dtype)
     by_group = spectra.reshape(groups, freqs // groups, comps, shot_dev, node_dev)

time: 228 us -> 224 us (0.982)
  other arithmetic: 14.9 us -> 11.2 us
    gather x1 -> x0, other arithmetic: 3.84 us -> none  [gather_sources(): wanted = source_block[column // SB] % per_device * SB + column % SB]
where the time goes in v11:
time: 224 us; the launch traced here: 221 us
  blocking collectives  87.3 us (39%)
  waiting for transfers between devices  80.9 us (36%)
  local copies, waits for them, and re-layouts  16.1 us (7%)
  between operations  13.5 us (6%)
  other arithmetic  11.2 us (5%)
  matrix products  7.78 us (3%)
  starting transfers between devices  4.63 us (2%)
    all_to_all x1, blocking collectives, exchange(): return lax.all_to_all(part, SHOT, 0, 2, tiled=True)  57.2 us
    all_to_all x1, waiting for transfers between devices, exchange(): return lax.all_to_all(part, SHOT, 0, 2, tiled=True)  48.9 us
    all_to_all x1, blocking collectives, gather_sources(): got = lax.all_to_all(both, ('zl',) + SHOT, 0, 0, tiled=True)  30.1 us
    reduce_scatter x1, waiting for transfers between devices, gather_sources(): slot = lax.psum_scatter(picked, PLANE, scatter_dimension=0, tiled=True)  24.4 us
    all_gather x1, waiting for transfers between devices, body(): gathered = lax.all_gather(mine, PLANE, axis=0, tiled=True)  7.54 us
    convert_element_type x1, other arithmetic, body(): (source.astype(jnp.float32) * weight_rows[None, None]).astype(jnp.bfloat16)  4.71 us
    all_to_all x1, starting transfers between devices, exchange(): return lax.all_to_all(part, SHOT, 0, 2, tiled=True)  4.59 us
  transfers between devices with their start and end apart: 3, of which 3 were waited for; matrix products, arithmetic and copies ran while one was open for 3% of the time, Pallas kernels for 0%

profile of v11, /device:TPU:73, one launch (start us, length us, event | category | flops | bytes accessed | tf_op | source)
XLA Modules:
  0.0 221.4 jit_solution(11559184032630844803)
XLA Ops:
  6.5 0.0 reduce-scatter.2.cloned.1.call-start
  6.5 1.5 fusion.20
  8.1 0.7 add_bitcast_fusion
  8.8 3.7 %fusion.16 = (pred[192]{0:T(512)(128)(4,1)S(1)}, s32[192]{0:T(256)S(1)}) fusion(s32[]{:T(128)S(6)} %add.61, s32[]{:T(128)} %bitcast.8, s32[]{:T(128)} %bitcast.7, s32[]{:T(128)} %bitcast.6, s32[]{:T(128)} %bitcast.5, s32[]{:T(128)} %bitcast.4, s32[]{:T(128)} %bitcast.3, s32[256]{0:T(256)S(1)} %add_bitcast_fusion), kind=kLoop, calls=%fused_computation.38 | loop fusion | flops 6528 | bytes 1756 | tf_op jit(solution)/shard_map/eq | solution.py:28
  12.6 4.0 %convert_bitcast_fusion = bf16[8,2,8,192,128]{4,3,1,0,2:T(8,128)(2,1)S(1)} fusion(bf16[8,8,2,128,128]{4,3,2,1,0:T(8,128)(2,1)} %bitcast.64, s32[192]{0:T(256)S(1)} %fusion.14, pred[192]{0:T(512)(128)(4,1)S(1)} %get-tuple-element.25), kind=kOutput, calls=%fused_computation.8 | convolution fusion | flops 808501248 | bytes 10486720 | tf_op jit(solution)/shard_map/gfckn,nq->fcgqk/dot_general | solution.py:32
  16.6 3.1 %copy.30 = bf16[8,2,8,192,128]{4,3,2,1,0:T(8,128)(2,1)} copy(bf16[8,2,8,192,128]{4,3,1,0,2:T(8,128)(2,1)S(1)} %convert_bitcast_fusion) | data formatting | bytes 12582912 | tf_op jit(solution)/shard_map/convert_element_type | solution.py:33
  19.7 0.0 reduce-scatter.2.cloned.1.call-update
  19.7 0.0 all-gather.2.cloned.1.call-start
  19.8 4.1 %fusion.19 = (bf16[8,1,4,2,128,128]{5,4,3,2,1,0:T(8,128)(2,1)S(1)}, bf16[8,1,4,2,128,128]{5,4,3,2,1,0:T(8,128)(2,1)}) fusion(bf16[8,2,4,2,128,128]{5,4,3,2,1,0:T(8,128)(2,1)} %bitcast.65), kind=kLoop, calls=%fused_computation.44 | loop fusion | bytes 8388608 | tf_op jit(solution)/shard_map/slice | solution.py:52
  23.9 57.2 %all_to_all.38 = bf16[32,2,128,128]{3,2,1,0:T(8,128)(2,1)S(1)} all-to-all(bf16[32,2,128,128]{3,2,1,0:T(8,128)(2,1)S(1)} %bitcast.69), channel_id=1, replica_groups=mesh['y'=4,'x'=4,'zl'=2,'zh'=4,'c'=2] {'zh','c'}, dimensions={0} | all-to-all | bytes 4194304 | tf_op jit(solution)/shard_map/all_to_all | solution.py:45
  81.2 0.0 copy-start.1
  81.2 1.5 copy.32
  82.6 24.4 %reduce-scatter.2.cloned.1.call-done = bf16[8,192,128]{2,1,0:T(8,128)(2,1)} async-done(((bf16[128,192,128]{2,1,0:T(8,128)(2,1)}), bf16[8,192,128]{2,1,0:T(8,128)(2,1)}) %reduce-scatter.2.cloned.1.call-update) | async-done | bytes 393232 | tf_op jit(solution)/shard_map/reduce_scatter | solution.py:34
  107.1 1.1 broadcast_in_dim.27
  108.2 30.1 %all_to_all.39 = bf16[16,192,128]{2,1,0:T(8,128)(2,1)S(1)} all-to-all(bf16[16,192,128]{2,1,0:T(8,128)(2,1)S(1)} %bitcast.73), channel_id=1, replica_groups=mesh['y'=4,'x'=4,'zl'=2,'zh'=4,'c'=2] {'zl','zh','c'}, dimensions={0} | all-to-all | bytes 1572864 | tf_op jit(solution)/shard_map/all_to_all | solution.py:38
  138.3 0.3 reduce_sum.12
  138.6 0.3 copy.33
  138.9 0.9 reshape.124
  139.8 0.0 all-gather.2.cloned.1.call-update
  139.8 4.6 %all-to-all-start.2 = ((bf16[32,2,128,128]{3,2,1,0:T(8,128)(2,1)}), bf16[32,2,128,128]{3,2,1,0:T(8,128)(2,1)S(1)}, u32[]{:S(2)}, u32[]{:S(2)}) async-start(bf16[32,2,128,128]{3,2,1,0:T(8,128)(2,1)} %bitcast.68), calls=%async_computation.3 | async-start | bytes 4194304 | tf_op jit(solution)/shard_map/all_to_all | solution.py:45
  144.4 0.0 copy-done.1
  144.4 0.1 multiply_subtract_fusion
  144.5 48.9 %all-to-all-done.2 = bf16[32,2,128,128]{3,2,1,0:T(8,128)(2,1)S(1)} async-done(((bf16[32,2,128,128]{3,2,1,0:T(8,128)(2,1)}), bf16[32,2,128,128]{3,2,1,0:T(8,128)(2,1)S(1)}, u32[]{:S(2)}, u32[]{:S(2)}) %all-to-all-start.2) | async-done | bytes 2097184 | tf_op jit(solution)/shard_map/all_to_all | solution.py:45
  193.4 1.5 copy.36
  194.9 7.5 %all-gather.2.cloned.1.call-done = bf16[16,192,1024]{2,1,0:T(8,128)(2,1)} async-done(((bf16[1,192,1024]{2,1,0:T(8,128)(2,1)}), bf16[16,192,1024]{2,1,0:T(8,128)(2,1)}) %all-gather.2.cloned.1.call-update) | async-done | bytes 6291472 | tf_op jit(solution)/shard_map/all_gather | solution.py:55
  202.5 0.1 broadcast_in_dim.28
  202.6 4.7 %fusion.4 = bf16[8,2,192,1024]{3,2,0,1:T(8,128)(2,1)S(1)} fusion(f32[192,1024]{1,0:T(8,128)S(1)} %bitcast.71, bf16[8,2,192,1024]{3,2,1,0:T(8,128)(2,1)} %bitcast.70), kind=kLoop, calls=%fused_computation.5 | loop fusion | flops 9437184 | bytes 13369344 | tf_op jit(solution)/shard_map/convert_element_type | solution.py:63
  207.3 0.2 fusion.18
  207.5 0.8 slice_bitcast_fusion
  208.3 0.0 copy-start
  208.3 1.4 maximum_bitcast_fusion
  209.7 0.2 copy-done
  209.9 3.8 %multiply_convert_fusion = bf16[8,2,192,128]{3,2,1,0:T(8,128)(2,1)S(1)} fusion(bf16[4,2048,128]{2,1,0:T(8,128)(2,1)} %bitcast.75, bf16[4,2048,128]{2,1,0:T(8,128)(2,1)S(1)} %bitcast.74, bf16[8,1,192,2048]{3,2,1,0:T(8,128)(2,1)S(1)} %get-tuple-element.32, bf16[8,1,192,2048]{3,2,1,0:T(8,128)(2,1)S(1)} %get-tuple-element.31), kind=kOutput, calls=%fused_computation.14 | convolution fusion | flops 1619787776 | bytes 17563648 | tf_op jit(solution)/shard_map/foqK,fKn->foqn/dot_general | solution.py:70
  213.6 1.0 copy.46
  (2 shorter events, 0.0 us)
Async XLA Ops:
  6.5 100.6 %reduce-scatter.2.cloned.1.call-start = ((), (), s32[]{:S(2)}) async-start(), calls=%async_computation.4 | async-start | bytes 6684672 | tf_op jit(solution)/shard_map/reduce_scatter | solution.py:34
  19.7 182.7 %all-gather.2.cloned.1.call-start = ((), (), s32[]{:S(2)}) async-start(), calls=%async_computation.5 | async-start | bytes 6684672 | tf_op jit(solution)/shard_map/all_gather | solution.py:55
  81.2 63.2 %copy-start.1 = (s32[6,1024]{1,0:T(8,128)S(1)}, s32[6,1024]{1,0:T(8,128)}, u32[]{:S(2)}) copy-start(s32[6,1024]{1,0:T(8,128)} %param.7) | copy-start | bytes 73732
  139.8 53.6 %all-to-all-start.2 = ((bf16[32,2,128,128]{3,2,1,0:T(8,128)(2,1)}), bf16[32,2,128,128]{3,2,1,0:T(8,128)(2,1)S(1)}, u32[]{:S(2)}, u32[]{:S(2)}) async-start(bf16[32,2,128,128]{3,2,1,0:T(8,128)(2,1)} %bitcast.68), calls=%async_computation.3 | async-start | bytes 4194304 | tf_op jit(solution)/shard_map/all_to_all | solution.py:45
  208.3 1.6 copy-start
Sparse Core Ops, SparseCore 0:
  19.9 87.1 reduce-scatter.1
  139.9 62.5 all-gather.1

commit v12 on v11

--- a/solution.py
+++ b/solution.py
@@ -51,23 +51,24 @@
     split = spectra.reshape(groups, 2, freqs_all // (groups * 2), comps, shot_dev, node_dev)
     first = exchange(split[:, 0].reshape(-1, comps, shot_dev, node_dev))
     mine, first = gather_sources(spectra, source_block, first)
+    weight_rows = jnp.repeat(taper_weights(taper_window), SB, axis=0)
+    mine = (mine.astype(jnp.float32) * weight_rows[None]).astype(jnp.bfloat16)
     second_part, mine = lax.optimization_barrier((split[:, 1].reshape(-1, comps, shot_dev, node_dev), mine))
     gathered = lax.all_gather(mine, PLANE, axis=0, tiled=True)
     second = exchange(second_part)
     receivers = jnp.concatenate((first, second), axis=0)
     freqs, _, shots, _ = receivers.shape
-    source = gathered.reshape(freqs, comps, ROUNDS * SB, shots)
+    tapered = gathered.reshape(freqs, comps, ROUNDS * SB, shots)
     scale = 1.0 / jnp.sqrt(jnp.float32(shots))
-    weight_rows = jnp.repeat(taper_weights(taper_window), SB, axis=0)
 
-    tapered = (source.astype(jnp.float32) * weight_rows[None, None]).astype(jnp.bfloat16)
-    real_part = tapered[:, 0]
-    imag_part = tapered[:, 1]
-    real_row = jnp.concatenate((real_part, imag_part), axis=2)
-    imag_row = jnp.concatenate((-imag_part, real_part), axis=2)
-    operator = jnp.stack((real_row, imag_row), axis=1)
-    stacked = receivers.reshape(freqs, 2 * shots, node_dev)
-    summed = jnp.einsum("foqK,fKn->foqn", operator, stacked, preferred_element_type=jnp.float32)
+    def dot(a, b):
+        return jnp.einsum("fqk,fkn->fqn", a, b, preferred_element_type=jnp.float32)
+
+    real_part, imag_part = tapered[:, 0], tapered[:, 1]
+    rec_real, rec_imag = receivers[:, 0], receivers[:, 1]
+    real = dot(real_part, rec_real) + dot(imag_part, rec_imag)
+    imag = dot(real_part, rec_imag) - dot(imag_part, rec_real)
+    summed = jnp.stack((real, imag), axis=1)
     out = (summed * scale).astype(jnp.bfloat16).reshape(freqs, 2, ROUNDS, SB, node_dev)
     return jnp.transpose(out, (2, 0, 1, 3, 4))
 

time: 224 us -> 224 us (level)
  waiting for transfers between devices: 80.9 us -> 55.2 us
  blocking collectives: 87.3 us -> 111 us
  starting transfers between devices: 4.63 us -> 8.85 us
  other arithmetic: 11.2 us -> 8.05 us
  matrix products: 7.78 us -> 10.2 us
    all_to_all x1 -> x2, blocking collectives: 57.2 us -> 111 us  [exchange(): return lax.all_to_all(part, SHOT, 0, 2, tiled=True)]
    all_to_all x1 -> x0, blocking collectives: 30.1 us -> none  [gather_sources(): got = lax.all_to_all(both, ('zl',) + SHOT, 0, 0, tiled=True)]
    all_to_all x1, waiting for transfers between devices: 48.9 us -> 21.3 us  [gather_sources(): got = lax.all_to_all(both, ('zl',) + SHOT, 0, 0, tiled=True)]
    all_to_all x1, starting transfers between devices: 4.59 us -> 8.81 us  [gather_sources(): got = lax.all_to_all(both, ('zl',) + SHOT, 0, 0, tiled=True)]
    convert_element_type x1 -> x2, other arithmetic: 4.71 us -> 2.07 us  [body(): mine = (mine.astype(jnp.float32) * weight_rows[None]).astype(jnp.bfloat16)]
    dot_general x1 -> x4, matrix products: 3.75 us -> 6.21 us  [dot(): return jnp.einsum('fqk,fkn->fqn', a, b, preferred_element_type=jnp.float32)]
where the time goes in v12:
time: 224 us; the launch traced here: 222 us
  blocking collectives  111 us (50%)
  waiting for transfers between devices  55.2 us (25%)
  local copies, waits for them, and re-layouts  15.2 us (7%)
  between operations  13.5 us (6%)
  matrix products  10.2 us (5%)
  starting transfers between devices  8.85 us (4%)
  other arithmetic  8.05 us (4%)
    all_to_all x2, blocking collectives, exchange(): return lax.all_to_all(part, SHOT, 0, 2, tiled=True)  111 us
    reduce_scatter x1, waiting for transfers between devices, gather_sources(): slot = lax.psum_scatter(picked, PLANE, scatter_dimension=0, tiled=True)  25.9 us
    all_to_all x1, waiting for transfers between devices, gather_sources(): got = lax.all_to_all(both, ('zl',) + SHOT, 0, 0, tiled=True)  21.3 us
    all_to_all x1, starting transfers between devices, gather_sources(): got = lax.all_to_all(both, ('zl',) + SHOT, 0, 0, tiled=True)  8.81 us
    all_gather x1, waiting for transfers between devices, body(): gathered = lax.all_gather(mine, PLANE, axis=0, tiled=True)  7.95 us
    dot_general x4, matrix products, dot(): return jnp.einsum('fqk,fkn->fqn', a, b, preferred_element_type=jnp.float32)  6.21 us
  transfers between devices with their start and end apart: 3, of which 3 were waited for; matrix products, arithmetic and copies ran while one was open for 3% of the time, Pallas kernels for 0%

profile of v12, /device:TPU:73, one launch (start us, length us, event | category | flops | bytes accessed | tf_op | source)
XLA Modules:
  0.0 221.7 jit_solution(18216266873673130187)
XLA Ops:
  6.5 0.0 reduce-scatter.2.cloned.1.call-start
  6.5 1.5 fusion.27
  8.1 0.7 add_bitcast_fusion
  8.8 3.7 %fusion.21 = (pred[192]{0:T(512)(128)(4,1)S(1)}, s32[192]{0:T(256)S(1)}) fusion(s32[]{:T(128)S(6)} %add.64, s32[]{:T(128)} %bitcast.8, s32[]{:T(128)} %bitcast.7, s32[]{:T(128)} %bitcast.6, s32[]{:T(128)} %bitcast.5, s32[]{:T(128)} %bitcast.4, s32[]{:T(128)} %bitcast.3, s32[256]{0:T(256)S(1)} %add_bitcast_fusion), kind=kLoop, calls=%fused_computation.44 | loop fusion | flops 6528 | bytes 1756 | tf_op jit(solution)/shard_map/eq | solution.py:28
  12.6 4.0 %convert_bitcast_fusion = bf16[8,2,8,192,128]{4,3,1,0,2:T(8,128)(2,1)S(1)} fusion(bf16[8,8,2,128,128]{4,3,2,1,0:T(8,128)(2,1)} %bitcast.72, s32[192]{0:T(256)S(1)} %fusion.19, pred[192]{0:T(512)(128)(4,1)S(1)} %get-tuple-element.25), kind=kOutput, calls=%fused_computation | convolution fusion | flops 808501248 | bytes 10486720 | tf_op jit(solution)/shard_map/gfckn,nq->fcgqk/dot_general | solution.py:32
  16.6 3.1 %copy.25 = bf16[8,2,8,192,128]{4,3,2,1,0:T(8,128)(2,1)} copy(bf16[8,2,8,192,128]{4,3,1,0,2:T(8,128)(2,1)S(1)} %convert_bitcast_fusion) | data formatting | bytes 12582912 | tf_op jit(solution)/shard_map/convert_element_type | solution.py:33
  19.7 0.0 reduce-scatter.2.cloned.1.call-update
  19.7 2.6 %fusion.26 = (bf16[8,1,4,2,128,128]{5,4,3,2,1,0:T(8,128)(2,1)S(1)}, bf16[8,1,4,2,128,128]{5,4,3,2,1,0:T(8,128)(2,1)S(1)}) fusion(bf16[8,2,4,2,128,128]{5,4,3,2,1,0:T(8,128)(2,1)} %bitcast.73), kind=kLoop, calls=%fused_computation.50 | loop fusion | bytes 8388608 | tf_op jit(solution)/shard_map/slice | solution.py:52
  22.4 57.2 %all_to_all.41 = bf16[32,2,128,128]{3,2,1,0:T(8,128)(2,1)S(1)} all-to-all(bf16[32,2,128,128]{3,2,1,0:T(8,128)(2,1)S(1)} %bitcast.77), channel_id=1, replica_groups=mesh['y'=4,'x'=4,'zl'=2,'zh'=4,'c'=2] {'zh','c'}, dimensions={0} | all-to-all | bytes 4194304 | tf_op jit(solution)/shard_map/all_to_all | solution.py:45
  79.6 1.5 copy.27
  81.1 0.0 copy-start.2
  81.1 25.9 %reduce-scatter.2.cloned.1.call-done = bf16[8,192,128]{2,1,0:T(8,128)(2,1)} async-done(((bf16[128,192,128]{2,1,0:T(8,128)(2,1)}), bf16[8,192,128]{2,1,0:T(8,128)(2,1)}) %reduce-scatter.2.cloned.1.call-update) | async-done | bytes 393232 | tf_op jit(solution)/shard_map/reduce_scatter | solution.py:34
  107.0 2.0 broadcast_in_dim.27
  109.1 8.8 %all-to-all-start.1 = ((bf16[16,192,128]{2,1,0:T(8,128)(2,1)}), bf16[16,192,128]{2,1,0:T(8,128)(2,1)S(1)}, u32[]{:S(2)}, u32[]{:S(2)}) async-start(bf16[16,192,128]{2,1,0:T(8,128)(2,1)} %bitcast.79), calls=%async_computation.2 | async-start | bytes 1572864 | tf_op jit(solution)/shard_map/all_to_all | solution.py:38
  117.9 0.0 all-gather.2.cloned.1.call-start
  117.9 0.0 copy-done.2
  117.9 0.1 multiply_subtract_fusion
  118.1 21.3 %all-to-all-done.1 = bf16[16,192,128]{2,1,0:T(8,128)(2,1)S(1)} async-done(((bf16[16,192,128]{2,1,0:T(8,128)(2,1)}), bf16[16,192,128]{2,1,0:T(8,128)(2,1)S(1)}, u32[]{:S(2)}, u32[]{:S(2)}) %all-to-all-start.1) | async-done | bytes 786464 | tf_op jit(solution)/shard_map/all_to_all | solution.py:38
  139.4 0.3 reduce_sum.12
  139.6 0.1 convert_bitcast_fusion.1
  139.7 0.5 copy.28
  140.2 1.0 reshape.150
  141.2 0.1 broadcast_in_dim.28
  141.2 2.0 fusion.11
  143.3 0.0 all-gather.2.cloned.1.call-update
  143.3 53.4 %all_to_all.42 = bf16[32,2,128,128]{3,2,1,0:T(8,128)(2,1)S(1)} all-to-all(bf16[32,2,128,128]{3,2,1,0:T(8,128)(2,1)S(1)} %bitcast.76), channel_id=1, replica_groups=mesh['y'=4,'x'=4,'zl'=2,'zh'=4,'c'=2] {'zh','c'}, dimensions={0} | all-to-all | bytes 4194304 | tf_op jit(solution)/shard_map/all_to_all | solution.py:45
  196.6 0.0 copy-start
  196.6 1.5 copy.30
  198.1 8.0 %all-gather.2.cloned.1.call-done = bf16[16,192,1024]{2,1,0:T(8,128)(2,1)} async-done(((bf16[1,192,1024]{2,1,0:T(8,128)(2,1)}), bf16[16,192,1024]{2,1,0:T(8,128)(2,1)}) %all-gather.2.cloned.1.call-update) | async-done | bytes 6291472 | tf_op jit(solution)/shard_map/all_gather | solution.py:57
  206.1 0.0 copy-done
  206.1 0.0 copy-start.1
  206.1 0.0 copy-start.3
  206.1 3.3 %fusion.1 = f32[8,192,128]{2,1,0:T(8,128)S(1)} fusion(bf16[8,2,192,1024]{3,2,1,0:T(8,128)(2,1)} %bitcast.91, bf16[4,2,1024,128]{3,2,0,1:T(8,128)(2,1)S(1)} %bitcast.81, bf16[4,2,1024,128]{3,2,0,1:T(8,128)(2,1)} %bitcast.85), kind=kOutput, calls=%fused_computation.6 | convolution fusion | flops 403701760 | bytes 8126464 | tf_op jit(solution)/shard_map/fqk,fkn->fqn/dot_general | solution.py:65
  209.4 0.0 copy-done.1
  209.4 1.4 copy-done.3
  210.8 1.0 fusion
  211.8 1.0 fusion.8
  212.7 1.0 fusion.9
  213.7 1.1 fusion.10
  (2 shorter events, 0.0 us)
Async XLA Ops:
  6.5 100.5 %reduce-scatter.2.cloned.1.call-start = ((), (), s32[]{:S(2)}) async-start(), calls=%async_computation.4 | async-start | bytes 6684672 | tf_op jit(solution)/shard_map/reduce_scatter | solution.py:34
  81.1 36.8 %copy-start.2 = (s32[6,1024]{1,0:T(8,128)S(1)}, s32[6,1024]{1,0:T(8,128)}, u32[]{:S(2)}) copy-start(s32[6,1024]{1,0:T(8,128)} %param.7) | copy-start | bytes 73732
  109.1 30.3 %all-to-all-start.1 = ((bf16[16,192,128]{2,1,0:T(8,128)(2,1)}), bf16[16,192,128]{2,1,0:T(8,128)(2,1)S(1)}, u32[]{:S(2)}, u32[]{:S(2)}) async-start(bf16[16,192,128]{2,1,0:T(8,128)(2,1)} %bitcast.79), calls=%async_computation.2 | async-start | bytes 1572864 | tf_op jit(solution)/shard_map/all_to_all | solution.py:38
  117.9 88.2 %all-gather.2.cloned.1.call-start = ((), (), s32[]{:S(2)}) async-start(), calls=%async_computation.5 | async-start | bytes 6684672 | tf_op jit(solution)/shard_map/all_gather | solution.py:57
  196.6 9.5 %copy-start = (bf16[4,2,8,128,128]{4,3,2,0,1:T(8,128)(2,1)S(1)}, bf16[4,2,8,128,128]{4,3,2,0,1:T(8,128)(2,1)}, u32[]{:S(2)}) copy-start(bf16[4,2,8,128,128]{4,3,2,0,1:T(8,128)(2,1)} %copy.27) | copy-start | bytes 6291460
  206.1 3.3 %copy-start.1 = (bf16[4,2,8,128,128]{4,3,2,0,1:T(8,128)(2,1)S(1)}, bf16[4,2,8,128,128]{4,3,2,0,1:T(8,128)(2,1)}, u32[]{:S(2)}) copy-start(bf16[4,2,8,128,128]{4,3,2,0,1:T(8,128)(2,1)} %copy.30) | copy-start | bytes 6291460
  206.1 4.7 %copy-start.3 = (bf16[16,192,1024]{2,1,0:T(8,128)(2,1)S(1)}, bf16[16,192,1024]{2,1,0:T(8,128)(2,1)}, u32[]{:S(2)}) copy-start(bf16[16,192,1024]{2,1,0:T(8,128)(2,1)} %all-gather.2.cloned.1.call-done) | copy-start | bytes 18874372
Sparse Core Ops, SparseCore 0:
  19.9 87.1 reduce-scatter.1
  143.4 62.6 all-gather.1

commit v13 on v11

--- a/solution.py
+++ b/solution.py
@@ -28,8 +28,8 @@
     keep = block // per_device == me
     node = jnp.arange(node_dev, dtype=jnp.int32)
     select = ((node[:, None] == wanted[None, :]) & keep[None, :]).astype(spectra.dtype)
-    by_group = spectra.reshape(groups, freqs // groups, comps, shot_dev, node_dev)
-    picked = jnp.einsum("gfckn,nq->fcgqk", by_group, select, preferred_element_type=jnp.float32)
+    by_slot = jnp.transpose(spectra.reshape(groups, planes, shot_dev, node_dev), (1, 0, 2, 3))
+    picked = jnp.einsum("pgkn,nq->pgqk", by_slot, select, preferred_element_type=jnp.float32)
     picked = picked.astype(spectra.dtype).reshape(planes * groups, ROUNDS * SB, shot_dev)
     slot = lax.psum_scatter(picked, PLANE, scatter_dimension=0, tiled=True)
     if receivers is not None:

time: 224 us -> 223 us (level)
  local copies, waits for them, and re-layouts: 16.1 us -> 13 us
  matrix products: 7.78 us -> 10.4 us
    convert_element_type x1 -> x0, local copies, waits for them, and re-layouts: 3.11 us -> none  [gather_sources(): picked.astype(spectra.dtype).reshape(planes * groups, ROUNDS * SB, shot_dev)]
    dot_general x1, matrix products: 4.03 us -> 6.69 us  [gather_sources(): jnp.einsum('pgkn,nq->pgqk', by_slot, select, preferred_element_type=jnp.f...]
where the time goes in v13:
time: 223 us; the launch traced here: 221 us
  blocking collectives  87.3 us (39%)
  waiting for transfers between devices  80.9 us (36%)
  between operations  13.5 us (6%)
  local copies, waits for them, and re-layouts  13 us (6%)
  other arithmetic  11.2 us (5%)
  matrix products  10.4 us (5%)
  starting transfers between devices  4.63 us (2%)
    all_to_all x1, blocking collectives, exchange(): return lax.all_to_all(part, SHOT, 0, 2, tiled=True)  57.2 us
    all_to_all x1, waiting for transfers between devices, exchange(): return lax.all_to_all(part, SHOT, 0, 2, tiled=True)  48.9 us
    all_to_all x1, blocking collectives, gather_sources(): got = lax.all_to_all(both, ('zl',) + SHOT, 0, 0, tiled=True)  30.1 us
    reduce_scatter x1, waiting for transfers between devices, gather_sources(): slot = lax.psum_scatter(picked, PLANE, scatter_dimension=0, tiled=True)  24.4 us
    all_gather x1, waiting for transfers between devices, body(): gathered = lax.all_gather(mine, PLANE, axis=0, tiled=True)  7.54 us
    dot_general x1, matrix products, gather_sources(): jnp.einsum('pgkn,nq->pgqk', by_slot, select, preferred_element_type=jnp.f...  6.69 us
    convert_element_type x1, other arithmetic, body(): (source.astype(jnp.float32) * weight_rows[None, None]).astype(jnp.bfloat16)  4.71 us
    all_to_all x1, starting transfers between devices, exchange(): return lax.all_to_all(part, SHOT, 0, 2, tiled=True)  4.59 us
  transfers between devices with their start and end apart: 3, of which 3 were waited for; matrix products, arithmetic and copies ran while one was open for 3% of the time, Pallas kernels for 0%

profile of v13, /device:TPU:73, one launch (start us, length us, event | category | flops | bytes accessed | tf_op | source)
XLA Modules:
  0.0 221.0 jit_solution(8968868274949475769)
XLA Ops:
  6.5 0.0 reduce-scatter.2.cloned.1.call-start
  6.5 1.5 fusion.26
  8.1 0.7 add_bitcast_fusion
  8.8 3.7 %fusion.22 = (pred[192]{0:T(512)(128)(4,1)S(1)}, s32[192]{0:T(256)S(1)}) fusion(s32[]{:T(128)S(6)} %add.61, s32[]{:T(128)} %bitcast.8, s32[]{:T(128)} %bitcast.7, s32[]{:T(128)} %bitcast.6, s32[]{:T(128)} %bitcast.5, s32[]{:T(128)} %bitcast.4, s32[]{:T(128)} %bitcast.3, s32[256]{0:T(256)S(1)} %add_bitcast_fusion), kind=kLoop, calls=%fused_computation.41 | loop fusion | flops 6528 | bytes 1756 | tf_op jit(solution)/shard_map/eq | solution.py:28
  12.6 6.7 %fusion.10 = bf16[192,16,8,128]{3,0,2,1:T(8,128)(2,1)} fusion(s32[192]{0:T(256)S(1)} %fusion.20, pred[192]{0:T(512)(128)(4,1)S(1)} %get-tuple-element.25, bf16[8,16,128,128]{3,2,1,0:T(8,128)(2,1)} %bitcast.74), kind=kOutput, calls=%fused_computation.14 | convolution fusion | flops 808501248 | bytes 10486720 | tf_op jit(solution)/shard_map/pgkn,nq->pgqk/dot_general | solution.py:32
  19.3 0.0 reduce-scatter.2.cloned.1.call-update
  19.3 0.0 all-gather.2.cloned.1.call-start
  19.3 4.1 %fusion.25 = (bf16[8,1,4,2,128,128]{5,4,3,2,1,0:T(8,128)(2,1)S(1)}, bf16[8,1,4,2,128,128]{5,4,3,2,1,0:T(8,128)(2,1)}) fusion(bf16[8,2,4,2,128,128]{5,4,3,2,1,0:T(8,128)(2,1)} %bitcast.75), kind=kLoop, calls=%fused_computation.47 | loop fusion | bytes 8388608 | tf_op jit(solution)/shard_map/slice | solution.py:52
  23.5 57.2 %all_to_all.38 = bf16[32,2,128,128]{3,2,1,0:T(8,128)(2,1)S(1)} all-to-all(bf16[32,2,128,128]{3,2,1,0:T(8,128)(2,1)S(1)} %bitcast.79), channel_id=1, replica_groups=mesh['y'=4,'x'=4,'zl'=2,'zh'=4,'c'=2] {'zh','c'}, dimensions={0} | all-to-all | bytes 4194304 | tf_op jit(solution)/shard_map/all_to_all | solution.py:45
  80.7 0.0 copy-start.1
  80.7 1.5 copy.33
  82.2 24.4 %reduce-scatter.2.cloned.1.call-done = bf16[8,192,128]{2,1,0:T(8,128)(2,1)} async-done(((bf16[128,192,128]{2,1,0:T(8,128)(2,1)}), bf16[8,192,128]{2,1,0:T(8,128)(2,1)}) %reduce-scatter.2.cloned.1.call-update) | async-done | bytes 393232 | tf_op jit(solution)/shard_map/reduce_scatter | solution.py:34
  106.6 1.1 broadcast_in_dim.27
  107.8 30.1 %all_to_all.39 = bf16[16,192,128]{2,1,0:T(8,128)(2,1)S(1)} all-to-all(bf16[16,192,128]{2,1,0:T(8,128)(2,1)S(1)} %bitcast.83), channel_id=1, replica_groups=mesh['y'=4,'x'=4,'zl'=2,'zh'=4,'c'=2] {'zl','zh','c'}, dimensions={0} | all-to-all | bytes 1572864 | tf_op jit(solution)/shard_map/all_to_all | solution.py:38
  137.9 0.3 reduce_sum.12
  138.1 0.3 copy.34
  138.4 0.9 reshape.124
  139.3 0.0 all-gather.2.cloned.1.call-update
  139.4 4.6 %all-to-all-start.2 = ((bf16[32,2,128,128]{3,2,1,0:T(8,128)(2,1)}), bf16[32,2,128,128]{3,2,1,0:T(8,128)(2,1)S(1)}, u32[]{:S(2)}, u32[]{:S(2)}) async-start(bf16[32,2,128,128]{3,2,1,0:T(8,128)(2,1)} %bitcast.78), calls=%async_computation.3 | async-start | bytes 4194304 | tf_op jit(solution)/shard_map/all_to_all | solution.py:45
  143.9 0.0 copy-done.1
  143.9 0.1 multiply_subtract_fusion
  144.1 48.9 %all-to-all-done.2 = bf16[32,2,128,128]{3,2,1,0:T(8,128)(2,1)S(1)} async-done(((bf16[32,2,128,128]{3,2,1,0:T(8,128)(2,1)}), bf16[32,2,128,128]{3,2,1,0:T(8,128)(2,1)S(1)}, u32[]{:S(2)}, u32[]{:S(2)}) %all-to-all-start.2) | async-done | bytes 2097184 | tf_op jit(solution)/shard_map/all_to_all | solution.py:45
  193.0 1.5 copy.37
  194.5 7.5 %all-gather.2.cloned.1.call-done = bf16[16,192,1024]{2,1,0:T(8,128)(2,1)} async-done(((bf16[1,192,1024]{2,1,0:T(8,128)(2,1)}), bf16[16,192,1024]{2,1,0:T(8,128)(2,1)}) %all-gather.2.cloned.1.call-update) | async-done | bytes 6291472 | tf_op jit(solution)/shard_map/all_gather | solution.py:55
  202.0 0.1 broadcast_in_dim.28
  202.1 4.7 %fusion.4 = bf16[8,2,192,1024]{3,2,0,1:T(8,128)(2,1)S(1)} fusion(f32[192,1024]{1,0:T(8,128)S(1)} %bitcast.81, bf16[8,2,192,1024]{3,2,1,0:T(8,128)(2,1)} %bitcast.80), kind=kLoop, calls=%fused_computation.5 | loop fusion | flops 9437184 | bytes 13369344 | tf_op jit(solution)/shard_map/convert_element_type | solution.py:63
  206.8 0.2 fusion.24
  207.1 0.8 slice_bitcast_fusion
  207.8 0.0 copy-start
  207.8 1.4 maximum_bitcast_fusion
  209.2 0.2 copy-done
  209.4 3.8 %multiply_convert_fusion = bf16[8,2,192,128]{3,2,1,0:T(8,128)(2,1)S(1)} fusion(bf16[4,2048,128]{2,1,0:T(8,128)(2,1)} %bitcast.85, bf16[4,2048,128]{2,1,0:T(8,128)(2,1)S(1)} %bitcast.84, bf16[8,1,192,2048]{3,2,1,0:T(8,128)(2,1)S(1)} %get-tuple-element.32, bf16[8,1,192,2048]{3,2,1,0:T(8,128)(2,1)S(1)} %get-tuple-element.31), kind=kOutput, calls=%fused_computation.17 | convolution fusion | flops 1619787776 | bytes 17563648 | tf_op jit(solution)/shard_map/foqK,fKn->foqn/dot_general | solution.py:70
  213.2 1.0 copy.53
  (2 shorter events, 0.0 us)
Async XLA Ops:
  6.5 100.1 %reduce-scatter.2.cloned.1.call-start = ((), (), s32[]{:S(2)}) async-start(), calls=%async_computation.4 | async-start | bytes 6684672 | tf_op jit(solution)/shard_map/reduce_scatter | solution.py:34
  19.3 182.7 %all-gather.2.cloned.1.call-start = ((), (), s32[]{:S(2)}) async-start(), calls=%async_computation.5 | async-start | bytes 6684672 | tf_op jit(solution)/shard_map/all_gather | solution.py:55
  80.7 63.2 %copy-start.1 = (s32[6,1024]{1,0:T(8,128)S(1)}, s32[6,1024]{1,0:T(8,128)}, u32[]{:S(2)}) copy-start(s32[6,1024]{1,0:T(8,128)} %param.7) | copy-start | bytes 73732
  139.4 53.6 %all-to-all-start.2 = ((bf16[32,2,128,128]{3,2,1,0:T(8,128)(2,1)}), bf16[32,2,128,128]{3,2,1,0:T(8,128)(2,1)S(1)}, u32[]{:S(2)}, u32[]{:S(2)}) async-start(bf16[32,2,128,128]{3,2,1,0:T(8,128)(2,1)} %bitcast.78), calls=%async_computation.3 | async-start | bytes 4194304 | tf_op jit(solution)/shard_map/all_to_all | solution.py:45
  207.8 1.6 copy-start
Sparse Core Ops, SparseCore 0:
  19.4 87.1 reduce-scatter.1
  139.5 62.5 all-gather.1

commit v14 on v13

--- a/solution.py
+++ b/solution.py
@@ -22,7 +22,7 @@
     zl_size = lax.axis_size("zl")
     per_device = node_dev // SB
     me = (lax.axis_index("y") * lax.axis_size("x") + lax.axis_index("x")) * zl_size + lax.axis_index("zl")
-    block = jnp.repeat(source_block, SB, total_repeat_length=ROUNDS * SB)
+    block = jnp.broadcast_to(source_block[:, None], (ROUNDS, SB)).reshape(ROUNDS * SB)
     column = jnp.arange(ROUNDS * SB, dtype=jnp.int32)
     wanted = block % per_device * SB + column % SB
     keep = block // per_device == me

time: 223 us -> 218 us (0.978)
  other arithmetic: 11.2 us -> 6.72 us
    eq x1, other arithmetic: 3.73 us -> 0.01 us  [gather_sources(): keep = block // per_device == me]
where the time goes in v14:
time: 218 us; the launch traced here: 216 us
  blocking collectives  87.3 us (40%)
  waiting for transfers between devices  80.9 us (37%)
  between operations  13.5 us (6%)
  local copies, waits for them, and re-layouts  12.2 us (6%)
  matrix products  10.4 us (5%)
  other arithmetic  6.72 us (3%)
  starting transfers between devices  4.63 us (2%)
    all_to_all x1, blocking collectives, exchange(): return lax.all_to_all(part, SHOT, 0, 2, tiled=True)  57.2 us
    all_to_all x1, waiting for transfers between devices, exchange(): return lax.all_to_all(part, SHOT, 0, 2, tiled=True)  48.9 us
    all_to_all x1, blocking collectives, gather_sources(): got = lax.all_to_all(both, ('zl',) + SHOT, 0, 0, tiled=True)  30.1 us
    reduce_scatter x1, waiting for transfers between devices, gather_sources(): slot = lax.psum_scatter(picked, PLANE, scatter_dimension=0, tiled=True)  24.4 us
    all_gather x1, waiting for transfers between devices, body(): gathered = lax.all_gather(mine, PLANE, axis=0, tiled=True)  7.52 us
    dot_general x1, matrix products, gather_sources(): jnp.einsum('pgkn,nq->pgqk', by_slot, select, preferred_element_type=jnp.f...  6.68 us
    convert_element_type x1, other arithmetic, body(): (source.astype(jnp.float32) * weight_rows[None, None]).astype(jnp.bfloat16)  4.71 us
    all_to_all x1, starting transfers between devices, exchange(): return lax.all_to_all(part, SHOT, 0, 2, tiled=True)  4.59 us
  transfers between devices with their start and end apart: 3, of which 3 were waited for; matrix products, arithmetic and copies ran while one was open for 3% of the time, Pallas kernels for 0%

profile of v14, /device:TPU:73, one launch (start us, length us, event | category | flops | bytes accessed | tf_op | source)
XLA Modules:
  0.0 215.8 jit_solution(15784072373665770738)
XLA Ops:
  6.5 0.0 reduce-scatter.2.cloned.1.call-start
  6.5 0.7 broadcast_in_dim.6
  7.3 0.1 reshape.96
  7.4 6.7 %fusion.10 = bf16[192,16,8,128]{3,0,2,1:T(8,128)(2,1)} fusion(s32[192]{0:T(256)S(1)} %fusion.20, pred[192]{0:T(512)(128)(4,1)S(1)} %fusion.22, bf16[8,16,128,128]{3,2,1,0:T(8,128)(2,1)} %bitcast.66), kind=kOutput, calls=%fused_computation.14 | convolution fusion | flops 808501248 | bytes 10486720 | tf_op jit(solution)/shard_map/pgkn,nq->pgqk/dot_general | solution.py:32
  14.1 0.0 reduce-scatter.2.cloned.1.call-update
  14.1 0.0 all-gather.2.cloned.1.call-start
  14.1 4.1 %fusion.25 = (bf16[8,1,4,2,128,128]{5,4,3,2,1,0:T(8,128)(2,1)S(1)}, bf16[8,1,4,2,128,128]{5,4,3,2,1,0:T(8,128)(2,1)}) fusion(bf16[8,2,4,2,128,128]{5,4,3,2,1,0:T(8,128)(2,1)} %bitcast.67), kind=kLoop, calls=%fused_computation.38 | loop fusion | bytes 8388608 | tf_op jit(solution)/shard_map/slice | solution.py:52
  18.3 57.2 %all_to_all.38 = bf16[32,2,128,128]{3,2,1,0:T(8,128)(2,1)S(1)} all-to-all(bf16[32,2,128,128]{3,2,1,0:T(8,128)(2,1)S(1)} %bitcast.71), channel_id=1, replica_groups=mesh['y'=4,'x'=4,'zl'=2,'zh'=4,'c'=2] {'zh','c'}, dimensions={0} | all-to-all | bytes 4194304 | tf_op jit(solution)/shard_map/all_to_all | solution.py:45
  75.5 0.0 copy-start.1
  75.5 1.5 copy.33
  77.0 24.4 %reduce-scatter.2.cloned.1.call-done = bf16[8,192,128]{2,1,0:T(8,128)(2,1)} async-done(((bf16[128,192,128]{2,1,0:T(8,128)(2,1)}), bf16[8,192,128]{2,1,0:T(8,128)(2,1)}) %reduce-scatter.2.cloned.1.call-update) | async-done | bytes 393232 | tf_op jit(solution)/shard_map/reduce_scatter | solution.py:34
  101.4 1.1 broadcast_in_dim.7
  102.6 30.1 %all_to_all.39 = bf16[16,192,128]{2,1,0:T(8,128)(2,1)S(1)} all-to-all(bf16[16,192,128]{2,1,0:T(8,128)(2,1)S(1)} %bitcast.75), channel_id=1, replica_groups=mesh['y'=4,'x'=4,'zl'=2,'zh'=4,'c'=2] {'zl','zh','c'}, dimensions={0} | all-to-all | bytes 1572864 | tf_op jit(solution)/shard_map/all_to_all | solution.py:38
  132.7 0.3 reduce_sum.12
  133.0 0.3 copy.34
  133.2 0.9 reshape.101
  134.1 0.0 all-gather.2.cloned.1.call-update
  134.2 4.6 %all-to-all-start.2 = ((bf16[32,2,128,128]{3,2,1,0:T(8,128)(2,1)}), bf16[32,2,128,128]{3,2,1,0:T(8,128)(2,1)S(1)}, u32[]{:S(2)}, u32[]{:S(2)}) async-start(bf16[32,2,128,128]{3,2,1,0:T(8,128)(2,1)} %bitcast.70), calls=%async_computation.3 | async-start | bytes 4194304 | tf_op jit(solution)/shard_map/all_to_all | solution.py:45
  138.8 0.0 copy-done.1
  138.8 0.1 multiply_subtract_fusion
  138.9 48.9 %all-to-all-done.2 = bf16[32,2,128,128]{3,2,1,0:T(8,128)(2,1)S(1)} async-done(((bf16[32,2,128,128]{3,2,1,0:T(8,128)(2,1)}), bf16[32,2,128,128]{3,2,1,0:T(8,128)(2,1)S(1)}, u32[]{:S(2)}, u32[]{:S(2)}) %all-to-all-start.2) | async-done | bytes 2097184 | tf_op jit(solution)/shard_map/all_to_all | solution.py:45
  187.8 1.5 copy.37
  189.3 7.5 %all-gather.2.cloned.1.call-done = bf16[16,192,1024]{2,1,0:T(8,128)(2,1)} async-done(((bf16[1,192,1024]{2,1,0:T(8,128)(2,1)}), bf16[16,192,1024]{2,1,0:T(8,128)(2,1)}) %all-gather.2.cloned.1.call-update) | async-done | bytes 6291472 | tf_op jit(solution)/shard_map/all_gather | solution.py:55
  196.8 0.1 broadcast_in_dim.8
  196.9 4.7 %fusion.4 = bf16[8,2,192,1024]{3,2,0,1:T(8,128)(2,1)S(1)} fusion(f32[192,1024]{1,0:T(8,128)S(1)} %bitcast.73, bf16[8,2,192,1024]{3,2,1,0:T(8,128)(2,1)} %bitcast.72), kind=kLoop, calls=%fused_computation.5 | loop fusion | flops 9437184 | bytes 13369344 | tf_op jit(solution)/shard_map/convert_element_type | solution.py:63
  201.6 0.2 fusion.24
  201.8 0.8 slice_bitcast_fusion
  202.6 0.0 copy-start
  202.6 1.4 maximum_bitcast_fusion
  204.0 0.2 copy-done
  204.2 3.7 %multiply_convert_fusion = bf16[8,2,192,128]{3,2,1,0:T(8,128)(2,1)S(1)} fusion(bf16[4,2048,128]{2,1,0:T(8,128)(2,1)} %bitcast.77, bf16[4,2048,128]{2,1,0:T(8,128)(2,1)S(1)} %bitcast.76, bf16[8,1,192,2048]{3,2,1,0:T(8,128)(2,1)S(1)} %get-tuple-element.18, bf16[8,1,192,2048]{3,2,1,0:T(8,128)(2,1)S(1)} %get-tuple-element.17), kind=kOutput, calls=%fused_computation.17 | convolution fusion | flops 1619787776 | bytes 17563648 | tf_op jit(solution)/shard_map/foqK,fKn->foqn/dot_general | solution.py:70
  208.0 1.0 copy.53
  (2 shorter events, 0.0 us)
Async XLA Ops:
  6.5 94.9 %reduce-scatter.2.cloned.1.call-start = ((), (), s32[]{:S(2)}) async-start(), calls=%async_computation.4 | async-start | bytes 6684672 | tf_op jit(solution)/shard_map/reduce_scatter | solution.py:34
  14.1 182.7 %all-gather.2.cloned.1.call-start = ((), (), s32[]{:S(2)}) async-start(), calls=%async_computation.5 | async-start | bytes 6684672 | tf_op jit(solution)/shard_map/all_gather | solution.py:55
  75.5 63.3 %copy-start.1 = (s32[6,1024]{1,0:T(8,128)S(1)}, s32[6,1024]{1,0:T(8,128)}, u32[]{:S(2)}) copy-start(s32[6,1024]{1,0:T(8,128)} %param.5) | copy-start | bytes 73732
  134.2 53.6 %all-to-all-start.2 = ((bf16[32,2,128,128]{3,2,1,0:T(8,128)(2,1)}), bf16[32,2,128,128]{3,2,1,0:T(8,128)(2,1)S(1)}, u32[]{:S(2)}, u32[]{:S(2)}) async-start(bf16[32,2,128,128]{3,2,1,0:T(8,128)(2,1)} %bitcast.70), calls=%async_computation.3 | async-start | bytes 4194304 | tf_op jit(solution)/shard_map/all_to_all | solution.py:45
  202.6 1.6 copy-start
Sparse Core Ops, SparseCore 0:
  14.2 87.1 reduce-scatter.1
  134.3 62.4 all-gather.1

commit v15 on v14

--- a/solution.py
+++ b/solution.py
@@ -61,13 +61,10 @@
     weight_rows = jnp.repeat(taper_weights(taper_window), SB, axis=0)
 
     tapered = (source.astype(jnp.float32) * weight_rows[None, None]).astype(jnp.bfloat16)
-    real_part = tapered[:, 0]
-    imag_part = tapered[:, 1]
-    real_row = jnp.concatenate((real_part, imag_part), axis=2)
-    imag_row = jnp.concatenate((-imag_part, real_part), axis=2)
-    operator = jnp.stack((real_row, imag_row), axis=1)
-    stacked = receivers.reshape(freqs, 2 * shots, node_dev)
-    summed = jnp.einsum("foqK,fKn->foqn", operator, stacked, preferred_element_type=jnp.float32)
+    swapped = jnp.stack((receivers[:, 1], -receivers[:, 0]), axis=1)
+    real = jnp.einsum("fcqk,fckn->fqn", tapered, receivers, preferred_element_type=jnp.float32)
+    imag = jnp.einsum("fcqk,fckn->fqn", tapered, swapped, preferred_element_type=jnp.float32)
+    summed = jnp.stack((real, imag), axis=1)
     out = (summed * scale).astype(jnp.bfloat16).reshape(freqs, 2, ROUNDS, SB, node_dev)
     return jnp.transpose(out, (2, 0, 1, 3, 4))
 

time: 218 us -> 215 us (0.986)
  matrix products: 10.4 us -> 14.2 us
  waiting for transfers between devices: 80.9 us -> 77.7 us
  other arithmetic: 6.72 us -> 3.84 us
    convert_element_type x1 -> x0, other arithmetic: 4.71 us -> none  [body(): (source.astype(jnp.float32) * weight_rows[None, None]).astype(jnp.bfloat16)]
    dot_general x1 -> x2, matrix products: 3.75 us -> 7.54 us  [the longest x1 5.66 us: body(): jnp.einsum('fcqk,fckn->fqn', tapered, receivers, preferred_element_type=j...]
    all_gather x1, waiting for transfers between devices: 7.52 us -> 4.38 us  [body(): gathered = lax.all_gather(mine, PLANE, axis=0, tiled=True)]
    unnamed x4 -> x16, local copies, waits for them, and re-layouts: 0.19 us -> 2.94 us
    concatenate x0 -> x1, other arithmetic: none -> 2.31 us  [body(): receivers = jnp.concatenate((first, second), axis=0)]
  transfers between devices with their start and end apart: 3 -> 3, of which waited for: 3 -> 3; matrix products, arithmetic and copies ran while one was open for 3% -> 4% of each run, Pallas kernels for 0% -> 0%
where the time goes in v15:
time: 215 us; the launch traced here: 213 us
  blocking collectives  87.3 us (41%)
  waiting for transfers between devices  77.7 us (36%)
  matrix products  14.2 us (7%)
  between operations  13.5 us (6%)
  local copies, waits for them, and re-layouts  11.9 us (6%)
  starting transfers between devices  4.63 us (2%)
  other arithmetic  3.84 us (2%)
    all_to_all x1, blocking collectives, exchange(): return lax.all_to_all(part, SHOT, 0, 2, tiled=True)  57.2 us
    all_to_all x1, waiting for transfers between devices, exchange(): return lax.all_to_all(part, SHOT, 0, 2, tiled=True)  48.9 us
    all_to_all x1, blocking collectives, gather_sources(): got = lax.all_to_all(both, ('zl',) + SHOT, 0, 0, tiled=True)  30.1 us
    reduce_scatter x1, waiting for transfers between devices, gather_sources(): slot = lax.psum_scatter(picked, PLANE, scatter_dimension=0, tiled=True)  24.4 us
    dot_general x1, matrix products, gather_sources(): jnp.einsum('pgkn,nq->pgqk', by_slot, select, preferred_element_type=jnp.f...  6.67 us
    dot_general x1, matrix products, body(): jnp.einsum('fcqk,fckn->fqn', tapered, receivers, preferred_element_type=j...  5.66 us
    all_to_all x1, starting transfers between devices, exchange(): return lax.all_to_all(part, SHOT, 0, 2, tiled=True)  4.59 us
    all_gather x1, waiting for transfers between devices, body(): gathered = lax.all_gather(mine, PLANE, axis=0, tiled=True)  4.38 us
  transfers between devices with their start and end apart: 3, of which 3 were waited for; matrix products, arithmetic and copies ran while one was open for 4% of the time, Pallas kernels for 0%

profile of v15, /device:TPU:73, one launch (start us, length us, event | category | flops | bytes accessed | tf_op | source)
XLA Modules:
  0.0 213.1 jit_solution(9209805655861540839)
XLA Ops:
  6.5 0.0 reduce-scatter.2.cloned.1.call-start
  6.5 0.7 broadcast_in_dim.6
  7.3 0.1 reshape.94
  7.4 6.7 %fusion.11 = bf16[192,16,8,128]{3,0,2,1:T(8,128)(2,1)} fusion(s32[192]{0:T(256)S(1)} %fusion.24, pred[192]{0:T(512)(128)(4,1)S(1)} %fusion.26, bf16[8,16,128,128]{3,2,1,0:T(8,128)(2,1)} %bitcast.52), kind=kOutput, calls=%fused_computation.15 | convolution fusion | flops 808501248 | bytes 10486720 | tf_op jit(solution)/shard_map/pgkn,nq->pgqk/dot_general | solution.py:32
  14.0 0.0 reduce-scatter.2.cloned.1.call-update
  14.1 0.0 all-gather.2.cloned.1.call-start
  14.1 4.1 %fusion.29 = (bf16[8,1,4,2,128,128]{5,4,3,2,1,0:T(8,128)(2,1)S(1)}, bf16[8,1,4,2,128,128]{5,4,3,2,1,0:T(8,128)(2,1)}) fusion(bf16[8,2,4,2,128,128]{5,4,3,2,1,0:T(8,128)(2,1)} %bitcast.53), kind=kLoop, calls=%fused_computation.42 | loop fusion | bytes 8388608 | tf_op jit(solution)/shard_map/slice | solution.py:52
  18.3 57.2 %all_to_all.41 = bf16[32,2,128,128]{3,2,1,0:T(8,128)(2,1)S(1)} all-to-all(bf16[32,2,128,128]{3,2,1,0:T(8,128)(2,1)S(1)} %bitcast.61), channel_id=1, replica_groups=mesh['y'=4,'x'=4,'zl'=2,'zh'=4,'c'=2] {'zh','c'}, dimensions={0} | all-to-all | bytes 4194304 | tf_op jit(solution)/shard_map/all_to_all | solution.py:45
  75.5 1.5 copy.31
  77.0 24.4 %reduce-scatter.2.cloned.1.call-done = bf16[8,192,128]{2,1,0:T(8,128)(2,1)} async-done(((bf16[128,192,128]{2,1,0:T(8,128)(2,1)}), bf16[8,192,128]{2,1,0:T(8,128)(2,1)}) %reduce-scatter.2.cloned.1.call-update) | async-done | bytes 393232 | tf_op jit(solution)/shard_map/reduce_scatter | solution.py:34
  101.3 1.1 broadcast_in_dim.7
  102.5 0.0 copy-start.5
  102.5 30.1 %all_to_all.42 = bf16[16,192,128]{2,1,0:T(8,128)(2,1)S(1)} all-to-all(bf16[16,192,128]{2,1,0:T(8,128)(2,1)S(1)} %bitcast.63), channel_id=1, replica_groups=mesh['y'=4,'x'=4,'zl'=2,'zh'=4,'c'=2] {'zl','zh','c'}, dimensions={0} | all-to-all | bytes 1572864 | tf_op jit(solution)/shard_map/all_to_all | solution.py:38
  132.6 0.3 reduce_sum.12
  132.9 0.3 copy.32
  133.1 0.9 reshape.99
  134.0 0.0 all-gather.2.cloned.1.call-update
  134.1 4.6 %all-to-all-start.2 = ((bf16[32,2,128,128]{3,2,1,0:T(8,128)(2,1)}), bf16[32,2,128,128]{3,2,1,0:T(8,128)(2,1)S(1)}, u32[]{:S(2)}, u32[]{:S(2)}) async-start(bf16[32,2,128,128]{3,2,1,0:T(8,128)(2,1)} %bitcast.58), calls=%async_computation.3 | async-start | bytes 4194304 | tf_op jit(solution)/shard_map/all_to_all | solution.py:45
  138.6 0.0 copy-done.5
  138.6 0.1 multiply_subtract_fusion
  138.8 48.9 %all-to-all-done.2 = bf16[32,2,128,128]{3,2,1,0:T(8,128)(2,1)S(1)} async-done(((bf16[32,2,128,128]{3,2,1,0:T(8,128)(2,1)}), bf16[32,2,128,128]{3,2,1,0:T(8,128)(2,1)S(1)}, u32[]{:S(2)}, u32[]{:S(2)}) %all-to-all-start.2) | async-done | bytes 2097184 | tf_op jit(solution)/shard_map/all_to_all | solution.py:45
  187.7 0.0 copy-start
  187.7 0.1 copy.33
  187.8 0.0 copy-start.2
  187.9 1.3 copy-done.2
  189.2 0.9 copy-done
  190.1 0.0 copy-start.1
  190.1 2.3 %fusion.14 = (bf16[8,1,1024,128]{3,2,1,0:T(8,128)(2,1)}, bf16[8,1,1024,128]{3,2,1,0:T(8,128)(2,1)}) fusion(bf16[4,2,1024,128]{3,2,1,0:T(8,128)(2,1)S(1)} %bitcast.56, bf16[4,2,1024,128]{3,2,1,0:T(8,128)(2,1)S(1)} %bitcast.59), kind=kLoop, calls=%fused_computation.16 | loop fusion | flops 3145728 | bytes 8388608 | tf_op jit(solution)/shard_map/concatenate | solution.py:57
  192.4 4.4 %all-gather.2.cloned.1.call-done = bf16[16,192,1024]{2,1,0:T(8,128)(2,1)} async-done(((bf16[1,192,1024]{2,1,0:T(8,128)(2,1)}), bf16[16,192,1024]{2,1,0:T(8,128)(2,1)}) %all-gather.2.cloned.1.call-update) | async-done | bytes 6291472 | tf_op jit(solution)/shard_map/all_gather | solution.py:55
  196.8 0.0 slice-start
  196.8 0.1 broadcast_in_dim.8
  196.9 0.0 copy-done.1
  196.9 0.0 copy-start.3
  196.9 0.0 copy-start.4
  196.9 0.0 slice-start.1
  196.9 5.7 %fusion.3 = f32[8,192,128,1]{2,1,3,0:T(8,128)S(1)} fusion(bf16[8,2,192,1024]{3,2,1,0:T(8,128)(2,1)} %bitcast.69, f32[192,1024]{1,0:T(8,128)S(1)} %bitcast.65, bf16[4,2,1024,128]{3,2,1,0:T(8,128)(2,1)} %bitcast.60, bf16[4,2,1024,128]{3,2,1,0:T(8,128)(2,1)S(1)} %bitcast.57), kind=kOutput, calls=%fused_computation.8 | convolution fusion | flops 816840704 | bytes 12058624 | tf_op jit(solution)/shard_map/fcqk,fckn->fqn/dot_general | solution.py:65
  202.6 0.0 slice-done
  202.6 0.0 copy-done.3
  202.6 0.1 copy-done.4
  202.7 0.6 slice-done.1
  203.3 1.9 fusion.1
  205.2 1.1 fusion.18
  (3 shorter events, 0.0 us)
Async XLA Ops:
  6.5 94.8 %reduce-scatter.2.cloned.1.call-start = ((), (), s32[]{:S(2)}) async-start(), calls=%async_computation.4 | async-start | bytes 6684672 | tf_op jit(solution)/shard_map/reduce_scatter | solution.py:34
  14.1 182.7 %all-gather.2.cloned.1.call-start = ((), (), s32[]{:S(2)}) async-start(), calls=%async_computation.5 | async-start | bytes 6684672 | tf_op jit(solution)/shard_map/all_gather | solution.py:55
  102.5 36.2 %copy-start.5 = (s32[6,1024]{1,0:T(8,128)S(1)}, s32[6,1024]{1,0:T(8,128)}, u32[]{:S(2)}) copy-start(s32[6,1024]{1,0:T(8,128)} %param.5) | copy-start | bytes 73732
  134.1 53.6 %all-to-all-start.2 = ((bf16[32,2,128,128]{3,2,1,0:T(8,128)(2,1)}), bf16[32,2,128,128]{3,2,1,0:T(8,128)(2,1)S(1)}, u32[]{:S(2)}, u32[]{:S(2)}) async-start(bf16[32,2,128,128]{3,2,1,0:T(8,128)(2,1)} %bitcast.58), calls=%async_computation.3 | async-start | bytes 4194304 | tf_op jit(solution)/shard_map/all_to_all | solution.py:45
  187.7 2.4 %copy-start = (bf16[4,2,8,128,128]{4,3,2,1,0:T(8,128)(2,1)S(1)}, bf16[4,2,8,128,128]{4,3,2,1,0:T(8,128)(2,1)}, u32[]{:S(2)}) copy-start(bf16[4,2,8,128,128]{4,3,2,1,0:T(8,128)(2,1)} %copy.31) | copy-start | bytes 6291460
  187.8 1.3 copy-start.2
  190.1 6.8 %copy-start.1 = (bf16[4,2,8,128,128]{4,3,2,1,0:T(8,128)(2,1)S(1)}, bf16[4,2,8,128,128]{4,3,2,1,0:T(8,128)(2,1)}, u32[]{:S(2)}) copy-start(bf16[4,2,8,128,128]{4,3,2,1,0:T(8,128)(2,1)} %copy.31) | copy-start | bytes 6291460
  196.8 5.8 %slice-start = ((s8[6291456]{0:T(1024)(128)(4,1)}), s8[4194304]{0:T(1024)(128)(4,1)S(1)}, s32[]{:S(2)}) async-start(s8[6291456]{0:T(1024)(128)(4,1)} %bitcast.70), calls=%async_computation.6 | async-start | bytes 8388608
  196.9 5.7 %copy-start.3 = (bf16[8,1,1024,128]{3,2,1,0:T(8,128)(2,1)S(1)}, bf16[8,1,1024,128]{3,2,1,0:T(8,128)(2,1)}, u32[]{:S(2)}) copy-start(bf16[8,1,1024,128]{3,2,1,0:T(8,128)(2,1)} %get-tuple-element.13) | copy-start | bytes 6291460
  196.9 5.8 %copy-start.4 = (bf16[8,1,1024,128]{3,2,1,0:T(8,128)(2,1)S(1)}, bf16[8,1,1024,128]{3,2,1,0:T(8,128)(2,1)}, u32[]{:S(2)}) copy-start(bf16[8,1,1024,128]{3,2,1,0:T(8,128)(2,1)} %get-tuple-element.14) | copy-start | bytes 6291460
  196.9 6.4 %slice-start.1 = ((s8[6291456]{0:T(1024)(128)(4,1)}), s8[2097152]{0:T(1024)(128)(4,1)S(1)}, s32[]{:S(2)}) async-start(s8[6291456]{0:T(1024)(128)(4,1)} %bitcast.70), calls=%async_computation.7 | async-start | bytes 4194304
Sparse Core Ops, SparseCore 0:
  14.2 87.0 reduce-scatter.1
  134.2 62.5 all-gather.1

commit v16 on v15

--- a/solution.py
+++ b/solution.py
@@ -51,16 +51,15 @@
     split = spectra.reshape(groups, 2, freqs_all // (groups * 2), comps, shot_dev, node_dev)
     first = exchange(split[:, 0].reshape(-1, comps, shot_dev, node_dev))
     mine, first = gather_sources(spectra, source_block, first)
+    weight_rows = jnp.repeat(taper_weights(taper_window), SB, axis=0)
+    mine = (mine.astype(jnp.float32) * weight_rows[None]).astype(jnp.bfloat16)
     second_part, mine = lax.optimization_barrier((split[:, 1].reshape(-1, comps, shot_dev, node_dev), mine))
     gathered = lax.all_gather(mine, PLANE, axis=0, tiled=True)
     second = exchange(second_part)
     receivers = jnp.concatenate((first, second), axis=0)
     freqs, _, shots, _ = receivers.shape
-    source = gathered.reshape(freqs, comps, ROUNDS * SB, shots)
+    tapered = gathered.reshape(freqs, comps, ROUNDS * SB, shots)
     scale = 1.0 / jnp.sqrt(jnp.float32(shots))
-    weight_rows = jnp.repeat(taper_weights(taper_window), SB, axis=0)
-
-    tapered = (source.astype(jnp.float32) * weight_rows[None, None]).astype(jnp.bfloat16)
     swapped = jnp.stack((receivers[:, 1], -receivers[:, 0]), axis=1)
     real = jnp.einsum("fcqk,fckn->fqn", tapered, receivers, preferred_element_type=jnp.float32)
     imag = jnp.einsum("fcqk,fckn->fqn", tapered, swapped, preferred_element_type=jnp.float32)

time: 215 us -> 219 us (1.019)
  waiting for transfers between devices: 77.7 us -> 52.2 us
  blocking collectives: 87.3 us -> 111 us
  starting transfers between devices: 4.63 us -> 8.85 us
    all_to_all x1 -> x2, blocking collectives: 57.2 us -> 111 us  [exchange(): return lax.all_to_all(part, SHOT, 0, 2, tiled=True)]
    all_to_all x1 -> x0, blocking collectives: 30.1 us -> none  [gather_sources(): got = lax.all_to_all(both, ('zl',) + SHOT, 0, 0, tiled=True)]
    all_to_all x1, waiting for transfers between devices: 48.9 us -> 21.3 us  [gather_sources(): got = lax.all_to_all(both, ('zl',) + SHOT, 0, 0, tiled=True)]
    all_to_all x1, starting transfers between devices: 4.59 us -> 8.81 us  [gather_sources(): got = lax.all_to_all(both, ('zl',) + SHOT, 0, 0, tiled=True)]
  transfers between devices with their start and end apart: 3 -> 3, of which waited for: 3 -> 3; matrix products, arithmetic and copies ran while one was open for 4% -> 3% of each run, Pallas kernels for 0% -> 0%
where the time goes in v16:
time: 219 us; the launch traced here: 216 us
  blocking collectives  111 us (51%)
  waiting for transfers between devices  52.2 us (24%)
  matrix products  14 us (6%)
  between operations  13.5 us (6%)
  local copies, waits for them, and re-layouts  11.2 us (5%)
  starting transfers between devices  8.85 us (4%)
  other arithmetic  5.85 us (3%)
    all_to_all x2, blocking collectives, exchange(): return lax.all_to_all(part, SHOT, 0, 2, tiled=True)  111 us
    reduce_scatter x1, waiting for transfers between devices, gather_sources(): slot = lax.psum_scatter(picked, PLANE, scatter_dimension=0, tiled=True)  25.7 us
    all_to_all x1, waiting for transfers between devices, gather_sources(): got = lax.all_to_all(both, ('zl',) + SHOT, 0, 0, tiled=True)  21.3 us
    all_to_all x1, starting transfers between devices, gather_sources(): got = lax.all_to_all(both, ('zl',) + SHOT, 0, 0, tiled=True)  8.81 us
    dot_general x1, matrix products, gather_sources(): jnp.einsum('pgkn,nq->pgqk', by_slot, select, preferred_element_type=jnp.f...  6.69 us
    dot_general x1, matrix products, body(): jnp.einsum('fcqk,fckn->fqn', tapered, receivers, preferred_element_type=j...  5.41 us
    all_gather x1, waiting for transfers between devices, body(): gathered = lax.all_gather(mine, PLANE, axis=0, tiled=True)  5.21 us
  transfers between devices with their start and end apart: 3, of which 3 were waited for; matrix products, arithmetic and copies ran while one was open for 3% of the time, Pallas kernels for 0%

profile of v16, /device:TPU:73, one launch (start us, length us, event | category | flops | bytes accessed | tf_op | source)
XLA Modules:
  0.0 216.5 jit_solution(5720694515412752925)
XLA Ops:
  6.5 0.0 reduce-scatter.2.cloned.1.call-start
  6.5 0.7 broadcast_in_dim.6
  7.3 0.1 reshape.121
  7.4 6.7 %fusion.8 = bf16[192,16,8,128]{3,0,2,1:T(8,128)(2,1)} fusion(s32[192]{0:T(256)S(1)} %fusion.22, pred[192]{0:T(512)(128)(4,1)S(1)} %fusion.24, bf16[8,16,128,128]{3,2,1,0:T(8,128)(2,1)} %bitcast.58), kind=kOutput, calls=%fused_computation.13 | convolution fusion | flops 808501248 | bytes 10486720 | tf_op jit(solution)/shard_map/pgkn,nq->pgqk/dot_general | solution.py:32
  14.1 0.0 reduce-scatter.2.cloned.1.call-update
  14.1 4.1 %fusion.27 = (bf16[8,1,4,2,128,128]{5,4,3,2,1,0:T(8,128)(2,1)S(1)}, bf16[8,1,4,2,128,128]{5,4,3,2,1,0:T(8,128)(2,1)}) fusion(bf16[8,2,4,2,128,128]{5,4,3,2,1,0:T(8,128)(2,1)} %bitcast.59), kind=kLoop, calls=%fused_computation.43 | loop fusion | bytes 8388608 | tf_op jit(solution)/shard_map/slice | solution.py:52
  18.2 57.2 %all_to_all.41 = bf16[32,2,128,128]{3,2,1,0:T(8,128)(2,1)S(1)} all-to-all(bf16[32,2,128,128]{3,2,1,0:T(8,128)(2,1)S(1)} %bitcast.67), channel_id=1, replica_groups=mesh['y'=4,'x'=4,'zl'=2,'zh'=4,'c'=2] {'zh','c'}, dimensions={0} | all-to-all | bytes 4194304 | tf_op jit(solution)/shard_map/all_to_all | solution.py:45
  75.4 0.1 copy.31
  75.6 0.0 copy-start.3
  75.6 25.7 %reduce-scatter.2.cloned.1.call-done = bf16[8,192,128]{2,1,0:T(8,128)(2,1)} async-done(((bf16[128,192,128]{2,1,0:T(8,128)(2,1)}), bf16[8,192,128]{2,1,0:T(8,128)(2,1)}) %reduce-scatter.2.cloned.1.call-update) | async-done | bytes 393232 | tf_op jit(solution)/shard_map/reduce_scatter | solution.py:34
  101.3 2.0 broadcast_in_dim.7
  103.3 8.8 %all-to-all-start.1 = ((bf16[16,192,128]{2,1,0:T(8,128)(2,1)}), bf16[16,192,128]{2,1,0:T(8,128)(2,1)S(1)}, u32[]{:S(2)}, u32[]{:S(2)}) async-start(bf16[16,192,128]{2,1,0:T(8,128)(2,1)} %bitcast.69), calls=%async_computation.2 | async-start | bytes 1572864 | tf_op jit(solution)/shard_map/all_to_all | solution.py:38
  112.1 0.0 all-gather.2.cloned.1.call-start
  112.2 0.0 copy-done.3
  112.2 0.1 multiply_subtract_fusion
  112.3 21.3 %all-to-all-done.1 = bf16[16,192,128]{2,1,0:T(8,128)(2,1)S(1)} async-done(((bf16[16,192,128]{2,1,0:T(8,128)(2,1)}), bf16[16,192,128]{2,1,0:T(8,128)(2,1)S(1)}, u32[]{:S(2)}, u32[]{:S(2)}) %all-to-all-start.1) | async-done | bytes 786464 | tf_op jit(solution)/shard_map/all_to_all | solution.py:38
  133.6 0.3 reduce_sum.12
  133.9 0.1 convert_bitcast_fusion
  133.9 0.5 copy.32
  134.4 1.0 reshape.127
  135.4 0.1 broadcast_in_dim.8
  135.5 2.0 fusion.16
  137.5 0.0 all-gather.2.cloned.1.call-update
  137.5 53.6 %all_to_all.42 = bf16[32,2,128,128]{3,2,1,0:T(8,128)(2,1)S(1)} all-to-all(bf16[32,2,128,128]{3,2,1,0:T(8,128)(2,1)} %bitcast.64), channel_id=1, replica_groups=mesh['y'=4,'x'=4,'zl'=2,'zh'=4,'c'=2] {'zh','c'}, dimensions={0} | all-to-all | bytes 4194304 | tf_op jit(solution)/shard_map/all_to_all | solution.py:45
  191.1 0.2 copy.33
  191.4 0.0 copy-start
  191.4 1.3 copy-done
  192.7 2.3 %fusion.11 = (bf16[8,1,1024,128]{3,2,1,0:T(8,128)(2,1)}, bf16[8,1,1024,128]{3,2,1,0:T(8,128)(2,1)}) fusion(bf16[4,2,1024,128]{3,2,1,0:T(8,128)(2,1)S(1)} %bitcast.62, bf16[4,2,1024,128]{3,2,1,0:T(8,128)(2,1)S(1)} %bitcast.65), kind=kLoop, calls=%fused_computation.14 | loop fusion | flops 3145728 | bytes 8388608 | tf_op jit(solution)/shard_map/concatenate | solution.py:59
  195.0 5.2 %all-gather.2.cloned.1.call-done = bf16[16,192,1024]{2,1,0:T(8,128)(2,1)} async-done(((bf16[1,192,1024]{2,1,0:T(8,128)(2,1)}), bf16[16,192,1024]{2,1,0:T(8,128)(2,1)}) %all-gather.2.cloned.1.call-update) | async-done | bytes 6291472 | tf_op jit(solution)/shard_map/all_gather | solution.py:57
  200.2 0.0 copy-start.1
  200.2 0.0 copy-start.2
  200.2 0.0 copy-start.4
  200.2 5.4 %fusion = f32[8,192,128,1]{2,1,3,0:T(8,128)S(1)} fusion(bf16[8,2,192,1024]{3,2,1,0:T(8,128)(2,1)} %bitcast.73, bf16[4,2,1024,128]{3,2,1,0:T(8,128)(2,1)} %bitcast.66, bf16[4,2,1024,128]{3,2,1,0:T(8,128)(2,1)S(1)} %bitcast.63), kind=kOutput, calls=%fused_computation.5 | convolution fusion | flops 807403520 | bytes 11272192 | tf_op jit(solution)/shard_map/fcqk,fckn->fqn/dot_general | solution.py:64
  205.6 0.0 copy-done.1
  205.6 0.0 copy-done.2
  205.6 1.0 copy-done.4
  206.7 1.9 fusion.1
  208.5 1.1 fusion.15
  (2 shorter events, 0.0 us)
Async XLA Ops:
  6.5 94.7 %reduce-scatter.2.cloned.1.call-start = ((), (), s32[]{:S(2)}) async-start(), calls=%async_computation.4 | async-start | bytes 6684672 | tf_op jit(solution)/shard_map/reduce_scatter | solution.py:34
  75.6 36.6 %copy-start.3 = (s32[6,1024]{1,0:T(8,128)S(1)}, s32[6,1024]{1,0:T(8,128)}, u32[]{:S(2)}) copy-start(s32[6,1024]{1,0:T(8,128)} %param.5) | copy-start | bytes 73732
  103.3 30.3 %all-to-all-start.1 = ((bf16[16,192,128]{2,1,0:T(8,128)(2,1)}), bf16[16,192,128]{2,1,0:T(8,128)(2,1)S(1)}, u32[]{:S(2)}, u32[]{:S(2)}) async-start(bf16[16,192,128]{2,1,0:T(8,128)(2,1)} %bitcast.69), calls=%async_computation.2 | async-start | bytes 1572864 | tf_op jit(solution)/shard_map/all_to_all | solution.py:38
  112.1 88.1 %all-gather.2.cloned.1.call-start = ((), (), s32[]{:S(2)}) async-start(), calls=%async_computation.5 | async-start | bytes 6684672 | tf_op jit(solution)/shard_map/all_gather | solution.py:57
  191.4 1.3 copy-start
  200.2 5.4 %copy-start.1 = (bf16[8,1,1024,128]{3,2,1,0:T(8,128)(2,1)S(1)}, bf16[8,1,1024,128]{3,2,1,0:T(8,128)(2,1)}, u32[]{:S(2)}) copy-start(bf16[8,1,1024,128]{3,2,1,0:T(8,128)(2,1)} %get-tuple-element.13) | copy-start | bytes 6291460
  200.2 5.4 %copy-start.2 = (bf16[8,1,1024,128]{3,2,1,0:T(8,128)(2,1)S(1)}, bf16[8,1,1024,128]{3,2,1,0:T(8,128)(2,1)}, u32[]{:S(2)}) copy-start(bf16[8,1,1024,128]{3,2,1,0:T(8,128)(2,1)} %get-tuple-element.14) | copy-start | bytes 6291460
  200.2 6.5 %copy-start.4 = (bf16[16,192,1024]{2,1,0:T(8,128)(2,1)S(1)}, bf16[16,192,1024]{2,1,0:T(8,128)(2,1)}, u32[]{:S(2)}) copy-start(bf16[16,192,1024]{2,1,0:T(8,128)(2,1)} %all-gather.2.cloned.1.call-done) | copy-start | bytes 18874372
Sparse Core Ops, SparseCore 0:
  14.2 87.0 reduce-scatter.1
  137.6 62.5 all-gather.1
